TPU v7x, 512 devices: a whole 4x8x8 slice. The times are simulated.
512 devices in a mesh: ctx: 64 (over z, y_hi, core), head: 8 (over y_lo, x).
Axes of the slice: x: 4, y: 8 (y_hi: 4, y_lo: 2; y = y_hi * 2 + y_lo), z: 8, core: 2. Of those that a mesh axis runs over, the one named last changes fastest.
Arguments:
- queries_cross: bfloat16 [8192, 3072], P('ctx', 'head'), may hold values from -38 to 38
- outputs_grad: bfloat16 [8192, 3072], P('ctx', 'head'), may hold values from -3 to 3
- keys_shared: bfloat16 [8192, 1024], P('ctx', 'head'), may hold values from -5 to 5
- values_shared: bfloat16 [8192, 1024], P('ctx', 'head'), may hold values from -6 to 6
- stripe_order: int32 [8192], replicated, may hold values from 0 to 8191, as said below
- segments: int32 [8192], replicated, may hold values from 0 to 7, as said below
- norm_input: bfloat16 [8192, 3072], P('ctx', 'head'), may hold values from -70 to 70
- norm_gain: float32 [3072], replicated, may hold values from 0.1 to 1.9
- weight_key: bfloat16 [3072, 1024], P(None, 'head'), may hold values from -0.109375 to 0.109375
- weight_value: bfloat16 [3072, 1024], P(None, 'head'), may hold values from -0.109375 to 0.109375
- upstream: bfloat16 [8192, 3072], P('ctx', 'head'), may hold values from -1.5 to 1.5
- weight_out: bfloat16 [3072, 3072], P('head'), may hold values from -0.109375 to 0.109375
- queries_window: bfloat16 [8192, 3072], P('ctx', 'head'), may hold values from -38 to 38
- keys_window: bfloat16 [8192, 1024], P('ctx', 'head'), may hold values from -5 to 5
- values_window: bfloat16 [8192, 1024], P('ctx', 'head'), may hold values from -6 to 6
Outputs:
- grad_cross: bfloat16 [8192, 3072], P('ctx', 'head')
- grad_stream: bfloat16 [8192, 3072], P('ctx', 'head')
- grad_queries: bfloat16 [8192, 3072], P('ctx', 'head')
- grad_keys: bfloat16 [8192, 1024], P('ctx', 'head')
- grad_values: bfloat16 [8192, 1024], P('ctx', 'head')
Inputs may be any that keep to these rules, and one draw needn't show every extreme that they name: `stripe_order`: a permutation of all positions; the row at index c * 128 + s holds a position from s * (64) to s * 64 + 8192 // 128 - 1. `segments`: starts at 0, never falls, rises by at most one from a position to the next.
All inputs are finite; a program needn't handle non-finite values.
Results may differ from a plain program's by a relative error of at most 0.022.
Values may be sent and summed in bfloat16 or wider, within the bound.
No kernel may reach another device: no remote copies, remote signals or barrier semaphores. Data moves between devices by JAX's collectives and lax.ppermute only.
A program may use at most 128 MiB of HBM per device.

v0:
```python
import jax
import jax.numpy as jnp
from jax import lax
from jax.sharding import PartitionSpec as P

D = 3072
HEADS = 24
KV_HEADS = 8
HEAD_DIM = 128
WINDOW = 1024


def from_behind(value, axis, steps):
    count = lax.axis_size(axis)
    first, last = (max(0, -steps), min(count, count - steps))
    return lax.ppermute(value, axis, [(source, source + steps) for source in range(first, last)])


def inverse_of(permutation):
    length = permutation.shape[0]
    return jnp.zeros((length,), jnp.int32).at[permutation].set(jnp.arange(length, dtype=jnp.int32))


def split_heads(matrix, groups):
    row_count = matrix.shape[0]
    group_size = HEADS // KV_HEADS
    return matrix.reshape(row_count, groups, group_size, HEAD_DIM).transpose(1, 2, 0, 3)


def join_heads(tensor):
    groups, group_size, row_count, head_width = tensor.shape
    return tensor.transpose(2, 0, 1, 3).reshape(row_count, groups * group_size * head_width)


def cross_backward(
    queries, out_grads, keys_all, values_all, query_place, query_segment, key_place, key_segment
):
    key_count = keys_all.shape[0]
    groups = queries.shape[0]
    factor = HEAD_DIM ** (-0.5)
    block_size = min(512, key_count)
    block_count = key_count // block_size
    key_blocks = keys_all.reshape(block_count, block_size, groups, HEAD_DIM)
    value_blocks = values_all.reshape(block_count, block_size, groups, HEAD_DIM)
    place_blocks = key_place.reshape(block_count, block_size)
    segment_blocks = key_segment.reshape(block_count, block_size)

    def masked_scores(operands):
        key_block, place_block, segment_block = operands
        scores = (
            jnp.einsum("gjre,kge->gjrk", queries, key_block, preferred_element_type=jnp.float32)
            * factor
        )
        allowed = (place_block[None, :] <= query_place[:, None]) & (
            segment_block[None, :] == query_segment[:, None]
        )
        return jnp.where(allowed, scores, -jnp.inf)

    stored = lax.map(masked_scores, (key_blocks, place_blocks, segment_blocks))
    row_peak = jnp.max(stored, axis=(0, 4))
    logsum = row_peak + jnp.log(
        jnp.sum(jnp.exp(stored - row_peak[None, :, :, :, None]), axis=(0, 4))
    )

    def forward_step(output, operands):
        scores, value_block = operands
        weights_low = jnp.exp(scores - logsum[..., None]).astype(jnp.bfloat16)
        return (
            output
            + jnp.einsum(
                "gjrk,kge->gjre", weights_low, value_block, preferred_element_type=jnp.float32
            ),
            None,
        )

    start_value = jnp.zeros(queries.shape, jnp.float32)
    output, unused = lax.scan(forward_step, start_value, (stored, value_blocks))
    row_inner = jnp.sum(out_grads.astype(jnp.float32) * output, axis=3)

    def backward_step(query_grad, operands):
        scores, key_block, value_block = operands
        weights = jnp.exp(scores - logsum[..., None])
        weights_low = weights.astype(jnp.bfloat16)
        weight_grads = jnp.einsum(
            "gjre,kge->gjrk", out_grads, value_block, preferred_element_type=jnp.float32
        )
        score_grads = (weights * (weight_grads - row_inner[..., None])).astype(jnp.bfloat16)
        query_grad = query_grad + jnp.einsum(
            "gjrk,kge->gjre", score_grads, key_block, preferred_element_type=jnp.float32
        )
        key_grad = (
            jnp.einsum("gjrk,gjre->kge", score_grads, queries, preferred_element_type=jnp.float32)
            * factor
        )
        value_grad = jnp.einsum(
            "gjrk,gjre->kge", weights_low, out_grads, preferred_element_type=jnp.float32
        )
        return (query_grad, jnp.stack([key_grad, value_grad], axis=1))

    query_grad, partial_value = lax.scan(
        backward_step, start_value, (stored, key_blocks, value_blocks)
    )
    return (query_grad * factor, partial_value.reshape(key_count, 2 * groups * HEAD_DIM))


def window_backward(queries, out_grads, keys_all, values_all, allowed):
    factor = HEAD_DIM ** (-0.5)
    scores = (
        jnp.einsum("gjre,kge->gjrk", queries, keys_all, preferred_element_type=jnp.float32) * factor
    )
    scores = jnp.where(allowed, scores, -jnp.inf)
    row_peak = jnp.max(scores, axis=3, keepdims=True)
    logsum = row_peak + jnp.log(jnp.sum(jnp.exp(scores - row_peak), axis=3, keepdims=True))
    weights = jnp.exp(scores - logsum)
    weights_low = weights.astype(jnp.bfloat16)
    output = jnp.einsum(
        "gjrk,kge->gjre", weights_low, values_all, preferred_element_type=jnp.float32
    )
    row_inner = jnp.sum(out_grads.astype(jnp.float32) * output, axis=3, keepdims=True)
    weight_grads = jnp.einsum(
        "gjre,kge->gjrk", out_grads, values_all, preferred_element_type=jnp.float32
    )
    score_grads = (weights * (weight_grads - row_inner)).astype(jnp.bfloat16)
    query_grad = (
        jnp.einsum("gjrk,kge->gjre", score_grads, keys_all, preferred_element_type=jnp.float32)
        * factor
    )
    key_grad = (
        jnp.einsum("gjrk,gjre->kge", score_grads, queries, preferred_element_type=jnp.float32)
        * factor
    )
    value_grad = jnp.einsum(
        "gjrk,gjre->kge", weights_low, out_grads, preferred_element_type=jnp.float32
    )
    return (query_grad, jnp.stack([key_grad, value_grad], axis=1).reshape(keys_all.shape[0], -1))


def local(
    queries_cross,
    outputs_grad,
    keys_shared,
    values_shared,
    stripe_order,
    segments,
    norm_input,
    norm_gain,
    weight_key,
    weight_value,
    upstream,
    weight_out,
    queries_window,
    keys_window,
    values_window,
):
    row_count = queries_cross.shape[0]
    groups = keys_shared.shape[1] // HEAD_DIM
    key_width = groups * HEAD_DIM
    shard_index = lax.axis_index("ctx")
    shard_count = lax.axis_size("ctx")
    inverse = inverse_of(stripe_order)
    first_row = shard_index * row_count
    query_place = lax.dynamic_slice_in_dim(stripe_order, first_row, row_count)
    query_segment = segments[query_place]
    keys_all, values_all = (
        lax.all_gather(keys_shared, "ctx", axis=0, tiled=True),
        lax.all_gather(values_shared, "ctx", axis=0, tiled=True),
    )
    key_segment = segments[stripe_order]
    query_grad, partial_value = cross_backward(
        split_heads(queries_cross, groups),
        split_heads(outputs_grad, groups),
        keys_all.reshape(-1, groups, HEAD_DIM),
        values_all.reshape(-1, groups, HEAD_DIM),
        query_place,
        query_segment,
        stripe_order,
        key_segment,
    )
    grad_cross = join_heads(query_grad).astype(jnp.bfloat16)
    partial_value = partial_value.reshape(partial_value.shape[0], 1, partial_value.shape[1])
    arrived = lax.all_to_all(partial_value, "ctx", split_axis=0, concat_axis=1, tiled=True)
    banded = jnp.sum(arrived, axis=1).astype(jnp.bfloat16)
    share_rows = row_count // shard_count
    placed = lax.all_to_all(
        banded.reshape(row_count, 1, banded.shape[1]),
        "ctx",
        split_axis=0,
        concat_axis=1,
        tiled=True,
    )
    source = inverse[first_row + jnp.arange(row_count, dtype=jnp.int32)]
    sender = source // row_count
    offset = source % row_count - shard_index * share_rows
    shared_grad = placed.reshape(share_rows * shard_count, banded.shape[1])[
        offset * shard_count + sender
    ]
    contract = (((1,), (1,)), ((), ()))
    normed_part = lax.dot_general(
        shared_grad[:, :key_width], weight_key, contract, preferred_element_type=jnp.float32
    )
    normed_part = normed_part + lax.dot_general(
        shared_grad[:, key_width:], weight_value, contract, preferred_element_type=jnp.float32
    )
    normed_cols = lax.psum_scatter(normed_part, "head", scatter_dimension=1, tiled=True)
    column_count = norm_input.shape[1]
    gain_cols = lax.dynamic_slice_in_dim(
        norm_gain, lax.axis_index("head") * column_count, column_count
    )
    inputs = norm_input.astype(jnp.float32)
    gained = normed_cols * gain_cols[None, :]
    square_sum, inner_sum = lax.psum(
        (jnp.sum(inputs * inputs, axis=1), jnp.sum(gained * inputs, axis=1)), "head"
    )
    scaling = lax.rsqrt(square_sum / D + 1e-06)[:, None]
    stream = (
        scaling * gained
        - inputs * scaling**3 * (inner_sum / D)[:, None]
        + upstream.astype(jnp.float32)
    )
    grad_stream = stream.astype(jnp.bfloat16)
    stream_full = lax.all_gather(grad_stream, "head", axis=1, tiled=True)
    head_grads = lax.dot_general(
        stream_full, weight_out, contract, preferred_element_type=jnp.float32
    ).astype(jnp.bfloat16)
    reach_count = WINDOW // row_count
    key_list = []
    value_list = []
    for distance in range(reach_count, 0, -1):
        earlier_keys, earlier_values = from_behind((keys_window, values_window), "ctx", distance)
        key_list.append(earlier_keys)
        value_list.append(earlier_values)
    window_keys = jnp.concatenate(key_list + [keys_window], axis=0).reshape(
        WINDOW + row_count, groups, HEAD_DIM
    )
    window_values = jnp.concatenate(value_list + [values_window], axis=0).reshape(
        WINDOW + row_count, groups, HEAD_DIM
    )
    own_place = first_row + jnp.arange(row_count, dtype=jnp.int32)
    window_place = first_row - WINDOW + jnp.arange(WINDOW + row_count, dtype=jnp.int32)
    padded = jnp.concatenate([jnp.full((WINDOW,), -1, jnp.int32), segments])
    window_segment = lax.dynamic_slice_in_dim(padded, first_row, WINDOW + row_count)
    own_segment = lax.dynamic_slice_in_dim(segments, first_row, row_count)
    allowed = (
        (window_place[None, :] <= own_place[:, None])
        & (window_place[None, :] > own_place[:, None] - WINDOW)
        & (window_segment[None, :] == own_segment[:, None])
    )
    window_qgrad, window_part = window_backward(
        split_heads(queries_window, groups),
        split_heads(head_grads, groups),
        window_keys,
        window_values,
        allowed,
    )
    grad_queries = join_heads(window_qgrad).astype(jnp.bfloat16)
    collected = window_part[WINDOW:]
    for distance in range(1, reach_count + 1):
        lower_row = (reach_count - distance) * row_count
        collected = collected + from_behind(
            window_part[lower_row : lower_row + row_count], "ctx", -distance
        )
    grad_keys = collected[:, :key_width].astype(jnp.bfloat16)
    grad_values = collected[:, key_width:].astype(jnp.bfloat16)
    return (grad_cross, grad_stream, grad_queries, grad_keys, grad_values)


def solution(mesh):
    in_specs = (
        P("ctx", "head"),
        P("ctx", "head"),
        P("ctx", "head"),
        P("ctx", "head"),
        P(),
        P(),
        P("ctx", "head"),
        P(),
        P(None, "head"),
        P(None, "head"),
        P("ctx", "head"),
        P("head", None),
        P("ctx", "head"),
        P("ctx", "head"),
        P("ctx", "head"),
    )
    out_specs = (
        P("ctx", "head"),
        P("ctx", "head"),
        P("ctx", "head"),
        P("ctx", "head"),
        P("ctx", "head"),
    )
    return jax.shard_map(local, mesh=mesh, in_specs=in_specs, out_specs=out_specs, check_vma=False)
```

profile of v0, /device:TPU:449, one launch (start us, length us, event | category | flops | bytes accessed | tf_op | source)
XLA Modules:
  0.0 827.0 jit_solution(7384837935874941985)
XLA Ops:
  13.9 45.5 %gather_fusion = s32[8192]{0:T(1024)S(1)} fusion(s32[8192]{0:T(1024)S(1)} %copy-done.1, s32[8192]{0:T(1024)S(1)} %get-tuple-element.314), kind=kCustom, calls=%fused_computation | custom fusion | bytes 98304 | tf_op jit(solution)/shard_map/gather | solution.py:168
  59.7 33.9 %all-gather.3.cloned.1.call-done = bf16[8192,128]{1,0:T(8,128)(2,1)} async-done(((bf16[128,128]{1,0:T(8,128)(2,1)}), bf16[8192,128]{1,0:T(8,128)(2,1)}) %all-gather.3.cloned.1.call-update) | async-done | bytes 2097168 | tf_op jit(solution)/shard_map/all_gather | solution.py:165
  93.6 36.7 %while.34 = (s32[]{:T(128)}, f32[16,1,3,128,512]{3,4,2,1,0:T(8,128)}, s32[16,512]{1,0:T(8,128)S(1)}, s32[128]{0:T(128)S(1)}, s32[16,512]{1,0:T(8,128)S(1)}, /*in...) while((s32[]{:T(128)}, ...), condition=%wide.region_1.2_spmd, body=%wide.region_0.0_spmd.sunk | while | flops 50921472 | bytes 1161313 | solution.py:59
  130.3 5.7 reduce_max.18
  136.0 6.2 exponential_reduce_fusion
  142.2 35.0 %all-gather.5.cloned.1.call-done = bf16[8192,128]{1,0:T(8,128)(2,1)} async-done(((bf16[128,128]{1,0:T(8,128)(2,1)}), bf16[8192,128]{1,0:T(8,128)(2,1)}) %all-gather.5.cloned.1.call-update) | async-done | bytes 2097168 | tf_op jit(solution)/shard_map/all_gather | solution.py:166
  177.2 89.0 %while.35 = (s32[]{:T(128)}, f32[1,3,128,128]{3,2,1,0:T(8,128)}, f32[16,1,3,128,512]{3,4,2,1,0:T(8,128)}, f32[1,3,128]{2,1,0:T(4,128)S(1)}, bf16[16,512,1,128]{3,1,2,0:T(8,128)(2,1)}, /*index=5*/s32[]{:T(128)}, s32[]{:T(128)}) while((s32[]{:T(128)}, f32[1,3,128,128]{3,2,1,0:T(8,128)}, f32[16,1,3,128,512]{3,4,2,1,0:T(8,128)}, ...), condition=%wide.region_5.6_spmd.clone, body=%wide.region_4.5_spmd.clone.sunk | while | flops 50823168 | bytes 4458587 | solution.py:77
  267.3 102.4 %while.36 = (s32[]{:T(128)}, f32[1,3,128,128]{3,2,1,0:T(8,128)}, f32[16,512,2,1,128]{4,2,1,0,3:T(2,128)}, f32[16,1,3,128,512]{3,4,2,1,0:T(8,128)}, f32[1,3,128]{...) while((s32[]{:T(128)}, f32[1,3,128,128]{3,2,1,0:T(8,128)}, ...), condition=%wide.region_8.9_spmd.clone, body=%wide.region_7.8_spmd.clone.sunk | while | flops 202801152 | bytes 7904439 | solution.py:100
  369.7 9.3 %all-to-all-start = ((f32[8192,1,256]{2,1,0:T(1,128)}), f32[8192,1,256]{2,1,0:T(1,128)}, u32[]{:S(2)}, u32[]{:S(2)}) async-start(f32[8192,1,256]{2,1,0:T(1,128)} %bitcast.276), calls=%async_computation | async-start | bytes 16777216 | tf_op jit(solution)/shard_map/all_to_all | solution.py:181
  381.7 5.2 collective-permute-start.2
  391.3 30.5 %scatter_custom_fusion = s32[8192]{0:T(1024)S(1)} fusion(s32[8192]{0:T(1024)S(1)} %get-tuple-element.313, s32[8192]{0:T(1024)S(1)} %iota.19, s32[]{:T(128)} %constant.61.clone.1), kind=kCustom, calls=%fused_computation.141 | custom fusion | bytes 32772 | tf_op jit(solution)/shard_map/scatter | solution.py:21
  423.0 168.4 %all-to-all-done = f32[8192,1,256]{2,1,0:T(1,128)} async-done(((f32[8192,1,256]{2,1,0:T(1,128)}), f32[8192,1,256]{2,1,0:T(1,128)}, u32[]{:S(2)}, u32[]{:S(2)}) %all-to-all-start) | async-done | bytes 8388640 | tf_op jit(solution)/shard_map/all_to_all | solution.py:181
  591.4 7.1 copy.130
  598.6 3.9 reduce_sum.69
  604.6 35.3 %all-to-all-start.1 = ((bf16[64,2,256]{2,1,0:T(2,128)(2,1)}), bf16[64,2,256]{2,1,0:T(2,128)(2,1)S(1)}, u32[]{:S(2)}, u32[]{:S(2)}) async-start(bf16[64,2,256]{2,1,0:T(2,128)(2,1)} %reshape.415), calls=%async_computation.1 | async-start | bytes 131072 | tf_op jit(solution)/shard_map/all_to_all | solution.py:184
  640.3 9.2 %all-to-all-done.1 = bf16[64,2,256]{2,1,0:T(2,128)(2,1)S(1)} async-done(((bf16[64,2,256]{2,1,0:T(2,128)(2,1)}), bf16[64,2,256]{2,1,0:T(2,128)(2,1)S(1)}, u32[]{:S(2)}, u32[]{:S(2)}) %all-to-all-start.1) | async-done | bytes 65568 | tf_op jit(solution)/shard_map/all_to_all | solution.py:184
  691.3 8.6 %reduce-scatter.2.cloned.1.call-done = f32[128,384]{1,0:T(8,128)} async-done(((f32[128,3072]{1,0:T(8,128)}), f32[128,384]{1,0:T(8,128)}) %reduce-scatter.2.cloned.1.call-update) | async-done | bytes 196624 | tf_op jit(solution)/shard_map/reduce_scatter | solution.py:204
  700.9 14.3 %all-reduce.1 = (f32[128]{0:T(128)S(1)}, f32[128]{0:T(128)S(1)}) all-reduce(f32[128]{0:T(128)S(1)} %get-tuple-element.249, f32[128]{0:T(128)S(1)} %get-tuple-element.248), channel_id=1, replica_groups=mesh['ctx'=64,'head'=8] {'head'}, use_global_device_ids=true, to_apply=%region_15.16 | all-reduce | flops 256 | bytes 2048 | tf_op jit(solution)/shard_map/psum | solution.py:211
  716.3 24.3 %all_gather.11 = bf16[128,3072]{1,0:T(8,128)(2,1)S(1)} all-gather(bf16[128,384]{1,0:T(8,128)(2,1)S(1)} %fusion.55), channel_id=1, replica_groups=mesh['ctx'=64,'head'=8] {'head'}, dimensions={1}, use_global_device_ids=true | all-gather | bytes 884736 | tf_op jit(solution)/shard_map/all_gather | solution.py:221
  748.7 15.5 %collective-permute-start.16 = (f32[128,256]{1,0:T(8,128)}, f32[128,256]{1,0:T(8,128)}, u32[]{:S(2)}, u32[]{:S(2)}) collective-permute-start(f32[128,256]{1,0:T(8,128)} %copy.102), channel_id=1, source_target_pairs={{8,0},{16,8},{24,16},{32,24},{40,32},{48,40},{56,48},{64,56},{72,6... | collective-permute-start | bytes 393224 | tf_op jit(solution)/shard_map/ppermute | solution.py:16
  765.9 7.2 collective-permute-start.17
  787.1 9.1 %collective-permute-start.20 = (f32[128,256]{1,0:T(8,128)}, f32[128,256]{1,0:T(8,128)}, u32[]{:S(2)}, u32[]{:S(2)}) collective-permute-start(f32[128,256]{1,0:T(8,128)} %copy.107), channel_id=1, source_target_pairs={{40,0},{48,8},{56,16},{64,24},{72,32},{80,40},{88,48},{96,56},{104... | collective-permute-start | bytes 393224 | tf_op jit(solution)/shard_map/ppermute | solution.py:16
  802.1 6.7 collective-permute-start.21
  808.9 3.9 collective-permute-start.22
  (426 shorter events, 326.3 us)
Async XLA Ops:
  7.2 86.4 %all-gather.3.cloned.1.call-start = ((), (), s32[]{:S(2)}) async-start(), calls=%async_computation.3 | async-start | bytes 2129920 | tf_op jit(solution)/shard_map/all_gather | solution.py:165
  7.9 169.3 %all-gather.5.cloned.1.call-start = ((), (), s32[]{:S(2)}) async-start(), calls=%async_computation.4 | async-start | bytes 2129920 | tf_op jit(solution)/shard_map/all_gather | solution.py:166
  369.7 221.7 %all-to-all-start = ((f32[8192,1,256]{2,1,0:T(1,128)}), f32[8192,1,256]{2,1,0:T(1,128)}, u32[]{:S(2)}, u32[]{:S(2)}) async-start(f32[8192,1,256]{2,1,0:T(1,128)} %bitcast.276), calls=%async_computation | async-start | bytes 16777216 | tf_op jit(solution)/shard_map/all_to_all | solution.py:181
  379.1 276.2 %collective-permute-start = (bf16[128,128]{1,0:T(8,128)(2,1)S(1)}, bf16[128,128]{1,0:T(8,128)(2,1)}, u32[]{:S(2)}, u32[]{:S(2)}) collective-permute-start(bf16[128,128]{1,0:T(8,128)(2,1)S(1)} %copy-done.17), channel_id=1, source_target_pairs={{0,64},{8,72},{16,80},{24,88},{32,96},{40,104},{48,112},{56,120},{... | collective-permute-start | bytes 98312 | tf_op jit(solution)/shard_map/ppermute | solution.py:16
  380.4 278.6 %collective-permute-start.1 = (bf16[128,128]{1,0:T(8,128)(2,1)S(1)}, bf16[128,128]{1,0:T(8,128)(2,1)}, u32[]{:S(2)}, u32[]{:S(2)}) collective-permute-start(bf16[128,128]{1,0:T(8,128)(2,1)S(1)} %copy-done.17), channel_id=1, source_target_pairs={{0,56},{8,64},{16,72},{24,80},{32,88},{40,96},{48,104},{56,112},{6... | collective-permute-start | bytes 98312 | tf_op jit(solution)/shard_map/ppermute | solution.py:16
  381.7 281.7 %collective-permute-start.2 = (bf16[128,128]{1,0:T(8,128)(2,1)S(1)}, bf16[128,128]{1,0:T(8,128)(2,1)}, u32[]{:S(2)}, u32[]{:S(2)}) collective-permute-start(bf16[128,128]{1,0:T(8,128)(2,1)S(1)} %copy-done.17), channel_id=1, source_target_pairs={{0,48},{8,56},{16,64},{24,72},{32,80},{40,88},{48,96},{56,104},{64... | collective-permute-start | bytes 98312 | tf_op jit(solution)/shard_map/ppermute | solution.py:16
  386.9 279.6 %collective-permute-start.3 = (bf16[128,128]{1,0:T(8,128)(2,1)S(1)}, bf16[128,128]{1,0:T(8,128)(2,1)}, u32[]{:S(2)}, u32[]{:S(2)}) collective-permute-start(bf16[128,128]{1,0:T(8,128)(2,1)S(1)} %copy-done.17), channel_id=1, source_target_pairs={{0,40},{8,48},{16,56},{24,64},{32,72},{40,80},{48,88},{56,96},{64,... | collective-permute-start | bytes 98312 | tf_op jit(solution)/shard_map/ppermute | solution.py:16
  388.9 279.8 %collective-permute-start.4 = (bf16[128,128]{1,0:T(8,128)(2,1)S(1)}, bf16[128,128]{1,0:T(8,128)(2,1)}, u32[]{:S(2)}, u32[]{:S(2)}) collective-permute-start(bf16[128,128]{1,0:T(8,128)(2,1)S(1)} %copy-done.17), channel_id=1, source_target_pairs={{0,32},{8,40},{16,48},{24,56},{32,64},{40,72},{48,80},{56,88},{64,... | collective-permute-start | bytes 98312 | tf_op jit(solution)/shard_map/ppermute | solution.py:16
  604.6 44.9 %all-to-all-start.1 = ((bf16[64,2,256]{2,1,0:T(2,128)(2,1)}), bf16[64,2,256]{2,1,0:T(2,128)(2,1)S(1)}, u32[]{:S(2)}, u32[]{:S(2)}) async-start(bf16[64,2,256]{2,1,0:T(2,128)(2,1)} %reshape.415), calls=%async_computation.1 | async-start | bytes 131072 | tf_op jit(solution)/shard_map/all_to_all | solution.py:184
  639.9 60.0 %reduce-scatter.2.cloned.1.call-start = ((), (), s32[]{:S(2)}) async-start(), calls=%async_computation.5 | async-start | bytes 1769472 | tf_op jit(solution)/shard_map/reduce_scatter | solution.py:204
  655.3 15.4 %collective-permute-start.5 = (bf16[128,128]{1,0:T(8,128)(2,1)S(1)}, bf16[128,128]{1,0:T(8,128)(2,1)S(1)}, u32[]{:S(2)}, u32[]{:S(2)}) collective-permute-start(bf16[128,128]{1,0:T(8,128)(2,1)S(1)} %copy-done.17), channel_id=1, source_target_pairs={{0,24},{8,32},{16,40},{24,48},{32,56},{40,64},{48,72},{56,80},{64,... | collective-permute-start | bytes 98312 | tf_op jit(solution)/shard_map/ppermute | solution.py:16
  659.0 13.7 %collective-permute-start.6 = (bf16[128,128]{1,0:T(8,128)(2,1)S(1)}, bf16[128,128]{1,0:T(8,128)(2,1)S(1)}, u32[]{:S(2)}, u32[]{:S(2)}) collective-permute-start(bf16[128,128]{1,0:T(8,128)(2,1)S(1)} %copy-done.17), channel_id=1, source_target_pairs={{0,16},{8,24},{16,32},{24,40},{32,48},{40,56},{48,64},{56,72},{64,... | collective-permute-start | bytes 98312 | tf_op jit(solution)/shard_map/ppermute | solution.py:16
  663.3 11.3 %collective-permute-start.7 = (bf16[128,128]{1,0:T(8,128)(2,1)S(1)}, bf16[128,128]{1,0:T(8,128)(2,1)S(1)}, u32[]{:S(2)}, u32[]{:S(2)}) collective-permute-start(bf16[128,128]{1,0:T(8,128)(2,1)S(1)} %copy-done.17), channel_id=1, source_target_pairs={{0,8},{8,16},{16,24},{24,32},{32,40},{40,48},{48,56},{56,64},{64,7... | collective-permute-start | bytes 98312 | tf_op jit(solution)/shard_map/ppermute | solution.py:16
  666.6 10.0 %collective-permute-start.8 = (bf16[128,128]{1,0:T(8,128)(2,1)S(1)}, bf16[128,128]{1,0:T(8,128)(2,1)S(1)}, u32[]{:S(2)}, u32[]{:S(2)}) collective-permute-start(bf16[128,128]{1,0:T(8,128)(2,1)S(1)} %copy-done.18), channel_id=1, source_target_pairs={{0,64},{8,72},{16,80},{24,88},{32,96},{40,104},{48,112},{56,120},{... | collective-permute-start | bytes 98312 | tf_op jit(solution)/shard_map/ppermute | solution.py:16
  668.7 9.9 %collective-permute-start.9 = (bf16[128,128]{1,0:T(8,128)(2,1)S(1)}, bf16[128,128]{1,0:T(8,128)(2,1)S(1)}, u32[]{:S(2)}, u32[]{:S(2)}) collective-permute-start(bf16[128,128]{1,0:T(8,128)(2,1)S(1)} %copy-done.18), channel_id=1, source_target_pairs={{0,56},{8,64},{16,72},{24,80},{32,88},{40,96},{48,104},{56,112},{6... | collective-permute-start | bytes 98312 | tf_op jit(solution)/shard_map/ppermute | solution.py:16
  672.7 10.5 %collective-permute-start.11 = (bf16[128,128]{1,0:T(8,128)(2,1)S(1)}, bf16[128,128]{1,0:T(8,128)(2,1)S(1)}, u32[]{:S(2)}, u32[]{:S(2)}) collective-permute-start(bf16[128,128]{1,0:T(8,128)(2,1)S(1)} %copy-done.18), channel_id=1, source_target_pairs={{0,40},{8,48},{16,56},{24,64},{32,72},{40,80},{48,88},{56,96},{64,... | collective-permute-start | bytes 98312 | tf_op jit(solution)/shard_map/ppermute | solution.py:16
  676.6 11.1 %collective-permute-start.13 = (bf16[128,128]{1,0:T(8,128)(2,1)S(1)}, bf16[128,128]{1,0:T(8,128)(2,1)S(1)}, u32[]{:S(2)}, u32[]{:S(2)}) collective-permute-start(bf16[128,128]{1,0:T(8,128)(2,1)S(1)} %copy-done.18), channel_id=1, source_target_pairs={{0,24},{8,32},{16,40},{24,48},{32,56},{40,64},{48,72},{56,80},{64,... | collective-permute-start | bytes 98312 | tf_op jit(solution)/shard_map/ppermute | solution.py:16
  678.5 9.9 %collective-permute-start.14 = (bf16[128,128]{1,0:T(8,128)(2,1)S(1)}, bf16[128,128]{1,0:T(8,128)(2,1)S(1)}, u32[]{:S(2)}, u32[]{:S(2)}) collective-permute-start(bf16[128,128]{1,0:T(8,128)(2,1)S(1)} %copy-done.18), channel_id=1, source_target_pairs={{0,16},{8,24},{16,32},{24,40},{32,48},{40,56},{48,64},{56,72},{64,... | collective-permute-start | bytes 98312 | tf_op jit(solution)/shard_map/ppermute | solution.py:16
  748.7 53.4 %collective-permute-start.16 = (f32[128,256]{1,0:T(8,128)}, f32[128,256]{1,0:T(8,128)}, u32[]{:S(2)}, u32[]{:S(2)}) collective-permute-start(f32[128,256]{1,0:T(8,128)} %copy.102), channel_id=1, source_target_pairs={{8,0},{16,8},{24,16},{32,24},{40,32},{48,40},{56,48},{64,56},{72,6... | collective-permute-start | bytes 393224 | tf_op jit(solution)/shard_map/ppermute | solution.py:16
  765.9 43.0 %collective-permute-start.17 = (f32[128,256]{1,0:T(8,128)}, f32[128,256]{1,0:T(8,128)}, u32[]{:S(2)}, u32[]{:S(2)}) collective-permute-start(f32[128,256]{1,0:T(8,128)} %copy.104), channel_id=1, source_target_pairs={{16,0},{24,8},{32,16},{40,24},{48,32},{56,40},{64,48},{72,56},{80,... | collective-permute-start | bytes 393224 | tf_op jit(solution)/shard_map/ppermute | solution.py:16
  774.7 38.1 %collective-permute-start.18 = (f32[128,256]{1,0:T(8,128)}, f32[128,256]{1,0:T(8,128)}, u32[]{:S(2)}, u32[]{:S(2)}) collective-permute-start(f32[128,256]{1,0:T(8,128)} %copy.105), channel_id=1, source_target_pairs={{24,0},{32,8},{40,16},{48,24},{56,32},{64,40},{72,48},{80,56},{88,... | collective-permute-start | bytes 393224 | tf_op jit(solution)/shard_map/ppermute | solution.py:16
  782.2 36.3 %collective-permute-start.19 = (f32[128,256]{1,0:T(8,128)}, f32[128,256]{1,0:T(8,128)}, u32[]{:S(2)}, u32[]{:S(2)}) collective-permute-start(f32[128,256]{1,0:T(8,128)} %copy.106), channel_id=1, source_target_pairs={{32,0},{40,8},{48,16},{56,24},{64,32},{72,40},{80,48},{88,56},{96,... | collective-permute-start | bytes 393224 | tf_op jit(solution)/shard_map/ppermute | solution.py:16
  787.1 31.4 %collective-permute-start.20 = (f32[128,256]{1,0:T(8,128)}, f32[128,256]{1,0:T(8,128)}, u32[]{:S(2)}, u32[]{:S(2)}) collective-permute-start(f32[128,256]{1,0:T(8,128)} %copy.107), channel_id=1, source_target_pairs={{40,0},{48,8},{56,16},{64,24},{72,32},{80,40},{88,48},{96,56},{104... | collective-permute-start | bytes 393224 | tf_op jit(solution)/shard_map/ppermute | solution.py:16
  802.1 16.3 %collective-permute-start.21 = (f32[128,256]{1,0:T(8,128)}, f32[128,256]{1,0:T(8,128)}, u32[]{:S(2)}, u32[]{:S(2)}) collective-permute-start(f32[128,256]{1,0:T(8,128)} %copy.108), channel_id=1, source_target_pairs={{48,0},{56,8},{64,16},{72,24},{80,32},{88,40},{96,48},{104,56},{11... | collective-permute-start | bytes 393224 | tf_op jit(solution)/shard_map/ppermute | solution.py:16
  (54 other events, 1123.1 us)
Sparse Core Ops, SparseCore 0:
  11.4 82.1 all-gather.2
  96.9 80.2 all-gather.4
  653.6 46.1 reduce-scatter.1
where the time goes:
time: 842 us; the launch traced here: 827 us
  waiting for transfers between devices  262 us (31%)
  local copies, waits for them, and re-layouts  204 us (24%)
  matrix products  145 us (17%)
  starting transfers between devices  133 us (16%)
  blocking collectives  38.7 us (5%)
  other arithmetic  28.6 us (3%)
  between operations  14.5 us (2%)
    all_to_all x1, waiting for transfers between devices, local(): lax.all_to_all(partial_value, 'ctx', split_axis=0, concat_axis=1, tiled=T...  168 us
    ppermute x24, starting transfers between devices, from_behind(): lax.ppermute(value, axis, [(source, source + steps) for source in range(f...  87.9 us
    dynamic_slice x32, local copies, waits for them, and re-layouts, cross_backward(): output, unused = lax.scan(forward_step, start_value, (stored, value_blocks))  56.9 us
    gather x1, local copies, waits for them, and re-layouts, local(): key_segment = segments[stripe_order]  45.5 us
    all_to_all x1, starting transfers between devices, local(): lax.all_to_all(banded.reshape(row_count, 1, banded.shape[1]), 'ctx', spli...  35.3 us
    all_gather x1, waiting for transfers between devices, local(): lax.all_gather(values_shared, 'ctx', axis=0, tiled=True)  35 us
    all_gather x1, waiting for transfers between devices, local(): lax.all_gather(keys_shared, 'ctx', axis=0, tiled=True)  33.9 us
    dot_general x16, matrix products, masked_scores(): jnp.einsum('gjre,kge->gjrk', queries, key_block, preferred_element_type=j...  33.2 us
  transfers between devices with their start and end apart: 29, of which 9 were waited for; matrix products, arithmetic and copies ran while one was open for 21% of the time, Pallas kernels for 0%

commit v1 on v0

v1 whole, which is shorter than its diff:
```python
import jax
import jax.numpy as jnp
from jax import lax
from jax.sharding import PartitionSpec as P

D = 3072
HEADS = 24
KV_HEADS = 8
HEAD_DIM = 128
WINDOW = 1024
DOCS = 8
QUERY_BLOCKS = 4


def from_behind(value, axis, steps):
    count = lax.axis_size(axis)
    first, last = (max(0, -steps), min(count, count - steps))
    return lax.ppermute(value, axis, [(source, source + steps) for source in range(first, last)])


def segment_of(segments, places):
    levels = jnp.arange(1, DOCS, dtype=jnp.int32)
    starts = jnp.sum((segments[None, :] < levels[:, None]).astype(jnp.int32), axis=1)
    return jnp.sum((places[..., None] >= starts).astype(jnp.int32), axis=-1)


def split_heads(matrix):
    row_count = matrix.shape[0]
    return matrix.reshape(row_count, -1, HEAD_DIM).transpose(1, 0, 2)


def join_heads(tensor):
    heads, row_count, width = tensor.shape
    return tensor.transpose(1, 0, 2).reshape(row_count, heads * width)


def attend_block(queries, out_grads, keys, values, allowed):
    factor = HEAD_DIM ** (-0.5)
    scores = (
        jnp.einsum("hre,ke->hrk", queries, keys, preferred_element_type=jnp.float32) * factor
    )
    scores = jnp.where(allowed[None], scores, -jnp.inf)
    row_peak = jnp.max(scores, axis=2, keepdims=True)
    logsum = row_peak + jnp.log(jnp.sum(jnp.exp(scores - row_peak), axis=2, keepdims=True))
    weights = jnp.exp(scores - logsum)
    weights_low = weights.astype(jnp.bfloat16)
    output = jnp.einsum("hrk,ke->hre", weights_low, values, preferred_element_type=jnp.float32)
    row_inner = jnp.sum(out_grads.astype(jnp.float32) * output, axis=2, keepdims=True)
    weight_grads = jnp.einsum(
        "hre,ke->hrk", out_grads, values, preferred_element_type=jnp.float32
    )
    score_grads = (weights * (weight_grads - row_inner)).astype(jnp.bfloat16)
    query_grad = (
        jnp.einsum("hrk,ke->hre", score_grads, keys, preferred_element_type=jnp.float32) * factor
    )
    key_grad = (
        jnp.einsum("hrk,hre->ke", score_grads, queries, preferred_element_type=jnp.float32)
        * factor
    )
    value_grad = jnp.einsum(
        "hrk,hre->ke", weights_low, out_grads, preferred_element_type=jnp.float32
    )
    return query_grad, key_grad, value_grad


def local(
    queries_cross,
    outputs_grad,
    keys_shared,
    values_shared,
    stripe_order,
    segments,
    norm_input,
    norm_gain,
    weight_key,
    weight_value,
    upstream,
    weight_out,
    queries_window,
    keys_window,
    values_window,
):
    row_count = queries_cross.shape[0]
    total_rows = stripe_order.shape[0]
    key_width = keys_shared.shape[1]
    shard_index = lax.axis_index("ctx")
    shard_count = lax.axis_size("ctx")
    stripe = total_rows // row_count
    first_row = shard_index * row_count

    shared = jnp.concatenate([keys_shared, values_shared], axis=1)
    gathered = lax.all_gather(shared, "ctx", axis=0, tiled=True)
    ordered = (
        gathered.reshape(shard_count, row_count, 2 * key_width)
        .transpose(1, 0, 2)
        .reshape(total_rows, 2 * key_width)
    )
    order_table = stripe_order.reshape(shard_count, row_count)
    key_place = order_table.T.reshape(total_rows)
    key_segment = segment_of(segments, key_place)
    query_place = lax.dynamic_slice_in_dim(stripe_order, first_row, row_count)
    query_segment = segment_of(segments, query_place)
    queries = split_heads(queries_cross)
    out_grads = split_heads(outputs_grad)
    block_rows = row_count // QUERY_BLOCKS
    query_grads = []
    key_total = jnp.zeros((total_rows, key_width), jnp.float32)
    value_total = jnp.zeros((total_rows, key_width), jnp.float32)
    for block in range(QUERY_BLOCKS):
        low = block * block_rows
        reach = (low + block_rows) * stripe
        block_place = query_place[low : low + block_rows]
        block_segment = query_segment[low : low + block_rows]
        allowed = (key_place[None, :reach] <= block_place[:, None]) & (
            key_segment[None, :reach] == block_segment[:, None]
        )
        query_grad, key_grad, value_grad = attend_block(
            queries[:, low : low + block_rows],
            out_grads[:, low : low + block_rows],
            ordered[:reach, :key_width],
            ordered[:reach, key_width:],
            allowed,
        )
        query_grads.append(query_grad)
        pad = ((0, total_rows - reach), (0, 0))
        key_total = key_total + jnp.pad(key_grad, pad)
        value_total = value_total + jnp.pad(value_grad, pad)
    grad_cross = join_heads(jnp.concatenate(query_grads, axis=1)).astype(jnp.bfloat16)

    partial = jnp.concatenate([key_total, value_total], axis=1)
    summed = lax.psum_scatter(partial, "ctx", scatter_dimension=0, tiled=True).astype(
        jnp.bfloat16
    )
    per_shard = row_count // stripe
    held_place = (
        lax.dynamic_slice_in_dim(order_table, shard_index * per_shard, per_shard, axis=1)
        .T.reshape(row_count)
    )
    local_place = held_place - first_row
    placement = (
        local_place[None, :] == jnp.arange(row_count, dtype=jnp.int32)[:, None]
    ).astype(jnp.bfloat16)
    shared_grad = jnp.dot(placement, summed, preferred_element_type=jnp.float32).astype(
        jnp.bfloat16
    )

    contract = (((1,), (1,)), ((), ()))
    normed_part = lax.dot_general(
        shared_grad[:, :key_width], weight_key, contract, preferred_element_type=jnp.float32
    )
    normed_part = normed_part + lax.dot_general(
        shared_grad[:, key_width:], weight_value, contract, preferred_element_type=jnp.float32
    )
    normed_cols = lax.psum_scatter(normed_part, "head", scatter_dimension=1, tiled=True)
    column_count = norm_input.shape[1]
    gain_cols = lax.dynamic_slice_in_dim(
        norm_gain, lax.axis_index("head") * column_count, column_count
    )
    inputs = norm_input.astype(jnp.float32)
    gained = normed_cols * gain_cols[None, :]
    square_sum, inner_sum = lax.psum(
        (jnp.sum(inputs * inputs, axis=1), jnp.sum(gained * inputs, axis=1)), "head"
    )
    scaling = lax.rsqrt(square_sum / D + 1e-06)[:, None]
    stream = (
        scaling * gained
        - inputs * scaling**3 * (inner_sum / D)[:, None]
        + upstream.astype(jnp.float32)
    )
    grad_stream = stream.astype(jnp.bfloat16)
    stream_full = lax.all_gather(grad_stream, "head", axis=1, tiled=True)
    head_grads = lax.dot_general(
        stream_full, weight_out, contract, preferred_element_type=jnp.float32
    ).astype(jnp.bfloat16)

    reach_count = WINDOW // row_count
    own_window = jnp.concatenate([keys_window, values_window], axis=1)
    pieces = [from_behind(own_window, "ctx", distance) for distance in range(reach_count, 0, -1)]
    window_all = jnp.concatenate(pieces + [own_window], axis=0)
    own_place = first_row + jnp.arange(row_count, dtype=jnp.int32)
    window_place = first_row - WINDOW + jnp.arange(WINDOW + row_count, dtype=jnp.int32)
    padded = jnp.concatenate([jnp.full((WINDOW,), -1, jnp.int32), segments])
    window_segment = lax.dynamic_slice_in_dim(padded, first_row, WINDOW + row_count)
    own_segment = lax.dynamic_slice_in_dim(segments, first_row, row_count)
    allowed = (
        (window_place[None, :] <= own_place[:, None])
        & (window_place[None, :] > own_place[:, None] - WINDOW)
        & (window_segment[None, :] == own_segment[:, None])
    )
    window_qgrad, window_kgrad, window_vgrad = attend_block(
        split_heads(queries_window),
        split_heads(head_grads),
        window_all[:, :key_width],
        window_all[:, key_width:],
        allowed,
    )
    grad_queries = join_heads(window_qgrad).astype(jnp.bfloat16)
    window_part = jnp.concatenate([window_kgrad, window_vgrad], axis=1)
    collected = window_part[WINDOW:]
    for distance in range(1, reach_count + 1):
        lower_row = (reach_count - distance) * row_count
        collected = collected + from_behind(
            window_part[lower_row : lower_row + row_count], "ctx", -distance
        )
    grad_keys = collected[:, :key_width].astype(jnp.bfloat16)
    grad_values = collected[:, key_width:].astype(jnp.bfloat16)
    return (grad_cross, grad_stream, grad_queries, grad_keys, grad_values)


def solution(mesh):
    in_specs = (
        P("ctx", "head"),
        P("ctx", "head"),
        P("ctx", "head"),
        P("ctx", "head"),
        P(),
        P(),
        P("ctx", "head"),
        P(),
        P(None, "head"),
        P(None, "head"),
        P("ctx", "head"),
        P("head", None),
        P("ctx", "head"),
        P("ctx", "head"),
        P("ctx", "head"),
    )
    out_specs = (
        P("ctx", "head"),
        P("ctx", "head"),
        P("ctx", "head"),
        P("ctx", "head"),
        P("ctx", "head"),
    )
    return jax.shard_map(local, mesh=mesh, in_specs=in_specs, out_specs=out_specs, check_vma=False)
```

time: 842 us -> 459 us (0.55); the launches traced: 827 us -> 456 us
  local copies, waits for them, and re-layouts: 204 us -> 33.2 us
  matrix products: 145 us -> 30.1 us
  starting transfers between devices: 133 us -> 71.5 us
  waiting for transfers between devices: 262 us -> 249 us
  other arithmetic: 28.6 us -> 19.5 us
    all_to_all x2 -> x0, waiting for transfers between devices: 178 us -> none  [the longest x1 168 us: local(): lax.all_to_all(partial_value, 'ctx', split_axis=0, concat_axis=1, tiled=T...]
    reduce_scatter x0 -> x1, waiting for transfers between devices: none -> 148 us  [local(): lax.psum_scatter(partial, 'ctx', scatter_dimension=0, tiled=True)]
    dot_general x102 -> x31, matrix products: 142 us -> 26.3 us  [the longest x5 6.83 us: attend_block(): jnp.einsum('hrk,ke->hre', score_grads, keys, preferred_element_type=jnp.f...]
    dynamic_slice x48 -> x1, local copies, waits for them, and re-layouts: 57 us -> 0.8 us  [local(): query_place = lax.dynamic_slice_in_dim(stripe_order, first_row, row_count)]
    gather x4 -> x0, local copies, waits for them, and re-layouts: 49.2 us -> none  [the longest x1 45.5 us: local(): key_segment = segments[stripe_order]]
    all_to_all x2 -> x0, starting transfers between devices: 44.7 us -> none  [the longest x1 35.3 us: local(): lax.all_to_all(banded.reshape(row_count, 1, banded.shape[1]), 'ctx', spli...]
    scatter x1 -> x0, local copies, waits for them, and re-layouts: 30.5 us -> none  [inverse_of(): jnp.zeros((length,), jnp.int32).at[permutation]]
    dynamic_update_slice x16 -> x0, local copies, waits for them, and re-layouts: 19.4 us -> none  [cross_backward(): lax.scan(backward_step, start_value, (stored, key_blocks, value_blocks))]
  transfers between devices with their start and end apart: 29 -> 19, of which waited for: 9 -> 6; matrix products, arithmetic and copies ran while one was open for 21% -> 10% of each run, Pallas kernels for 0% -> 0%
where the time goes in v1:
time: 459 us; the launch traced here: 456 us
  waiting for transfers between devices  249 us (54%)
  starting transfers between devices  71.5 us (16%)
  blocking collectives  39 us (8%)
  local copies, waits for them, and re-layouts  33.2 us (7%)
  matrix products  30.1 us (7%)
  other arithmetic  19.5 us (4%)
  between operations  14.5 us (3%)
    reduce_scatter x1, waiting for transfers between devices, local(): lax.psum_scatter(partial, 'ctx', scatter_dimension=0, tiled=True)  148 us
    all_gather x1, waiting for transfers between devices, local(): gathered = lax.all_gather(shared, 'ctx', axis=0, tiled=True)  79 us
    ppermute x16, starting transfers between devices, from_behind(): lax.ppermute(value, axis, [(source, source + steps) for source in range(f...  71.3 us
    all_gather x1, blocking collectives, local(): stream_full = lax.all_gather(grad_stream, 'head', axis=1, tiled=True)  24.2 us
    unnamed x71, local copies, waits for them, and re-layouts  16.5 us
    psum x1, blocking collectives, local(): lax.psum((jnp.sum(inputs * inputs, axis=1), jnp.sum(gained * inputs, axis...  14.8 us
    reduce_scatter x1, waiting for transfers between devices, local(): lax.psum_scatter(normed_part, 'head', scatter_dimension=1, tiled=True)  12.4 us
    ppermute x16, waiting for transfers between devices, from_behind(): lax.ppermute(value, axis, [(source, source + steps) for source in range(f...  9.22 us
  transfers between devices with their start and end apart: 19, of which 6 were waited for; matrix products, arithmetic and copies ran while one was open for 10% of the time, Pallas kernels for 0%

profile of v1, /device:TPU:449, one launch (start us, length us, event | category | flops | bytes accessed | tf_op | source)
XLA Modules:
  0.0 456.3 jit_solution(13607392537910475668)
XLA Ops:
  17.9 79.0 %all-gather.2.cloned.1.call-done = bf16[8192,256]{1,0:T(8,128)(2,1)} async-done(((bf16[128,256]{1,0:T(8,128)(2,1)}), bf16[8192,256]{1,0:T(8,128)(2,1)}) %all-gather.2.cloned.1.call-update) | async-done | bytes 4194320 | tf_op jit(solution)/shard_map/all_gather | solution.py:92
  96.9 4.6 copy.87
  117.1 3.8 pad_maximum_fusion
  126.3 3.5 collective-permute-start.2
  129.8 1.9 collective-permute-start.3
  131.7 2.2 collective-permute-start.4
  139.3 147.8 %reduce-scatter.3.cloned.1.call-done = f32[128,256]{0,1:T(8,128)} async-done(((f32[8192,256]{0,1:T(8,128)}), f32[128,256]{0,1:T(8,128)}) %reduce-scatter.3.cloned.1.call-update) | async-done | bytes 131088 | tf_op jit(solution)/shard_map/reduce_scatter | solution.py:131
  291.4 2.1 compare_and_fusion.2
  295.9 9.6 %collective-permute-start.5 = (bf16[128,256]{1,0:T(8,128)(2,1)}, bf16[128,256]{1,0:T(8,128)(2,1)S(1)}, u32[]{:S(2)}, u32[]{:S(2)}) collective-permute-start(bf16[128,256]{1,0:T(8,128)(2,1)} %constant_dynamic-update-slice_fusion), channel_id=1, source_target_pairs={{0,24},{8,32},{16,40},{24,48},{32,56},{40,64},{48,72},{56,80},{64,... | collective-permute-start | bytes 196616 | tf_op jit(solution)/shard_map/ppermute | solution.py:18
  306.3 3.3 collective-permute-start.6
  323.6 12.4 %reduce-scatter.5.cloned.1.call-done = f32[128,384]{1,0:T(8,128)} async-done(((f32[128,3072]{1,0:T(8,128)}), f32[128,384]{1,0:T(8,128)}) %reduce-scatter.5.cloned.1.call-update) | async-done | bytes 196624 | tf_op jit(solution)/shard_map/reduce_scatter | solution.py:154
  337.1 14.8 %all-reduce.7 = (f32[128]{0:T(128)S(1)}, f32[128]{0:T(128)S(1)}) all-reduce(f32[128]{0:T(128)S(1)} %get-tuple-element.26, f32[128]{0:T(128)S(1)} %get-tuple-element.25), channel_id=1, replica_groups=mesh['ctx'=64,'head'=8] {'head'}, use_global_device_ids=true, to_apply=%region_20.21 | all-reduce | flops 256 | bytes 2048 | tf_op jit(solution)/shard_map/psum | solution.py:161
  353.7 24.2 %all_gather.7 = bf16[128,3072]{1,0:T(8,128)(2,1)S(1)} all-gather(bf16[128,384]{1,0:T(8,128)(2,1)S(1)} %fusion.66), channel_id=1, replica_groups=mesh['ctx'=64,'head'=8] {'head'}, dimensions={1}, use_global_device_ids=true | all-gather | bytes 884736 | tf_op jit(solution)/shard_map/all_gather | solution.py:171
  378.8 2.1 fusion.40
  383.4 5.0 %collective-permute-start.15 = (f32[128,256]{0,1:T(8,128)}, f32[128,256]{0,1:T(8,128)}, u32[]{:S(2)}, u32[]{:S(2)}) collective-permute-start(f32[128,256]{0,1:T(8,128)} %get-tuple-element.35), channel_id=1, source_target_pairs={{64,0},{72,8},{80,16},{88,24},{96,32},{104,40},{112,48},{120,56},{... | collective-permute-start | bytes 393224 | tf_op jit(solution)/shard_map/ppermute | solution.py:18
  388.3 17.6 %collective-permute-start.14 = (f32[128,256]{0,1:T(8,128)}, f32[128,256]{0,1:T(8,128)}, u32[]{:S(2)}, u32[]{:S(2)}) collective-permute-start(f32[128,256]{0,1:T(8,128)} %get-tuple-element.36), channel_id=1, source_target_pairs={{56,0},{64,8},{72,16},{80,24},{88,32},{96,40},{104,48},{112,56},{1... | collective-permute-start | bytes 393224 | tf_op jit(solution)/shard_map/ppermute | solution.py:18
  405.9 5.2 %collective-permute-start.13 = (f32[128,256]{0,1:T(8,128)}, f32[128,256]{0,1:T(8,128)}, u32[]{:S(2)}, u32[]{:S(2)}) collective-permute-start(f32[128,256]{0,1:T(8,128)} %get-tuple-element.34), channel_id=1, source_target_pairs={{48,0},{56,8},{64,16},{72,24},{80,32},{88,40},{96,48},{104,56},{11... | collective-permute-start | bytes 393224 | tf_op jit(solution)/shard_map/ppermute | solution.py:18
  416.4 2.5 collective-permute-start.12
  419.0 4.4 collective-permute-start.11
  423.4 3.1 collective-permute-start.10
  426.5 3.7 collective-permute-start.9
  430.2 4.9 %collective-permute-start.8 = (f32[128,256]{0,1:T(8,128)}, f32[128,256]{0,1:T(8,128)}, u32[]{:S(2)}, u32[]{:S(2)}) collective-permute-start(f32[128,256]{0,1:T(8,128)} %get-tuple-element.29), channel_id=1, source_target_pairs={{8,0},{16,8},{24,16},{32,24},{40,32},{48,40},{56,48},{64,56},{72,6... | collective-permute-start | bytes 393224 | tf_op jit(solution)/shard_map/ppermute | solution.py:18
  435.1 2.3 fusion.39
  439.0 7.4 %collective-permute-done.9 = f32[128,256]{0,1:T(8,128)} collective-permute-done((f32[128,256]{0,1:T(8,128)}, f32[128,256]{0,1:T(8,128)}, u32[]{:S(2)}, u32[]{:S(2)}) %collective-permute-start.9) | collective-permute-done | bytes 131104 | tf_op jit(solution)/shard_map/ppermute | solution.py:18
  (180 shorter events, 74.5 us)
Async XLA Ops:
  7.2 370.7 %copy-start = (bf16[384,3072]{1,0:T(8,128)(2,1)S(1)}, bf16[384,3072]{1,0:T(8,128)(2,1)}, u32[]{:S(2)}) copy-start(bf16[384,3072]{1,0:T(8,128)(2,1)} %param.26) | copy-start | bytes 7077892
  7.2 89.8 %all-gather.2.cloned.1.call-start = ((), (), s32[]{:S(2)}) async-start(), calls=%async_computation.2 | async-start | bytes 4259840 | tf_op jit(solution)/shard_map/all_gather | solution.py:92
  8.8 278.4 %reduce-scatter.3.cloned.1.call-start = ((), (), s32[]{:S(2)}) async-start(), calls=%async_computation.3 | async-start | bytes 8519680 | tf_op jit(solution)/shard_map/reduce_scatter | solution.py:131
  12.2 95.4 %copy-start.18 = (bf16[128,3,128]{2,0,1:T(8,128)(2,1)}, bf16[128,3,128]{2,0,1:T(8,128)(2,1)S(1)}, u32[]{:S(2)}) copy-start(bf16[128,3,128]{2,0,1:T(8,128)(2,1)S(1)} %copy.89) | copy-start | bytes 294916
  14.1 95.7 %copy-start.12 = (bf16[128,3,128]{2,0,1:T(8,128)(2,1)}, bf16[128,3,128]{2,0,1:T(8,128)(2,1)S(1)}, u32[]{:S(2)}) copy-start(bf16[128,3,128]{2,0,1:T(8,128)(2,1)S(1)} %copy.91) | copy-start | bytes 294916
  120.9 215.2 %reduce-scatter.5.cloned.1.call-start = ((), (), s32[]{:S(2)}) async-start(), calls=%async_computation.4 | async-start | bytes 1769472 | tf_op jit(solution)/shard_map/reduce_scatter | solution.py:154
  123.7 172.2 %collective-permute-start = (bf16[128,256]{1,0:T(8,128)(2,1)}, bf16[128,256]{1,0:T(8,128)(2,1)}, u32[]{:S(2)}, u32[]{:S(2)}) collective-permute-start(bf16[128,256]{1,0:T(8,128)(2,1)} %constant_dynamic-update-slice_fusion), channel_id=1, source_target_pairs={{0,64},{8,72},{16,80},{24,88},{32,96},{40,104},{48,112},{56,120},{... | collective-permute-start | bytes 196616 | tf_op jit(solution)/shard_map/ppermute | solution.py:18
  125.0 181.4 %collective-permute-start.1 = (bf16[128,256]{1,0:T(8,128)(2,1)}, bf16[128,256]{1,0:T(8,128)(2,1)}, u32[]{:S(2)}, u32[]{:S(2)}) collective-permute-start(bf16[128,256]{1,0:T(8,128)(2,1)} %constant_dynamic-update-slice_fusion), channel_id=1, source_target_pairs={{0,56},{8,64},{16,72},{24,80},{32,88},{40,96},{48,104},{56,112},{6... | collective-permute-start | bytes 196616 | tf_op jit(solution)/shard_map/ppermute | solution.py:18
  126.3 184.2 %collective-permute-start.2 = (bf16[128,256]{1,0:T(8,128)(2,1)}, bf16[128,256]{1,0:T(8,128)(2,1)}, u32[]{:S(2)}, u32[]{:S(2)}) collective-permute-start(bf16[128,256]{1,0:T(8,128)(2,1)} %constant_dynamic-update-slice_fusion), channel_id=1, source_target_pairs={{0,48},{8,56},{16,64},{24,72},{32,80},{40,88},{48,96},{56,104},{64... | collective-permute-start | bytes 196616 | tf_op jit(solution)/shard_map/ppermute | solution.py:18
  129.8 183.5 %collective-permute-start.3 = (bf16[128,256]{1,0:T(8,128)(2,1)}, bf16[128,256]{1,0:T(8,128)(2,1)}, u32[]{:S(2)}, u32[]{:S(2)}) collective-permute-start(bf16[128,256]{1,0:T(8,128)(2,1)} %constant_dynamic-update-slice_fusion), channel_id=1, source_target_pairs={{0,40},{8,48},{16,56},{24,64},{32,72},{40,80},{48,88},{56,96},{64,... | collective-permute-start | bytes 196616 | tf_op jit(solution)/shard_map/ppermute | solution.py:18
  131.7 182.4 %collective-permute-start.4 = (bf16[128,256]{1,0:T(8,128)(2,1)}, bf16[128,256]{1,0:T(8,128)(2,1)}, u32[]{:S(2)}, u32[]{:S(2)}) collective-permute-start(bf16[128,256]{1,0:T(8,128)(2,1)} %constant_dynamic-update-slice_fusion), channel_id=1, source_target_pairs={{0,32},{8,40},{16,48},{24,56},{32,64},{40,72},{48,80},{56,88},{64,... | collective-permute-start | bytes 196616 | tf_op jit(solution)/shard_map/ppermute | solution.py:18
  295.9 19.1 %collective-permute-start.5 = (bf16[128,256]{1,0:T(8,128)(2,1)}, bf16[128,256]{1,0:T(8,128)(2,1)S(1)}, u32[]{:S(2)}, u32[]{:S(2)}) collective-permute-start(bf16[128,256]{1,0:T(8,128)(2,1)} %constant_dynamic-update-slice_fusion), channel_id=1, source_target_pairs={{0,24},{8,32},{16,40},{24,48},{32,56},{40,64},{48,72},{56,80},{64,... | collective-permute-start | bytes 196616 | tf_op jit(solution)/shard_map/ppermute | solution.py:18
  306.3 9.9 %collective-permute-start.6 = (bf16[128,256]{1,0:T(8,128)(2,1)}, bf16[128,256]{1,0:T(8,128)(2,1)S(1)}, u32[]{:S(2)}, u32[]{:S(2)}) collective-permute-start(bf16[128,256]{1,0:T(8,128)(2,1)} %constant_dynamic-update-slice_fusion), channel_id=1, source_target_pairs={{0,16},{8,24},{16,32},{24,40},{32,48},{40,56},{48,64},{56,72},{64,... | collective-permute-start | bytes 196616 | tf_op jit(solution)/shard_map/ppermute | solution.py:18
  310.5 5.8 %collective-permute-start.7 = (bf16[128,256]{1,0:T(8,128)(2,1)}, bf16[128,256]{1,0:T(8,128)(2,1)S(1)}, u32[]{:S(2)}, u32[]{:S(2)}) collective-permute-start(bf16[128,256]{1,0:T(8,128)(2,1)} %constant_dynamic-update-slice_fusion), channel_id=1, source_target_pairs={{0,8},{8,16},{16,24},{24,32},{32,40},{40,48},{48,56},{56,64},{64,7... | collective-permute-start | bytes 196616 | tf_op jit(solution)/shard_map/ppermute | solution.py:18
  381.9 30.6 %copy-start.5 = (bf16[3,128,1152]{1,2,0:T(8,128)(2,1)}, bf16[3,128,1152]{1,2,0:T(8,128)(2,1)S(1)}, u32[]{:S(2)}) copy-start(bf16[3,128,1152]{1,2,0:T(8,128)(2,1)S(1)} %fusion.23) | copy-start | bytes 2654212
  381.9 30.6 %copy-start.24 = (bf16[3,32,128]{2,1,0:T(8,128)(2,1)S(1)}, bf16[3,32,128]{2,1,0:T(8,128)(2,1)}, u32[]{:S(2)}) copy-start(bf16[3,32,128]{2,1,0:T(8,128)(2,1)} %fusion.46) | copy-start | bytes 73732
  383.4 40.0 %collective-permute-start.15 = (f32[128,256]{0,1:T(8,128)}, f32[128,256]{0,1:T(8,128)}, u32[]{:S(2)}, u32[]{:S(2)}) collective-permute-start(f32[128,256]{0,1:T(8,128)} %get-tuple-element.35), channel_id=1, source_target_pairs={{64,0},{72,8},{80,16},{88,24},{96,32},{104,40},{112,48},{120,56},{... | collective-permute-start | bytes 393224 | tf_op jit(solution)/shard_map/ppermute | solution.py:18
  388.3 38.2 %collective-permute-start.14 = (f32[128,256]{0,1:T(8,128)}, f32[128,256]{0,1:T(8,128)}, u32[]{:S(2)}, u32[]{:S(2)}) collective-permute-start(f32[128,256]{0,1:T(8,128)} %get-tuple-element.36), channel_id=1, source_target_pairs={{56,0},{64,8},{72,16},{80,24},{88,32},{96,40},{104,48},{112,56},{1... | collective-permute-start | bytes 393224 | tf_op jit(solution)/shard_map/ppermute | solution.py:18
  405.9 24.3 %collective-permute-start.13 = (f32[128,256]{0,1:T(8,128)}, f32[128,256]{0,1:T(8,128)}, u32[]{:S(2)}, u32[]{:S(2)}) collective-permute-start(f32[128,256]{0,1:T(8,128)} %get-tuple-element.34), channel_id=1, source_target_pairs={{48,0},{56,8},{64,16},{72,24},{80,32},{88,40},{96,48},{104,56},{11... | collective-permute-start | bytes 393224 | tf_op jit(solution)/shard_map/ppermute | solution.py:18
  416.4 22.6 %collective-permute-start.12 = (f32[128,256]{0,1:T(8,128)}, f32[128,256]{0,1:T(8,128)}, u32[]{:S(2)}, u32[]{:S(2)}) collective-permute-start(f32[128,256]{0,1:T(8,128)} %get-tuple-element.33), channel_id=1, source_target_pairs={{40,0},{48,8},{56,16},{64,24},{72,32},{80,40},{88,48},{96,56},{104... | collective-permute-start | bytes 393224 | tf_op jit(solution)/shard_map/ppermute | solution.py:18
  419.0 20.0 %collective-permute-start.11 = (f32[128,256]{0,1:T(8,128)}, f32[128,256]{0,1:T(8,128)}, u32[]{:S(2)}, u32[]{:S(2)}) collective-permute-start(f32[128,256]{0,1:T(8,128)} %get-tuple-element.32), channel_id=1, source_target_pairs={{32,0},{40,8},{48,16},{56,24},{64,32},{72,40},{80,48},{88,56},{96,... | collective-permute-start | bytes 393224 | tf_op jit(solution)/shard_map/ppermute | solution.py:18
  423.4 15.6 %collective-permute-start.10 = (f32[128,256]{0,1:T(8,128)}, f32[128,256]{0,1:T(8,128)}, u32[]{:S(2)}, u32[]{:S(2)}) collective-permute-start(f32[128,256]{0,1:T(8,128)} %get-tuple-element.31), channel_id=1, source_target_pairs={{24,0},{32,8},{40,16},{48,24},{56,32},{64,40},{72,48},{80,56},{88,... | collective-permute-start | bytes 393224 | tf_op jit(solution)/shard_map/ppermute | solution.py:18
  426.5 19.9 %collective-permute-start.9 = (f32[128,256]{0,1:T(8,128)}, f32[128,256]{0,1:T(8,128)}, u32[]{:S(2)}, u32[]{:S(2)}) collective-permute-start(f32[128,256]{0,1:T(8,128)} %get-tuple-element.30), channel_id=1, source_target_pairs={{16,0},{24,8},{32,16},{40,24},{48,32},{56,40},{64,48},{72,56},{80,... | collective-permute-start | bytes 393224 | tf_op jit(solution)/shard_map/ppermute | solution.py:18
  430.2 16.8 %collective-permute-start.8 = (f32[128,256]{0,1:T(8,128)}, f32[128,256]{0,1:T(8,128)}, u32[]{:S(2)}, u32[]{:S(2)}) collective-permute-start(f32[128,256]{0,1:T(8,128)} %get-tuple-element.29), channel_id=1, source_target_pairs={{8,0},{16,8},{24,16},{32,24},{40,32},{48,40},{56,48},{64,56},{72,6... | collective-permute-start | bytes 393224 | tf_op jit(solution)/shard_map/ppermute | solution.py:18
  (22 other events, 209.7 us)
Sparse Core Ops, SparseCore 0:
  11.9 84.9 all-gather.1
  121.0 166.1 reduce-scatter.2
  291.5 44.4 reduce-scatter.4

commit v2 on v1

--- a/solution.py
+++ b/solution.py
@@ -127,10 +127,15 @@
         value_total = value_total + jnp.pad(value_grad, pad)
     grad_cross = join_heads(jnp.concatenate(query_grads, axis=1)).astype(jnp.bfloat16)
 
-    partial = jnp.concatenate([key_total, value_total], axis=1)
-    summed = lax.psum_scatter(partial, "ctx", scatter_dimension=0, tiled=True).astype(
-        jnp.bfloat16
-    )
+    partial = jnp.concatenate([key_total, value_total], axis=1).astype(jnp.bfloat16)
+    arrived = lax.all_to_all(
+        partial.reshape(shard_count, row_count, 2 * key_width),
+        "ctx",
+        split_axis=0,
+        concat_axis=0,
+        tiled=True,
+    )
+    summed = jnp.sum(arrived.astype(jnp.float32), axis=0).astype(jnp.bfloat16)
     per_shard = row_count // stripe
     held_place = (
         lax.dynamic_slice_in_dim(order_table, shard_index * per_shard, per_shard, axis=1)

time: 459 us -> 407 us (0.89)
  waiting for transfers between devices: 249 us -> 184 us
  starting transfers between devices: 71.5 us -> 79 us
    reduce_scatter x1 -> x0, waiting for transfers between devices: 148 us -> none  [local(): lax.psum_scatter(partial, 'ctx', scatter_dimension=0, tiled=True)]
    all_to_all x0 -> x1, waiting for transfers between devices: none -> 81 us  [local(): lax.all_to_all(partial.reshape(shard_count, row_count, 2 * key_width), 'c...]
    all_to_all x0 -> x1, starting transfers between devices: none -> 9.52 us  [local(): lax.all_to_all(partial.reshape(shard_count, row_count, 2 * key_width), 'c...]
    reduce_scatter x1, waiting for transfers between devices: 12.4 us -> 17.3 us  [local(): lax.psum_scatter(normed_part, 'head', scatter_dimension=1, tiled=True)]
  transfers between devices with their start and end apart: 19 -> 19, of which waited for: 6 -> 6; matrix products, arithmetic and copies ran while one was open for 10% -> 12% of each run, Pallas kernels for 0% -> 0%
where the time goes in v2:
time: 407 us; the launch traced here: 403 us
  waiting for transfers between devices  184 us (45%)
  starting transfers between devices  79 us (19%)
  blocking collectives  39.5 us (10%)
  local copies, waits for them, and re-layouts  33.8 us (8%)
  matrix products  30.3 us (7%)
  other arithmetic  21.7 us (5%)
  between operations  14.8 us (4%)
    all_to_all x1, waiting for transfers between devices, local(): lax.all_to_all(partial.reshape(shard_count, row_count, 2 * key_width), 'c...  81 us
    all_gather x1, waiting for transfers between devices, local(): gathered = lax.all_gather(shared, 'ctx', axis=0, tiled=True)  79.1 us
    ppermute x16, starting transfers between devices, from_behind(): lax.ppermute(value, axis, [(source, source + steps) for source in range(f...  69.4 us
    all_gather x1, blocking collectives, local(): stream_full = lax.all_gather(grad_stream, 'head', axis=1, tiled=True)  24.5 us
    reduce_scatter x1, waiting for transfers between devices, local(): lax.psum_scatter(normed_part, 'head', scatter_dimension=1, tiled=True)  17.3 us
    unnamed x71, local copies, waits for them, and re-layouts  16.8 us
    psum x1, blocking collectives, local(): lax.psum((jnp.sum(inputs * inputs, axis=1), jnp.sum(gained * inputs, axis...  15 us
    all_to_all x1, starting transfers between devices, local(): lax.all_to_all(partial.reshape(shard_count, row_count, 2 * key_width), 'c...  9.52 us
  transfers between devices with their start and end apart: 19, of which 6 were waited for; matrix products, arithmetic and copies ran while one was open for 12% of the time, Pallas kernels for 0%

profile of v2, /device:TPU:449, one launch (start us, length us, event | category | flops | bytes accessed | tf_op | source)
XLA Modules:
  0.0 402.9 jit_solution(9681057033012043514)
XLA Ops:
  17.8 79.1 %all-gather.2.cloned.1.call-done = bf16[8192,256]{1,0:T(8,128)(2,1)} async-done(((bf16[128,256]{1,0:T(8,128)(2,1)}), bf16[8192,256]{1,0:T(8,128)(2,1)}) %all-gather.2.cloned.1.call-update) | async-done | bytes 4194320 | tf_op jit(solution)/shard_map/all_gather | solution.py:92
  96.9 4.6 %copy.87 = bf16[64,128,256]{2,0,1:T(8,128)(2,1)S(1)} copy(bf16[64,128,256]{2,1,0:T(8,128)(2,1)} %bitcast.216) | data formatting | bytes 8388608 | tf_op jit(solution)/shard_map/reshape | solution.py:94
  117.3 2.7 pad_maximum_fusion
  119.9 9.5 %all-to-all-start = ((bf16[64,128,256]{2,1,0:T(8,128)(2,1)}), bf16[64,128,256]{2,1,0:T(8,128)(2,1)}, u32[]{:S(2)}, u32[]{:S(2)}) async-start(bf16[64,128,256]{2,1,0:T(8,128)(2,1)} %pad_maximum_fusion), calls=%async_computation | async-start | bytes 8388608 | tf_op jit(solution)/shard_map/all_to_all | solution.py:131
  134.8 5.2 %collective-permute-start.2 = (bf16[128,256]{1,0:T(8,128)(2,1)}, bf16[128,256]{1,0:T(8,128)(2,1)}, u32[]{:S(2)}, u32[]{:S(2)}) collective-permute-start(bf16[128,256]{1,0:T(8,128)(2,1)} %constant_dynamic-update-slice_fusion), channel_id=1, source_target_pairs={{0,48},{8,56},{16,64},{24,72},{32,80},{40,88},{48,96},{56,104},{64... | collective-permute-start | bytes 196616 | tf_op jit(solution)/shard_map/ppermute | solution.py:18
  142.0 2.4 collective-permute-start.4
  149.9 81.0 %all-to-all-done = bf16[64,128,256]{2,1,0:T(8,128)(2,1)} async-done(((bf16[64,128,256]{2,1,0:T(8,128)(2,1)}), bf16[64,128,256]{2,1,0:T(8,128)(2,1)}, u32[]{:S(2)}, u32[]{:S(2)}) %all-to-all-start) | async-done | bytes 4194336 | tf_op jit(solution)/shard_map/all_to_all | solution.py:131
  230.9 3.4 reduce_sum.163
  243.0 4.4 %collective-permute-start.5 = (bf16[128,256]{1,0:T(8,128)(2,1)}, bf16[128,256]{1,0:T(8,128)(2,1)S(1)}, u32[]{:S(2)}, u32[]{:S(2)}) collective-permute-start(bf16[128,256]{1,0:T(8,128)(2,1)} %constant_dynamic-update-slice_fusion), channel_id=1, source_target_pairs={{0,24},{8,32},{16,40},{24,48},{32,56},{40,64},{48,72},{56,80},{64,... | collective-permute-start | bytes 196616 | tf_op jit(solution)/shard_map/ppermute | solution.py:18
  248.2 3.3 collective-permute-start.6
  252.4 3.2 collective-permute-start.7
  265.8 17.3 %reduce-scatter.2.cloned.1.call-done = f32[128,384]{1,0:T(8,128)} async-done(((f32[128,3072]{1,0:T(8,128)}), f32[128,384]{1,0:T(8,128)}) %reduce-scatter.2.cloned.1.call-update) | async-done | bytes 196624 | tf_op jit(solution)/shard_map/reduce_scatter | solution.py:159
  284.1 15.0 %all-reduce.7 = (f32[128]{0:T(128)S(1)}, f32[128]{0:T(128)S(1)}) all-reduce(f32[128]{0:T(128)S(1)} %get-tuple-element.26, f32[128]{0:T(128)S(1)} %get-tuple-element.25), channel_id=1, replica_groups=mesh['ctx'=64,'head'=8] {'head'}, use_global_device_ids=true, to_apply=%region_20.21 | all-reduce | flops 256 | bytes 2048 | tf_op jit(solution)/shard_map/psum | solution.py:166
  300.8 24.5 %all_gather.7 = bf16[128,3072]{1,0:T(8,128)(2,1)S(1)} all-gather(bf16[128,384]{1,0:T(8,128)(2,1)S(1)} %fusion.68), channel_id=1, replica_groups=mesh['ctx'=64,'head'=8] {'head'}, dimensions={1}, use_global_device_ids=true | all-gather | bytes 884736 | tf_op jit(solution)/shard_map/all_gather | solution.py:176
  331.2 4.1 %collective-permute-start.15 = (f32[128,256]{0,1:T(8,128)}, f32[128,256]{0,1:T(8,128)}, u32[]{:S(2)}, u32[]{:S(2)}) collective-permute-start(f32[128,256]{0,1:T(8,128)} %get-tuple-element.35), channel_id=1, source_target_pairs={{64,0},{72,8},{80,16},{88,24},{96,32},{104,40},{112,48},{120,56},{... | collective-permute-start | bytes 393224 | tf_op jit(solution)/shard_map/ppermute | solution.py:18
  335.3 17.5 %collective-permute-start.14 = (f32[128,256]{0,1:T(8,128)}, f32[128,256]{0,1:T(8,128)}, u32[]{:S(2)}, u32[]{:S(2)}) collective-permute-start(f32[128,256]{0,1:T(8,128)} %get-tuple-element.36), channel_id=1, source_target_pairs={{56,0},{64,8},{72,16},{80,24},{88,32},{96,40},{104,48},{112,56},{1... | collective-permute-start | bytes 393224 | tf_op jit(solution)/shard_map/ppermute | solution.py:18
  352.7 4.8 %collective-permute-start.13 = (f32[128,256]{0,1:T(8,128)}, f32[128,256]{0,1:T(8,128)}, u32[]{:S(2)}, u32[]{:S(2)}) collective-permute-start(f32[128,256]{0,1:T(8,128)} %get-tuple-element.34), channel_id=1, source_target_pairs={{48,0},{56,8},{64,16},{72,24},{80,32},{88,40},{96,48},{104,56},{11... | collective-permute-start | bytes 393224 | tf_op jit(solution)/shard_map/ppermute | solution.py:18
  362.8 2.1 collective-permute-start.12
  364.9 4.3 %collective-permute-start.11 = (f32[128,256]{0,1:T(8,128)}, f32[128,256]{0,1:T(8,128)}, u32[]{:S(2)}, u32[]{:S(2)}) collective-permute-start(f32[128,256]{0,1:T(8,128)} %get-tuple-element.32), channel_id=1, source_target_pairs={{32,0},{40,8},{48,16},{56,24},{64,32},{72,40},{80,48},{88,56},{96,... | collective-permute-start | bytes 393224 | tf_op jit(solution)/shard_map/ppermute | solution.py:18
  369.2 5.0 %collective-permute-start.10 = (f32[128,256]{0,1:T(8,128)}, f32[128,256]{0,1:T(8,128)}, u32[]{:S(2)}, u32[]{:S(2)}) collective-permute-start(f32[128,256]{0,1:T(8,128)} %get-tuple-element.31), channel_id=1, source_target_pairs={{24,0},{32,8},{40,16},{48,24},{56,32},{64,40},{72,48},{80,56},{88,... | collective-permute-start | bytes 393224 | tf_op jit(solution)/shard_map/ppermute | solution.py:18
  374.3 3.4 collective-permute-start.9
  377.7 5.2 %collective-permute-start.8 = (f32[128,256]{0,1:T(8,128)}, f32[128,256]{0,1:T(8,128)}, u32[]{:S(2)}, u32[]{:S(2)}) collective-permute-start(f32[128,256]{0,1:T(8,128)} %get-tuple-element.29), channel_id=1, source_target_pairs={{8,0},{16,8},{24,16},{32,24},{40,32},{48,40},{56,48},{64,56},{72,6... | collective-permute-start | bytes 393224 | tf_op jit(solution)/shard_map/ppermute | solution.py:18
  382.9 2.3 fusion.41
  388.0 5.1 %collective-permute-done.9 = f32[128,256]{0,1:T(8,128)} collective-permute-done((f32[128,256]{0,1:T(8,128)}, f32[128,256]{0,1:T(8,128)}, u32[]{:S(2)}, u32[]{:S(2)}) %collective-permute-start.9) | collective-permute-done | bytes 131104 | tf_op jit(solution)/shard_map/ppermute | solution.py:18
  (180 shorter events, 78.8 us)
Async XLA Ops:
  7.2 318.2 %copy-start = (bf16[384,3072]{1,0:T(8,128)(2,1)S(1)}, bf16[384,3072]{1,0:T(8,128)(2,1)}, u32[]{:S(2)}) copy-start(bf16[384,3072]{1,0:T(8,128)(2,1)} %param.26) | copy-start | bytes 7077892
  7.2 89.8 %all-gather.2.cloned.1.call-start = ((), (), s32[]{:S(2)}) async-start(), calls=%async_computation.2 | async-start | bytes 4259840 | tf_op jit(solution)/shard_map/all_gather | solution.py:92
  12.1 95.6 %copy-start.19 = (bf16[128,3,128]{2,0,1:T(8,128)(2,1)}, bf16[128,3,128]{2,0,1:T(8,128)(2,1)S(1)}, u32[]{:S(2)}) copy-start(bf16[128,3,128]{2,0,1:T(8,128)(2,1)S(1)} %copy.89) | copy-start | bytes 294916
  14.1 95.9 %copy-start.10 = (bf16[128,3,128]{2,0,1:T(8,128)(2,1)}, bf16[128,3,128]{2,0,1:T(8,128)(2,1)S(1)}, u32[]{:S(2)}) copy-start(bf16[128,3,128]{2,0,1:T(8,128)(2,1)S(1)} %copy.91) | copy-start | bytes 294916
  119.9 111.0 %all-to-all-start = ((bf16[64,128,256]{2,1,0:T(8,128)(2,1)}), bf16[64,128,256]{2,1,0:T(8,128)(2,1)}, u32[]{:S(2)}, u32[]{:S(2)}) async-start(bf16[64,128,256]{2,1,0:T(8,128)(2,1)} %pad_maximum_fusion), calls=%async_computation | async-start | bytes 8388608 | tf_op jit(solution)/shard_map/all_to_all | solution.py:131
  129.5 153.6 %reduce-scatter.2.cloned.1.call-start = ((), (), s32[]{:S(2)}) async-start(), calls=%async_computation.3 | async-start | bytes 1769472 | tf_op jit(solution)/shard_map/reduce_scatter | solution.py:159
  132.3 110.7 %collective-permute-start = (bf16[128,256]{1,0:T(8,128)(2,1)}, bf16[128,256]{1,0:T(8,128)(2,1)}, u32[]{:S(2)}, u32[]{:S(2)}) collective-permute-start(bf16[128,256]{1,0:T(8,128)(2,1)} %constant_dynamic-update-slice_fusion), channel_id=1, source_target_pairs={{0,64},{8,72},{16,80},{24,88},{32,96},{40,104},{48,112},{56,120},{... | collective-permute-start | bytes 196616 | tf_op jit(solution)/shard_map/ppermute | solution.py:18
  133.5 114.7 %collective-permute-start.1 = (bf16[128,256]{1,0:T(8,128)(2,1)}, bf16[128,256]{1,0:T(8,128)(2,1)}, u32[]{:S(2)}, u32[]{:S(2)}) collective-permute-start(bf16[128,256]{1,0:T(8,128)(2,1)} %constant_dynamic-update-slice_fusion), channel_id=1, source_target_pairs={{0,56},{8,64},{16,72},{24,80},{32,88},{40,96},{48,104},{56,112},{6... | collective-permute-start | bytes 196616 | tf_op jit(solution)/shard_map/ppermute | solution.py:18
  134.8 117.5 %collective-permute-start.2 = (bf16[128,256]{1,0:T(8,128)(2,1)}, bf16[128,256]{1,0:T(8,128)(2,1)}, u32[]{:S(2)}, u32[]{:S(2)}) collective-permute-start(bf16[128,256]{1,0:T(8,128)(2,1)} %constant_dynamic-update-slice_fusion), channel_id=1, source_target_pairs={{0,48},{8,56},{16,64},{24,72},{32,80},{40,88},{48,96},{56,104},{64... | collective-permute-start | bytes 196616 | tf_op jit(solution)/shard_map/ppermute | solution.py:18
  140.1 116.4 %collective-permute-start.3 = (bf16[128,256]{1,0:T(8,128)(2,1)}, bf16[128,256]{1,0:T(8,128)(2,1)}, u32[]{:S(2)}, u32[]{:S(2)}) collective-permute-start(bf16[128,256]{1,0:T(8,128)(2,1)} %constant_dynamic-update-slice_fusion), channel_id=1, source_target_pairs={{0,40},{8,48},{16,56},{24,64},{32,72},{40,80},{48,88},{56,96},{64,... | collective-permute-start | bytes 196616 | tf_op jit(solution)/shard_map/ppermute | solution.py:18
  142.0 115.4 %collective-permute-start.4 = (bf16[128,256]{1,0:T(8,128)(2,1)}, bf16[128,256]{1,0:T(8,128)(2,1)}, u32[]{:S(2)}, u32[]{:S(2)}) collective-permute-start(bf16[128,256]{1,0:T(8,128)(2,1)} %constant_dynamic-update-slice_fusion), channel_id=1, source_target_pairs={{0,32},{8,40},{16,48},{24,56},{32,64},{40,72},{48,80},{56,88},{64,... | collective-permute-start | bytes 196616 | tf_op jit(solution)/shard_map/ppermute | solution.py:18
  243.0 15.3 %collective-permute-start.5 = (bf16[128,256]{1,0:T(8,128)(2,1)}, bf16[128,256]{1,0:T(8,128)(2,1)S(1)}, u32[]{:S(2)}, u32[]{:S(2)}) collective-permute-start(bf16[128,256]{1,0:T(8,128)(2,1)} %constant_dynamic-update-slice_fusion), channel_id=1, source_target_pairs={{0,24},{8,32},{16,40},{24,48},{32,56},{40,64},{48,72},{56,80},{64,... | collective-permute-start | bytes 196616 | tf_op jit(solution)/shard_map/ppermute | solution.py:18
  248.2 10.0 %collective-permute-start.6 = (bf16[128,256]{1,0:T(8,128)(2,1)}, bf16[128,256]{1,0:T(8,128)(2,1)S(1)}, u32[]{:S(2)}, u32[]{:S(2)}) collective-permute-start(bf16[128,256]{1,0:T(8,128)(2,1)} %constant_dynamic-update-slice_fusion), channel_id=1, source_target_pairs={{0,16},{8,24},{16,32},{24,40},{32,48},{40,56},{48,64},{56,72},{64,... | collective-permute-start | bytes 196616 | tf_op jit(solution)/shard_map/ppermute | solution.py:18
  252.4 5.9 %collective-permute-start.7 = (bf16[128,256]{1,0:T(8,128)(2,1)}, bf16[128,256]{1,0:T(8,128)(2,1)S(1)}, u32[]{:S(2)}, u32[]{:S(2)}) collective-permute-start(bf16[128,256]{1,0:T(8,128)(2,1)} %constant_dynamic-update-slice_fusion), channel_id=1, source_target_pairs={{0,8},{8,16},{16,24},{24,32},{32,40},{40,48},{48,56},{56,64},{64,7... | collective-permute-start | bytes 196616 | tf_op jit(solution)/shard_map/ppermute | solution.py:18
  264.6 34.5 %copy-start.21 = (bf16[128,384]{1,0:T(8,128)(2,1)S(1)}, bf16[128,384]{1,0:T(8,128)(2,1)}, u32[]{:S(2)}) copy-start(bf16[128,384]{1,0:T(8,128)(2,1)} %param.25) | copy-start | bytes 294916
  329.8 29.0 %copy-start.24 = (bf16[3,32,128]{2,1,0:T(8,128)(2,1)S(1)}, bf16[3,32,128]{2,1,0:T(8,128)(2,1)}, u32[]{:S(2)}) copy-start(bf16[3,32,128]{2,1,0:T(8,128)(2,1)} %fusion.49) | copy-start | bytes 73732
  331.2 38.0 %collective-permute-start.15 = (f32[128,256]{0,1:T(8,128)}, f32[128,256]{0,1:T(8,128)}, u32[]{:S(2)}, u32[]{:S(2)}) collective-permute-start(f32[128,256]{0,1:T(8,128)} %get-tuple-element.35), channel_id=1, source_target_pairs={{64,0},{72,8},{80,16},{88,24},{96,32},{104,40},{112,48},{120,56},{... | collective-permute-start | bytes 393224 | tf_op jit(solution)/shard_map/ppermute | solution.py:18
  335.3 39.0 %collective-permute-start.14 = (f32[128,256]{0,1:T(8,128)}, f32[128,256]{0,1:T(8,128)}, u32[]{:S(2)}, u32[]{:S(2)}) collective-permute-start(f32[128,256]{0,1:T(8,128)} %get-tuple-element.36), channel_id=1, source_target_pairs={{56,0},{64,8},{72,16},{80,24},{88,32},{96,40},{104,48},{112,56},{1... | collective-permute-start | bytes 393224 | tf_op jit(solution)/shard_map/ppermute | solution.py:18
  352.7 24.9 %collective-permute-start.13 = (f32[128,256]{0,1:T(8,128)}, f32[128,256]{0,1:T(8,128)}, u32[]{:S(2)}, u32[]{:S(2)}) collective-permute-start(f32[128,256]{0,1:T(8,128)} %get-tuple-element.34), channel_id=1, source_target_pairs={{48,0},{56,8},{64,16},{72,24},{80,32},{88,40},{96,48},{104,56},{11... | collective-permute-start | bytes 393224 | tf_op jit(solution)/shard_map/ppermute | solution.py:18
  362.8 24.0 %collective-permute-start.12 = (f32[128,256]{0,1:T(8,128)}, f32[128,256]{0,1:T(8,128)}, u32[]{:S(2)}, u32[]{:S(2)}) collective-permute-start(f32[128,256]{0,1:T(8,128)} %get-tuple-element.33), channel_id=1, source_target_pairs={{40,0},{48,8},{56,16},{64,24},{72,32},{80,40},{88,48},{96,56},{104... | collective-permute-start | bytes 393224 | tf_op jit(solution)/shard_map/ppermute | solution.py:18
  364.9 21.9 %collective-permute-start.11 = (f32[128,256]{0,1:T(8,128)}, f32[128,256]{0,1:T(8,128)}, u32[]{:S(2)}, u32[]{:S(2)}) collective-permute-start(f32[128,256]{0,1:T(8,128)} %get-tuple-element.32), channel_id=1, source_target_pairs={{32,0},{40,8},{48,16},{56,24},{64,32},{72,40},{80,48},{88,56},{96,... | collective-permute-start | bytes 393224 | tf_op jit(solution)/shard_map/ppermute | solution.py:18
  369.2 18.8 %collective-permute-start.10 = (f32[128,256]{0,1:T(8,128)}, f32[128,256]{0,1:T(8,128)}, u32[]{:S(2)}, u32[]{:S(2)}) collective-permute-start(f32[128,256]{0,1:T(8,128)} %get-tuple-element.31), channel_id=1, source_target_pairs={{24,0},{32,8},{40,16},{48,24},{56,32},{64,40},{72,48},{80,56},{88,... | collective-permute-start | bytes 393224 | tf_op jit(solution)/shard_map/ppermute | solution.py:18
  374.3 18.8 %collective-permute-start.9 = (f32[128,256]{0,1:T(8,128)}, f32[128,256]{0,1:T(8,128)}, u32[]{:S(2)}, u32[]{:S(2)}) collective-permute-start(f32[128,256]{0,1:T(8,128)} %get-tuple-element.30), channel_id=1, source_target_pairs={{16,0},{24,8},{32,16},{40,24},{48,32},{56,40},{64,48},{72,56},{80,... | collective-permute-start | bytes 393224 | tf_op jit(solution)/shard_map/ppermute | solution.py:18
  377.7 15.6 %collective-permute-start.8 = (f32[128,256]{0,1:T(8,128)}, f32[128,256]{0,1:T(8,128)}, u32[]{:S(2)}, u32[]{:S(2)}) collective-permute-start(f32[128,256]{0,1:T(8,128)} %get-tuple-element.29), channel_id=1, source_target_pairs={{8,0},{16,8},{24,16},{32,24},{40,32},{48,40},{56,48},{64,56},{72,6... | collective-permute-start | bytes 393224 | tf_op jit(solution)/shard_map/ppermute | solution.py:18
  (22 other events, 205.1 us)
Sparse Core Ops, SparseCore 0:
  11.9 84.9 all-gather.1
  238.6 44.3 reduce-scatter.1

commit v3 on v1

--- a/solution.py
+++ b/solution.py
@@ -10,6 +10,8 @@
 WINDOW = 1024
 DOCS = 8
 QUERY_BLOCKS = 4
+CTX = ("z", "yh", "core")
+HEAD = ("yl", "x")
 
 
 def from_behind(value, axis, steps):
@@ -83,13 +85,15 @@
     row_count = queries_cross.shape[0]
     total_rows = stripe_order.shape[0]
     key_width = keys_shared.shape[1]
-    shard_index = lax.axis_index("ctx")
-    shard_count = lax.axis_size("ctx")
+    shard_index = lax.axis_index(CTX)
+    shard_count = lax.axis_size(CTX)
     stripe = total_rows // row_count
     first_row = shard_index * row_count
 
     shared = jnp.concatenate([keys_shared, values_shared], axis=1)
-    gathered = lax.all_gather(shared, "ctx", axis=0, tiled=True)
+    gathered = shared
+    for axis in reversed(CTX):
+        gathered = lax.all_gather(gathered, axis, axis=0, tiled=True)
     ordered = (
         gathered.reshape(shard_count, row_count, 2 * key_width)
         .transpose(1, 0, 2)
@@ -127,10 +131,12 @@
         value_total = value_total + jnp.pad(value_grad, pad)
     grad_cross = join_heads(jnp.concatenate(query_grads, axis=1)).astype(jnp.bfloat16)
 
-    partial = jnp.concatenate([key_total, value_total], axis=1)
-    summed = lax.psum_scatter(partial, "ctx", scatter_dimension=0, tiled=True).astype(
-        jnp.bfloat16
-    )
+    partial = jnp.concatenate([key_total, value_total], axis=1).astype(jnp.bfloat16)
+    sizes = tuple(lax.axis_size(axis) for axis in CTX)
+    summed = partial.reshape(sizes + (row_count, 2 * key_width))
+    for place in reversed(range(len(CTX))):
+        arrived = lax.all_to_all(summed, CTX[place], split_axis=place, concat_axis=place, tiled=True)
+        summed = jnp.sum(arrived.astype(jnp.float32), axis=place).astype(jnp.bfloat16)
     per_shard = row_count // stripe
     held_place = (
         lax.dynamic_slice_in_dim(order_table, shard_index * per_shard, per_shard, axis=1)
@@ -151,15 +157,17 @@
     normed_part = normed_part + lax.dot_general(
         shared_grad[:, key_width:], weight_value, contract, preferred_element_type=jnp.float32
     )
-    normed_cols = lax.psum_scatter(normed_part, "head", scatter_dimension=1, tiled=True)
+    normed_cols = normed_part
+    for axis in HEAD:
+        normed_cols = lax.psum_scatter(normed_cols, axis, scatter_dimension=1, tiled=True)
     column_count = norm_input.shape[1]
     gain_cols = lax.dynamic_slice_in_dim(
-        norm_gain, lax.axis_index("head") * column_count, column_count
+        norm_gain, lax.axis_index(HEAD) * column_count, column_count
     )
     inputs = norm_input.astype(jnp.float32)
     gained = normed_cols * gain_cols[None, :]
     square_sum, inner_sum = lax.psum(
-        (jnp.sum(inputs * inputs, axis=1), jnp.sum(gained * inputs, axis=1)), "head"
+        (jnp.sum(inputs * inputs, axis=1), jnp.sum(gained * inputs, axis=1)), HEAD
     )
     scaling = lax.rsqrt(square_sum / D + 1e-06)[:, None]
     stream = (
@@ -168,14 +176,16 @@
         + upstream.astype(jnp.float32)
     )
     grad_stream = stream.astype(jnp.bfloat16)
-    stream_full = lax.all_gather(grad_stream, "head", axis=1, tiled=True)
+    stream_full = grad_stream
+    for axis in reversed(HEAD):
+        stream_full = lax.all_gather(stream_full, axis, axis=1, tiled=True)
     head_grads = lax.dot_general(
         stream_full, weight_out, contract, preferred_element_type=jnp.float32
     ).astype(jnp.bfloat16)
 
     reach_count = WINDOW // row_count
     own_window = jnp.concatenate([keys_window, values_window], axis=1)
-    pieces = [from_behind(own_window, "ctx", distance) for distance in range(reach_count, 0, -1)]
+    pieces = [from_behind(own_window, CTX, distance) for distance in range(reach_count, 0, -1)]
     window_all = jnp.concatenate(pieces + [own_window], axis=0)
     own_place = first_row + jnp.arange(row_count, dtype=jnp.int32)
     window_place = first_row - WINDOW + jnp.arange(WINDOW + row_count, dtype=jnp.int32)
@@ -200,7 +210,7 @@
     for distance in range(1, reach_count + 1):
         lower_row = (reach_count - distance) * row_count
         collected = collected + from_behind(
-            window_part[lower_row : lower_row + row_count], "ctx", -distance
+            window_part[lower_row : lower_row + row_count], CTX, -distance
         )
     grad_keys = collected[:, :key_width].astype(jnp.bfloat16)
     grad_values = collected[:, key_width:].astype(jnp.bfloat16)
@@ -208,28 +218,28 @@
 
 
 def solution(mesh):
+    ctx_parts = (mesh.shape["ctx"] // 8, 4, 2)
+    head_parts = (2, mesh.shape["head"] // 2)
+    parts = jax.sharding.Mesh(
+        mesh.devices.reshape(ctx_parts + head_parts), CTX + HEAD
+    )
+    rows = P(CTX, HEAD)
     in_specs = (
-        P("ctx", "head"),
-        P("ctx", "head"),
-        P("ctx", "head"),
-        P("ctx", "head"),
+        rows,
+        rows,
+        rows,
+        rows,
         P(),
         P(),
-        P("ctx", "head"),
+        rows,
         P(),
-        P(None, "head"),
-        P(None, "head"),
-        P("ctx", "head"),
-        P("head", None),
-        P("ctx", "head"),
-        P("ctx", "head"),
-        P("ctx", "head"),
-    )
-    out_specs = (
-        P("ctx", "head"),
-        P("ctx", "head"),
-        P("ctx", "head"),
-        P("ctx", "head"),
-        P("ctx", "head"),
-    )
-    return jax.shard_map(local, mesh=mesh, in_specs=in_specs, out_specs=out_specs, check_vma=False)
+        P(None, HEAD),
+        P(None, HEAD),
+        rows,
+        P(HEAD, None),
+        rows,
+        rows,
+        rows,
+    )
+    out_specs = (rows, rows, rows, rows, rows)
+    return jax.shard_map(local, mesh=parts, in_specs=in_specs, out_specs=out_specs, check_vma=False)

time: 459 us -> 390 us (0.85)
  waiting for transfers between devices: 249 us -> 98 us
  blocking collectives: 39 us -> 115 us
  other arithmetic: 19.5 us -> 24.2 us
    reduce_scatter x2, waiting for transfers between devices: 160 us -> 30.9 us  [local(): lax.psum_scatter(normed_cols, axis, scatter_dimension=1, tiled=True)]
    all_to_all x0 -> x2, blocking collectives: none -> 63.8 us  [local(): lax.all_to_all(summed, CTX[place], split_axis=place, concat_axis=place, t...]
    all_gather x1, waiting for transfers between devices: 79 us -> 49.6 us  [local(): gathered = lax.all_gather(gathered, axis, axis=0, tiled=True)]
    all_gather x1 -> x4, blocking collectives: 24.2 us -> 37 us  [the longest x2 19.6 us: local(): gathered = lax.all_gather(gathered, axis, axis=0, tiled=True)]
    reduce_sum x0 -> x3, other arithmetic: none -> 9.74 us  [local(): jnp.sum(arrived.astype(jnp.float32), axis=place).astype(jnp.bfloat16)]
    ppermute x16, starting transfers between devices: 71.3 us -> 61.7 us  [from_behind(): lax.ppermute(value, axis, [(source, source + steps) for source in range(f...]
    all_to_all x0 -> x1, waiting for transfers between devices: none -> 6.77 us  [local(): lax.all_to_all(summed, CTX[place], split_axis=place, concat_axis=place, t...]
    all_to_all x0 -> x1, starting transfers between devices: none -> 5.7 us  [local(): lax.all_to_all(summed, CTX[place], split_axis=place, concat_axis=place, t...]
  transfers between devices with their start and end apart: 19 -> 20, of which waited for: 6 -> 7; matrix products, arithmetic and copies ran while one was open for 10% -> 11% of each run, Pallas kernels for 0% -> 0%
where the time goes in v3:
time: 390 us; the launch traced here: 387 us
  blocking collectives  115 us (29%)
  waiting for transfers between devices  98 us (25%)
  starting transfers between devices  67.5 us (17%)
  local copies, waits for them, and re-layouts  35.1 us (9%)
  matrix products  33.2 us (9%)
  other arithmetic  24.2 us (6%)
  between operations  14.5 us (4%)
    all_to_all x2, blocking collectives, local(): lax.all_to_all(summed, CTX[place], split_axis=place, concat_axis=place, t...  63.8 us
    ppermute x16, starting transfers between devices, from_behind(): lax.ppermute(value, axis, [(source, source + steps) for source in range(f...  61.7 us
    all_gather x1, waiting for transfers between devices, local(): gathered = lax.all_gather(gathered, axis, axis=0, tiled=True)  49.6 us
    reduce_scatter x2, waiting for transfers between devices, local(): lax.psum_scatter(normed_cols, axis, scatter_dimension=1, tiled=True)  30.9 us
    all_gather x2, blocking collectives, local(): gathered = lax.all_gather(gathered, axis, axis=0, tiled=True)  19.6 us
    unnamed x69, local copies, waits for them, and re-layouts  19.5 us
    all_gather x2, blocking collectives, local(): stream_full = lax.all_gather(stream_full, axis, axis=1, tiled=True)  17.4 us
    psum x1, blocking collectives, local(): lax.psum((jnp.sum(inputs * inputs, axis=1), jnp.sum(gained * inputs, axis...  14 us
  transfers between devices with their start and end apart: 20, of which 7 were waited for; matrix products, arithmetic and copies ran while one was open for 11% of the time, Pallas kernels for 0%

profile of v3, /device:TPU:449, one launch (start us, length us, event | category | flops | bytes accessed | tf_op | source)
XLA Modules:
  0.0 387.3 jit_solution(2300335374762938146)
XLA Ops:
  10.4 17.3 %all_gather.16 = bf16[1024,256]{1,0:T(8,128)(2,1)} all-gather(bf16[256,256]{1,0:T(8,128)(2,1)S(1)} %all_gather.15), channel_id=1, replica_groups=mesh['z'=8,'yh'=4,'core'=2,'yl'=2,'x'=4] {'yh'}, dimensions={0}, use_global_device_ids=true | all-gather | bytes 655360 | tf_op jit(solution)/shard_map/all_gather | solution.py:96
  32.9 49.6 %all-gather.2.cloned.1.call-done = bf16[8192,256]{1,0:T(8,128)(2,1)} async-done(((bf16[1024,256]{1,0:T(8,128)(2,1)}), bf16[8192,256]{1,0:T(8,128)(2,1)}) %all-gather.2.cloned.1.call-update) | async-done | bytes 4194320 | tf_op jit(solution)/shard_map/all_gather | solution.py:96
  82.5 4.6 %copy.144 = bf16[64,128,256]{2,0,1:T(8,128)(2,1)S(1)} copy(bf16[64,128,256]{2,1,0:T(8,128)(2,1)} %bitcast.216) | data formatting | bytes 8388608 | tf_op jit(solution)/shard_map/reshape | solution.py:98
  104.1 8.4 %all_to_all.15 = bf16[8,4,2,128,256]{4,3,1,0,2:T(8,128)(2,1)} all-to-all(bf16[8,4,2,128,256]{4,3,1,0,2:T(8,128)(2,1)S(1)} %copy.180), channel_id=1, replica_groups=mesh['z'=8,'yh'=4,'core'=2,'yl'=2,'x'=4] {'core'}, dimensions={2} | all-to-all | bytes 8388608 | tf_op jit(solution)/shard_map/all_to_all | solution.py:138
  112.6 5.1 %reduce_sum.187 = bf16[8,4,128,256]{3,2,1,0:T(8,128)(2,1)} reduce(bf16[8,4,2,128,256]{4,3,1,0,2:T(8,128)(2,1)} %all_to_all.15, bf16[]{:T(256)} %constant.22.clone.1), dimensions={2}, to_apply=%region_17.18 | reduce | flops 1048576 | bytes 6291458 | tf_op jit(solution)/shard_map/reduce_sum | solution.py:139
  119.4 55.4 %all_to_all.16 = bf16[8,4,128,256]{3,2,0,1:T(8,128)(2,1)} all-to-all(bf16[8,4,128,256]{3,2,0,1:T(8,128)(2,1)S(1)} %copy.155), channel_id=1, replica_groups=mesh['z'=8,'yh'=4,'core'=2,'yl'=2,'x'=4] {'yh'}, dimensions={1} | all-to-all | bytes 4194304 | tf_op jit(solution)/shard_map/all_to_all | solution.py:138
  174.8 2.9 reduce_sum.188
  177.7 5.7 %all-to-all-start.2 = ((bf16[8,128,256]{2,1,0:T(8,128)(2,1)}), bf16[8,128,256]{2,1,0:T(8,128)(2,1)}, u32[]{:S(2)}, u32[]{:S(2)}) async-start(bf16[8,128,256]{2,1,0:T(8,128)(2,1)} %reduce_sum.188), calls=%async_computation.2 | async-start | bytes 1048576 | tf_op jit(solution)/shard_map/all_to_all | solution.py:138
  185.7 6.8 %all-to-all-done.2 = bf16[8,128,256]{2,1,0:T(8,128)(2,1)} async-done(((bf16[8,128,256]{2,1,0:T(8,128)(2,1)}), bf16[8,128,256]{2,1,0:T(8,128)(2,1)}, u32[]{:S(2)}, u32[]{:S(2)}) %all-to-all-start.2) | async-done | bytes 524320 | tf_op jit(solution)/shard_map/all_to_all | solution.py:138
  203.8 4.1 %collective-permute-start.2 = (bf16[128,256]{1,0:T(8,128)(2,1)}, bf16[128,256]{1,0:T(8,128)(2,1)}, u32[]{:S(2)}, u32[]{:S(2)}) collective-permute-start(bf16[128,256]{1,0:T(8,128)(2,1)} %constant_dynamic-update-slice_fusion), channel_id=1, source_target_pairs={{0,48},{8,56},{16,64},{24,72},{32,80},{40,88},{48,96},{56,104},{64... | collective-permute-start | bytes 196616 | tf_op jit(solution)/shard_map/ppermute | solution.py:20
  207.9 4.7 %collective-permute-start.3 = (bf16[128,256]{1,0:T(8,128)(2,1)}, bf16[128,256]{1,0:T(8,128)(2,1)}, u32[]{:S(2)}, u32[]{:S(2)}) collective-permute-start(bf16[128,256]{1,0:T(8,128)(2,1)} %constant_dynamic-update-slice_fusion), channel_id=1, source_target_pairs={{0,40},{8,48},{16,56},{24,64},{32,72},{40,80},{48,88},{56,96},{64,... | collective-permute-start | bytes 196616 | tf_op jit(solution)/shard_map/ppermute | solution.py:20
  227.5 2.8 collective-permute-start.7
  248.5 30.9 %reduce-scatter.5.cloned.1.call-done = f32[128,384]{1,0:T(8,128)} async-done(((f32[128,1536]{1,0:T(8,128)}), f32[128,384]{1,0:T(8,128)}) %reduce-scatter.5.cloned.1.call-update) | async-done | bytes 196624 | tf_op jit(solution)/shard_map/reduce_scatter | solution.py:162
  280.4 14.0 %all-reduce.7 = (f32[128]{0:T(128)S(1)}, f32[128]{0:T(128)S(1)}) all-reduce(f32[128]{0:T(128)S(1)} %get-tuple-element.36, f32[128]{0:T(128)S(1)} %get-tuple-element.35), channel_id=1, replica_groups=mesh['z'=8,'yh'=4,'core'=2,'yl'=2,'x'=4] {'yl','x'}, use_global_device_ids=true, to_apply=%region_23.24 | all-reduce | flops 256 | bytes 2048 | tf_op jit(solution)/shard_map/psum | solution.py:169
  295.5 9.8 %all_gather.18 = bf16[128,1536]{1,0:T(8,128)(2,1)S(1)} all-gather(bf16[128,384]{1,0:T(8,128)(2,1)S(1)} %fusion.68), channel_id=1, replica_groups=mesh['z'=8,'yh'=4,'core'=2,'yl'=2,'x'=4] {'x'}, dimensions={1}, use_global_device_ids=true | all-gather | bytes 491520 | tf_op jit(solution)/shard_map/all_gather | solution.py:181
  305.3 7.6 %all_gather.19 = bf16[128,3072]{1,0:T(8,128)(2,1)S(1)} all-gather(bf16[128,1536]{1,0:T(8,128)(2,1)S(1)} %all_gather.18), channel_id=1, replica_groups=mesh['z'=8,'yh'=4,'core'=2,'yl'=2,'x'=4] {'yl'}, dimensions={1}, use_global_device_ids=true | all-gather | bytes 1179648 | tf_op jit(solution)/shard_map/all_gather | solution.py:181
  319.3 3.6 collective-permute-start.15
  322.9 14.0 %collective-permute-start.14 = (f32[128,256]{0,1:T(8,128)}, f32[128,256]{0,1:T(8,128)}, u32[]{:S(2)}, u32[]{:S(2)}) collective-permute-start(f32[128,256]{0,1:T(8,128)} %get-tuple-element.46), channel_id=1, source_target_pairs={{56,0},{64,8},{72,16},{80,24},{88,32},{96,40},{104,48},{112,56},{1... | collective-permute-start | bytes 393224 | tf_op jit(solution)/shard_map/ppermute | solution.py:20
  336.9 4.4 %collective-permute-start.13 = (f32[128,256]{0,1:T(8,128)}, f32[128,256]{0,1:T(8,128)}, u32[]{:S(2)}, u32[]{:S(2)}) collective-permute-start(f32[128,256]{0,1:T(8,128)} %get-tuple-element.44), channel_id=1, source_target_pairs={{48,0},{56,8},{64,16},{72,24},{80,32},{88,40},{96,48},{104,56},{11... | collective-permute-start | bytes 393224 | tf_op jit(solution)/shard_map/ppermute | solution.py:20
  348.8 4.8 %collective-permute-start.11 = (f32[128,256]{0,1:T(8,128)}, f32[128,256]{0,1:T(8,128)}, u32[]{:S(2)}, u32[]{:S(2)}) collective-permute-start(f32[128,256]{0,1:T(8,128)} %get-tuple-element.42), channel_id=1, source_target_pairs={{32,0},{40,8},{48,16},{56,24},{64,32},{72,40},{80,48},{88,56},{96,... | collective-permute-start | bytes 393224 | tf_op jit(solution)/shard_map/ppermute | solution.py:20
  353.7 3.7 collective-permute-start.10
  357.4 3.0 collective-permute-start.9
  360.5 5.2 %collective-permute-start.8 = (f32[128,256]{0,1:T(8,128)}, f32[128,256]{0,1:T(8,128)}, u32[]{:S(2)}, u32[]{:S(2)}) collective-permute-start(f32[128,256]{0,1:T(8,128)} %get-tuple-element.39), channel_id=1, source_target_pairs={{8,0},{16,8},{24,16},{32,24},{40,32},{48,40},{56,48},{64,56},{72,6... | collective-permute-start | bytes 393224 | tf_op jit(solution)/shard_map/ppermute | solution.py:20
  372.0 5.8 %collective-permute-done.9 = f32[128,256]{0,1:T(8,128)} collective-permute-done((f32[128,256]{0,1:T(8,128)}, f32[128,256]{0,1:T(8,128)}, u32[]{:S(2)}, u32[]{:S(2)}) %collective-permute-start.9) | collective-permute-done | bytes 131104 | tf_op jit(solution)/shard_map/ppermute | solution.py:20
  (190 shorter events, 98.5 us)
Async XLA Ops:
  7.2 305.7 %copy-start = (bf16[384,3072]{1,0:T(8,128)(2,1)S(1)}, bf16[384,3072]{1,0:T(8,128)(2,1)}, u32[]{:S(2)}) copy-start(bf16[384,3072]{1,0:T(8,128)(2,1)} %param.26) | copy-start | bytes 7077892
  7.2 75.3 %all-gather.2.cloned.1.call-start = ((), (), s32[]{:S(2)}) async-start(), calls=%async_computation.5 | async-start | bytes 4718592 | tf_op jit(solution)/shard_map/all_gather | solution.py:96
  31.1 62.2 %copy-start.17 = (bf16[128,3,128]{2,0,1:T(8,128)(2,1)}, bf16[128,3,128]{2,0,1:T(8,128)(2,1)S(1)}, u32[]{:S(2)}) copy-start(bf16[128,3,128]{2,0,1:T(8,128)(2,1)S(1)} %copy.146) | copy-start | bytes 294916
  31.4 64.2 %copy-start.10 = (bf16[128,3,128]{2,0,1:T(8,128)(2,1)}, bf16[128,3,128]{2,0,1:T(8,128)(2,1)S(1)}, u32[]{:S(2)}) copy-start(bf16[128,3,128]{2,0,1:T(8,128)(2,1)S(1)} %copy.148) | copy-start | bytes 294916
  177.7 14.8 %all-to-all-start.2 = ((bf16[8,128,256]{2,1,0:T(8,128)(2,1)}), bf16[8,128,256]{2,1,0:T(8,128)(2,1)}, u32[]{:S(2)}, u32[]{:S(2)}) async-start(bf16[8,128,256]{2,1,0:T(8,128)(2,1)} %reduce_sum.188), calls=%async_computation.2 | async-start | bytes 1048576 | tf_op jit(solution)/shard_map/all_to_all | solution.py:138
  183.4 58.2 %reduce-scatter.3.cloned.1.call-start = ((), (), s32[]{:S(2)}) async-start(), calls=%async_computation.6 | async-start | bytes 2359296 | tf_op jit(solution)/shard_map/reduce_scatter | solution.py:162
  198.4 80.9 %reduce-scatter.5.cloned.1.call-start = ((), (), s32[]{:S(2)}) async-start(), calls=%async_computation.7 | async-start | bytes 983040 | tf_op jit(solution)/shard_map/reduce_scatter | solution.py:162
  201.2 18.7 %collective-permute-start = (bf16[128,256]{1,0:T(8,128)(2,1)}, bf16[128,256]{1,0:T(8,128)(2,1)}, u32[]{:S(2)}, u32[]{:S(2)}) collective-permute-start(bf16[128,256]{1,0:T(8,128)(2,1)} %constant_dynamic-update-slice_fusion), channel_id=1, source_target_pairs={{0,64},{8,72},{16,80},{24,88},{32,96},{40,104},{48,112},{56,120},{... | collective-permute-start | bytes 196616 | tf_op jit(solution)/shard_map/ppermute | solution.py:20
  202.5 20.8 %collective-permute-start.1 = (bf16[128,256]{1,0:T(8,128)(2,1)}, bf16[128,256]{1,0:T(8,128)(2,1)}, u32[]{:S(2)}, u32[]{:S(2)}) collective-permute-start(bf16[128,256]{1,0:T(8,128)(2,1)} %constant_dynamic-update-slice_fusion), channel_id=1, source_target_pairs={{0,56},{8,64},{16,72},{24,80},{32,88},{40,96},{48,104},{56,112},{6... | collective-permute-start | bytes 196616 | tf_op jit(solution)/shard_map/ppermute | solution.py:20
  203.8 23.7 %collective-permute-start.2 = (bf16[128,256]{1,0:T(8,128)(2,1)}, bf16[128,256]{1,0:T(8,128)(2,1)}, u32[]{:S(2)}, u32[]{:S(2)}) collective-permute-start(bf16[128,256]{1,0:T(8,128)(2,1)} %constant_dynamic-update-slice_fusion), channel_id=1, source_target_pairs={{0,48},{8,56},{16,64},{24,72},{32,80},{40,88},{48,96},{56,104},{64... | collective-permute-start | bytes 196616 | tf_op jit(solution)/shard_map/ppermute | solution.py:20
  207.9 23.9 %collective-permute-start.3 = (bf16[128,256]{1,0:T(8,128)(2,1)}, bf16[128,256]{1,0:T(8,128)(2,1)}, u32[]{:S(2)}, u32[]{:S(2)}) collective-permute-start(bf16[128,256]{1,0:T(8,128)(2,1)} %constant_dynamic-update-slice_fusion), channel_id=1, source_target_pairs={{0,40},{8,48},{16,56},{24,64},{32,72},{40,80},{48,88},{56,96},{64,... | collective-permute-start | bytes 196616 | tf_op jit(solution)/shard_map/ppermute | solution.py:20
  212.6 20.6 %collective-permute-start.4 = (bf16[128,256]{1,0:T(8,128)(2,1)}, bf16[128,256]{1,0:T(8,128)(2,1)}, u32[]{:S(2)}, u32[]{:S(2)}) collective-permute-start(bf16[128,256]{1,0:T(8,128)(2,1)} %constant_dynamic-update-slice_fusion), channel_id=1, source_target_pairs={{0,32},{8,40},{16,48},{24,56},{32,64},{40,72},{48,80},{56,88},{64,... | collective-permute-start | bytes 196616 | tf_op jit(solution)/shard_map/ppermute | solution.py:20
  219.9 14.8 %collective-permute-start.5 = (bf16[128,256]{1,0:T(8,128)(2,1)}, bf16[128,256]{1,0:T(8,128)(2,1)S(1)}, u32[]{:S(2)}, u32[]{:S(2)}) collective-permute-start(bf16[128,256]{1,0:T(8,128)(2,1)} %constant_dynamic-update-slice_fusion), channel_id=1, source_target_pairs={{0,24},{8,32},{16,40},{24,48},{32,56},{40,64},{48,72},{56,80},{64,... | collective-permute-start | bytes 196616 | tf_op jit(solution)/shard_map/ppermute | solution.py:20
  223.3 14.3 %collective-permute-start.6 = (bf16[128,256]{1,0:T(8,128)(2,1)}, bf16[128,256]{1,0:T(8,128)(2,1)S(1)}, u32[]{:S(2)}, u32[]{:S(2)}) collective-permute-start(bf16[128,256]{1,0:T(8,128)(2,1)} %constant_dynamic-update-slice_fusion), channel_id=1, source_target_pairs={{0,16},{8,24},{16,32},{24,40},{32,48},{40,56},{48,64},{56,72},{64,... | collective-permute-start | bytes 196616 | tf_op jit(solution)/shard_map/ppermute | solution.py:20
  227.5 10.7 %collective-permute-start.7 = (bf16[128,256]{1,0:T(8,128)(2,1)}, bf16[128,256]{1,0:T(8,128)(2,1)S(1)}, u32[]{:S(2)}, u32[]{:S(2)}) collective-permute-start(bf16[128,256]{1,0:T(8,128)(2,1)} %constant_dynamic-update-slice_fusion), channel_id=1, source_target_pairs={{0,8},{8,16},{16,24},{24,32},{32,40},{40,48},{48,56},{56,64},{64,7... | collective-permute-start | bytes 196616 | tf_op jit(solution)/shard_map/ppermute | solution.py:20
  247.3 47.1 %copy-start.20 = (bf16[128,384]{1,0:T(8,128)(2,1)S(1)}, bf16[128,384]{1,0:T(8,128)(2,1)}, u32[]{:S(2)}) copy-start(bf16[128,384]{1,0:T(8,128)(2,1)} %param.25) | copy-start | bytes 294916
  319.3 34.3 %collective-permute-start.15 = (f32[128,256]{0,1:T(8,128)}, f32[128,256]{0,1:T(8,128)}, u32[]{:S(2)}, u32[]{:S(2)}) collective-permute-start(f32[128,256]{0,1:T(8,128)} %get-tuple-element.45), channel_id=1, source_target_pairs={{64,0},{72,8},{80,16},{88,24},{96,32},{104,40},{112,48},{120,56},{... | collective-permute-start | bytes 393224 | tf_op jit(solution)/shard_map/ppermute | solution.py:20
  322.9 34.5 %collective-permute-start.14 = (f32[128,256]{0,1:T(8,128)}, f32[128,256]{0,1:T(8,128)}, u32[]{:S(2)}, u32[]{:S(2)}) collective-permute-start(f32[128,256]{0,1:T(8,128)} %get-tuple-element.46), channel_id=1, source_target_pairs={{56,0},{64,8},{72,16},{80,24},{88,32},{96,40},{104,48},{112,56},{1... | collective-permute-start | bytes 393224 | tf_op jit(solution)/shard_map/ppermute | solution.py:20
  336.9 23.5 %collective-permute-start.13 = (f32[128,256]{0,1:T(8,128)}, f32[128,256]{0,1:T(8,128)}, u32[]{:S(2)}, u32[]{:S(2)}) collective-permute-start(f32[128,256]{0,1:T(8,128)} %get-tuple-element.44), channel_id=1, source_target_pairs={{48,0},{56,8},{64,16},{72,24},{80,32},{88,40},{96,48},{104,56},{11... | collective-permute-start | bytes 393224 | tf_op jit(solution)/shard_map/ppermute | solution.py:20
  346.6 22.9 %collective-permute-start.12 = (f32[128,256]{0,1:T(8,128)}, f32[128,256]{0,1:T(8,128)}, u32[]{:S(2)}, u32[]{:S(2)}) collective-permute-start(f32[128,256]{0,1:T(8,128)} %get-tuple-element.43), channel_id=1, source_target_pairs={{40,0},{48,8},{56,16},{64,24},{72,32},{80,40},{88,48},{96,56},{104... | collective-permute-start | bytes 393224 | tf_op jit(solution)/shard_map/ppermute | solution.py:20
  348.8 20.7 %collective-permute-start.11 = (f32[128,256]{0,1:T(8,128)}, f32[128,256]{0,1:T(8,128)}, u32[]{:S(2)}, u32[]{:S(2)}) collective-permute-start(f32[128,256]{0,1:T(8,128)} %get-tuple-element.42), channel_id=1, source_target_pairs={{32,0},{40,8},{48,16},{56,24},{64,32},{72,40},{80,48},{88,56},{96,... | collective-permute-start | bytes 393224 | tf_op jit(solution)/shard_map/ppermute | solution.py:20
  353.7 18.3 %collective-permute-start.10 = (f32[128,256]{0,1:T(8,128)}, f32[128,256]{0,1:T(8,128)}, u32[]{:S(2)}, u32[]{:S(2)}) collective-permute-start(f32[128,256]{0,1:T(8,128)} %get-tuple-element.41), channel_id=1, source_target_pairs={{24,0},{32,8},{40,16},{48,24},{56,32},{64,40},{72,48},{80,56},{88,... | collective-permute-start | bytes 393224 | tf_op jit(solution)/shard_map/ppermute | solution.py:20
  357.4 20.4 %collective-permute-start.9 = (f32[128,256]{0,1:T(8,128)}, f32[128,256]{0,1:T(8,128)}, u32[]{:S(2)}, u32[]{:S(2)}) collective-permute-start(f32[128,256]{0,1:T(8,128)} %get-tuple-element.40), channel_id=1, source_target_pairs={{16,0},{24,8},{32,16},{40,24},{48,32},{56,40},{64,48},{72,56},{80,... | collective-permute-start | bytes 393224 | tf_op jit(solution)/shard_map/ppermute | solution.py:20
  360.5 17.5 %collective-permute-start.8 = (f32[128,256]{0,1:T(8,128)}, f32[128,256]{0,1:T(8,128)}, u32[]{:S(2)}, u32[]{:S(2)}) collective-permute-start(f32[128,256]{0,1:T(8,128)} %get-tuple-element.39), channel_id=1, source_target_pairs={{8,0},{16,8},{24,16},{32,24},{40,32},{48,40},{56,48},{64,56},{72,6... | collective-permute-start | bytes 393224 | tf_op jit(solution)/shard_map/ppermute | solution.py:20
  (22 other events, 254.8 us)
Sparse Core Ops, SparseCore 0:
  27.9 54.5 all-gather.1
  198.5 38.5 reduce-scatter.2
  241.7 37.5 reduce-scatter.4

commit v4 on v3

--- a/solution.py
+++ b/solution.py
@@ -157,18 +157,25 @@
     normed_part = normed_part + lax.dot_general(
         shared_grad[:, key_width:], weight_value, contract, preferred_element_type=jnp.float32
     )
-    normed_cols = normed_part
+    column_count = norm_input.shape[1]
+    inputs_full = norm_input
+    for axis in reversed(HEAD):
+        inputs_full = lax.all_gather(inputs_full, axis, axis=1, tiled=True)
+    inputs_full = inputs_full.astype(jnp.float32)
+    square_sum = jnp.sum(inputs_full * inputs_full, axis=1)
+    inner_part = jnp.sum(normed_part * norm_gain[None, :] * inputs_full, axis=1)
+    head_count = normed_part.shape[1] // column_count
+    extra = jnp.tile(jnp.pad(inner_part, (0, column_count - row_count)), head_count)
+    reduced = jnp.concatenate([normed_part, extra[None, :]], axis=0)
     for axis in HEAD:
-        normed_cols = lax.psum_scatter(normed_cols, axis, scatter_dimension=1, tiled=True)
-    column_count = norm_input.shape[1]
+        reduced = lax.psum_scatter(reduced, axis, scatter_dimension=1, tiled=True)
+    normed_cols = reduced[:row_count]
+    inner_sum = reduced[row_count, :row_count]
     gain_cols = lax.dynamic_slice_in_dim(
         norm_gain, lax.axis_index(HEAD) * column_count, column_count
     )
     inputs = norm_input.astype(jnp.float32)
     gained = normed_cols * gain_cols[None, :]
-    square_sum, inner_sum = lax.psum(
-        (jnp.sum(inputs * inputs, axis=1), jnp.sum(gained * inputs, axis=1)), HEAD
-    )
     scaling = lax.rsqrt(square_sum / D + 1e-06)[:, None]
     stream = (
         scaling * gained
@@ -185,8 +192,13 @@
 
     reach_count = WINDOW // row_count
     own_window = jnp.concatenate([keys_window, values_window], axis=1)
-    pieces = [from_behind(own_window, CTX, distance) for distance in range(reach_count, 0, -1)]
-    window_all = jnp.concatenate(pieces + [own_window], axis=0)
+    block = own_window
+    for axis in reversed(CTX[1:]):
+        block = lax.all_gather(block, axis, axis=0, tiled=True)
+    earlier = from_behind(block, CTX[0], 1)
+    frame = jnp.concatenate([earlier, block], axis=0)
+    in_block = shard_index % (block.shape[0] // row_count)
+    window_all = lax.dynamic_slice_in_dim(frame, in_block * row_count, WINDOW + row_count)
     own_place = first_row + jnp.arange(row_count, dtype=jnp.int32)
     window_place = first_row - WINDOW + jnp.arange(WINDOW + row_count, dtype=jnp.int32)
     padded = jnp.concatenate([jnp.full((WINDOW,), -1, jnp.int32), segments])

time: 390 us -> 375 us (0.962)
  blocking collectives: 115 us -> 143 us
  starting transfers between devices: 67.5 us -> 45.4 us
  local copies, waits for them, and re-layouts: 35.1 us -> 21.3 us
  waiting for transfers between devices: 98 us -> 87.8 us
  other arithmetic: 24.2 us -> 28.9 us
    all_gather x0 -> x4, blocking collectives: none -> 41.5 us  [the longest x2 22.6 us: local(): block = lax.all_gather(block, axis, axis=0, tiled=True)]
    ppermute x16 -> x9, starting transfers between devices: 61.7 us -> 39.7 us  [from_behind(): lax.ppermute(value, axis, [(source, source + steps) for source in range(f...]
    psum x1 -> x0, blocking collectives: 14 us -> none  [local(): lax.psum((jnp.sum(inputs * inputs, axis=1), jnp.sum(gained * inputs, axis...]
    unnamed x69 -> x73, local copies, waits for them, and re-layouts: 19.5 us -> 8.71 us
    reduce_scatter x2, waiting for transfers between devices: 30.9 us -> 23.8 us  [local(): reduced = lax.psum_scatter(reduced, axis, scatter_dimension=1, tiled=True)]
    all_to_all x1, waiting for transfers between devices: 6.77 us -> 0.01 us  [local(): lax.all_to_all(summed, CTX[place], split_axis=place, concat_axis=place, t...]
    concatenate x0 -> x3, other arithmetic: none -> 4.4 us  [the longest x1 2.22 us: local(): frame = jnp.concatenate([earlier, block], axis=0)]
    ppermute x16 -> x9, waiting for transfers between devices: 10.6 us -> 14.4 us  [from_behind(): lax.ppermute(value, axis, [(source, source + steps) for source in range(f...]
  transfers between devices with their start and end apart: 20 -> 13, of which waited for: 7 -> 7; matrix products, arithmetic and copies ran while one was open for 11% -> 9% of each run, Pallas kernels for 0% -> 0%
where the time goes in v4:
time: 375 us; the launch traced here: 373 us
  blocking collectives  143 us (38%)
  waiting for transfers between devices  87.8 us (23%)
  starting transfers between devices  45.4 us (12%)
  matrix products  32.6 us (9%)
  other arithmetic  28.9 us (8%)
  local copies, waits for them, and re-layouts  21.3 us (6%)
  between operations  14.5 us (4%)
    all_to_all x2, blocking collectives, local(): lax.all_to_all(summed, CTX[place], split_axis=place, concat_axis=place, t...  63.8 us
    all_gather x1, waiting for transfers between devices, local(): gathered = lax.all_gather(gathered, axis, axis=0, tiled=True)  49.6 us
    ppermute x9, starting transfers between devices, from_behind(): lax.ppermute(value, axis, [(source, source + steps) for source in range(f...  39.7 us
    reduce_scatter x2, waiting for transfers between devices, local(): reduced = lax.psum_scatter(reduced, axis, scatter_dimension=1, tiled=True)  23.8 us
    all_gather x2, blocking collectives, local(): block = lax.all_gather(block, axis, axis=0, tiled=True)  22.6 us
    all_gather x2, blocking collectives, local(): gathered = lax.all_gather(gathered, axis, axis=0, tiled=True)  19.6 us
    all_gather x2, blocking collectives, local(): inputs_full = lax.all_gather(inputs_full, axis, axis=1, tiled=True)  18.9 us
    all_gather x2, blocking collectives, local(): stream_full = lax.all_gather(stream_full, axis, axis=1, tiled=True)  17.6 us
  transfers between devices with their start and end apart: 13, of which 7 were waited for; matrix products, arithmetic and copies ran while one was open for 9% of the time, Pallas kernels for 0%

profile of v4, /device:TPU:449, one launch (start us, length us, event | category | flops | bytes accessed | tf_op | source)
XLA Modules:
  0.0 373.2 jit_solution(6548407052704707457)
XLA Ops:
  10.4 17.3 %all_gather.28 = bf16[1024,256]{1,0:T(8,128)(2,1)} all-gather(bf16[256,256]{1,0:T(8,128)(2,1)S(1)} %all_gather.27), channel_id=1, replica_groups=mesh['z'=8,'yh'=4,'core'=2,'yl'=2,'x'=4] {'yh'}, dimensions={0}, use_global_device_ids=true | all-gather | bytes 655360 | tf_op jit(solution)/shard_map/all_gather | solution.py:96
  32.9 49.6 %all-gather.2.cloned.1.call-done = bf16[8192,256]{1,0:T(8,128)(2,1)} async-done(((bf16[1024,256]{1,0:T(8,128)(2,1)}), bf16[8192,256]{1,0:T(8,128)(2,1)}) %all-gather.2.cloned.1.call-update) | async-done | bytes 4194320 | tf_op jit(solution)/shard_map/all_gather | solution.py:96
  82.5 4.6 %copy.144 = bf16[64,128,256]{2,0,1:T(8,128)(2,1)S(1)} copy(bf16[64,128,256]{2,1,0:T(8,128)(2,1)} %bitcast.222) | data formatting | bytes 8388608 | tf_op jit(solution)/shard_map/reshape | solution.py:98
  104.1 8.4 %all_to_all.15 = bf16[8,4,2,128,256]{4,3,1,0,2:T(8,128)(2,1)} all-to-all(bf16[8,4,2,128,256]{4,3,1,0,2:T(8,128)(2,1)S(1)} %copy.180), channel_id=1, replica_groups=mesh['z'=8,'yh'=4,'core'=2,'yl'=2,'x'=4] {'core'}, dimensions={2} | all-to-all | bytes 8388608 | tf_op jit(solution)/shard_map/all_to_all | solution.py:138
  112.6 5.1 %reduce_sum.187 = bf16[8,4,128,256]{3,2,1,0:T(8,128)(2,1)} reduce(bf16[8,4,2,128,256]{4,3,1,0,2:T(8,128)(2,1)} %all_to_all.15, bf16[]{:T(256)} %constant.78.clone.1), dimensions={2}, to_apply=%region_16.17 | reduce | flops 1048576 | bytes 6291458 | tf_op jit(solution)/shard_map/reduce_sum | solution.py:139
  119.4 55.4 %all_to_all.16 = bf16[8,4,128,256]{3,2,0,1:T(8,128)(2,1)} all-to-all(bf16[8,4,128,256]{3,2,0,1:T(8,128)(2,1)S(1)} %copy.155), channel_id=1, replica_groups=mesh['z'=8,'yh'=4,'core'=2,'yl'=2,'x'=4] {'yh'}, dimensions={1} | all-to-all | bytes 4194304 | tf_op jit(solution)/shard_map/all_to_all | solution.py:138
  174.8 2.9 reduce_sum.188
  177.7 5.7 %all-to-all-start.2 = ((bf16[8,128,256]{2,1,0:T(8,128)(2,1)}), bf16[8,128,256]{2,1,0:T(8,128)(2,1)}, u32[]{:S(2)}, u32[]{:S(2)}) async-start(bf16[8,128,256]{2,1,0:T(8,128)(2,1)} %reduce_sum.188), calls=%async_computation.2 | async-start | bytes 1048576 | tf_op jit(solution)/shard_map/all_to_all | solution.py:138
  185.7 11.3 %all_gather.30 = bf16[128,1536]{1,0:T(8,128)(2,1)S(1)} all-gather(bf16[128,384]{1,0:T(8,128)(2,1)} %param.21), channel_id=1, replica_groups=mesh['z'=8,'yh'=4,'core'=2,'yl'=2,'x'=4] {'x'}, dimensions={1}, use_global_device_ids=true | all-gather | bytes 491520 | tf_op jit(solution)/shard_map/all_gather | solution.py:163
  197.1 7.5 %all_gather.31 = bf16[128,3072]{1,0:T(8,128)(2,1)} all-gather(bf16[128,1536]{1,0:T(8,128)(2,1)S(1)} %all_gather.30), channel_id=1, replica_groups=mesh['z'=8,'yh'=4,'core'=2,'yl'=2,'x'=4] {'yl'}, dimensions={1}, use_global_device_ids=true | all-gather | bytes 1179648 | tf_op jit(solution)/shard_map/all_gather | solution.py:163
  212.4 6.9 %all_gather.32 = bf16[256,256]{1,0:T(8,128)(2,1)S(1)} all-gather(bf16[128,256]{1,0:T(8,128)(2,1)S(1)} %pad_maximum_fusion.4), channel_id=1, replica_groups=mesh['z'=8,'yh'=4,'core'=2,'yl'=2,'x'=4] {'core'}, dimensions={0}, use_global_device_ids=true | all-gather | bytes 196608 | tf_op jit(solution)/shard_map/all_gather | solution.py:197
  219.3 15.8 %all_gather.33 = bf16[1024,256]{1,0:T(8,128)(2,1)} all-gather(bf16[256,256]{1,0:T(8,128)(2,1)S(1)} %all_gather.32), channel_id=1, replica_groups=mesh['z'=8,'yh'=4,'core'=2,'yl'=2,'x'=4] {'yh'}, dimensions={0}, use_global_device_ids=true | all-gather | bytes 655360 | tf_op jit(solution)/shard_map/all_gather | solution.py:197
  242.2 6.8 %collective-permute-done = bf16[1024,256]{1,0:T(8,128)(2,1)} collective-permute-done((bf16[1024,256]{1,0:T(8,128)(2,1)}, bf16[1024,256]{1,0:T(8,128)(2,1)}, u32[]{:S(2)}, u32[]{:S(2)}) %collective-permute-start) | collective-permute-done | bytes 524320 | tf_op jit(solution)/shard_map/ppermute | solution.py:20
  260.2 21.6 %reduce-scatter.5.cloned.1.call-done = f32[129,384]{1,0:T(8,128)} async-done(((f32[129,1536]{1,0:T(8,128)}), f32[129,384]{1,0:T(8,128)}) %reduce-scatter.5.cloned.1.call-update) | async-done | bytes 198160 | tf_op jit(solution)/shard_map/reduce_scatter | solution.py:171
  283.6 10.0 %all_gather.34 = bf16[128,1536]{1,0:T(8,128)(2,1)S(1)} all-gather(bf16[128,384]{1,0:T(8,128)(2,1)S(1)} %fusion.70), channel_id=1, replica_groups=mesh['z'=8,'yh'=4,'core'=2,'yl'=2,'x'=4] {'x'}, dimensions={1}, use_global_device_ids=true | all-gather | bytes 491520 | tf_op jit(solution)/shard_map/all_gather | solution.py:188
  293.6 7.6 %all_gather.35 = bf16[128,3072]{1,0:T(8,128)(2,1)S(1)} all-gather(bf16[128,1536]{1,0:T(8,128)(2,1)S(1)} %all_gather.34), channel_id=1, replica_groups=mesh['z'=8,'yh'=4,'core'=2,'yl'=2,'x'=4] {'yl'}, dimensions={1}, use_global_device_ids=true | all-gather | bytes 1179648 | tf_op jit(solution)/shard_map/all_gather | solution.py:188
  308.6 3.4 collective-permute-start.8
  312.1 10.7 %collective-permute-start.7 = (f32[128,256]{0,1:T(8,128)}, f32[128,256]{0,1:T(8,128)}, u32[]{:S(2)}, u32[]{:S(2)}) collective-permute-start(f32[128,256]{0,1:T(8,128)} %get-tuple-element.44), channel_id=1, source_target_pairs={{56,0},{64,8},{72,16},{80,24},{88,32},{96,40},{104,48},{112,56},{1... | collective-permute-start | bytes 393224 | tf_op jit(solution)/shard_map/ppermute | solution.py:20
  322.7 5.5 %collective-permute-start.6 = (f32[128,256]{0,1:T(8,128)}, f32[128,256]{0,1:T(8,128)}, u32[]{:S(2)}, u32[]{:S(2)}) collective-permute-start(f32[128,256]{0,1:T(8,128)} %get-tuple-element.42), channel_id=1, source_target_pairs={{48,0},{56,8},{64,16},{72,24},{80,32},{88,40},{96,48},{104,56},{11... | collective-permute-start | bytes 393224 | tf_op jit(solution)/shard_map/ppermute | solution.py:20
  335.7 3.8 %collective-permute-start.4 = (f32[128,256]{0,1:T(8,128)}, f32[128,256]{0,1:T(8,128)}, u32[]{:S(2)}, u32[]{:S(2)}) collective-permute-start(f32[128,256]{0,1:T(8,128)} %get-tuple-element.40), channel_id=1, source_target_pairs={{32,0},{40,8},{48,16},{56,24},{64,32},{72,40},{80,48},{88,56},{96,... | collective-permute-start | bytes 393224 | tf_op jit(solution)/shard_map/ppermute | solution.py:20
  339.5 3.7 %collective-permute-start.3 = (f32[128,256]{0,1:T(8,128)}, f32[128,256]{0,1:T(8,128)}, u32[]{:S(2)}, u32[]{:S(2)}) collective-permute-start(f32[128,256]{0,1:T(8,128)} %get-tuple-element.39), channel_id=1, source_target_pairs={{24,0},{32,8},{40,16},{48,24},{56,32},{64,40},{72,48},{80,56},{88,... | collective-permute-start | bytes 393224 | tf_op jit(solution)/shard_map/ppermute | solution.py:20
  343.2 4.1 %collective-permute-start.2 = (f32[128,256]{0,1:T(8,128)}, f32[128,256]{0,1:T(8,128)}, u32[]{:S(2)}, u32[]{:S(2)}) collective-permute-start(f32[128,256]{0,1:T(8,128)} %get-tuple-element.38), channel_id=1, source_target_pairs={{16,0},{24,8},{32,16},{40,24},{48,32},{56,40},{64,48},{72,56},{80,... | collective-permute-start | bytes 393224 | tf_op jit(solution)/shard_map/ppermute | solution.py:20
  347.3 5.0 %collective-permute-start.1 = (f32[128,256]{0,1:T(8,128)}, f32[128,256]{0,1:T(8,128)}, u32[]{:S(2)}, u32[]{:S(2)}) collective-permute-start(f32[128,256]{0,1:T(8,128)} %get-tuple-element.37), channel_id=1, source_target_pairs={{8,0},{16,8},{24,16},{32,24},{40,32},{48,40},{56,48},{64,56},{72,6... | collective-permute-start | bytes 393224 | tf_op jit(solution)/shard_map/ppermute | solution.py:20
  357.8 6.0 %collective-permute-done.2 = f32[128,256]{0,1:T(8,128)} collective-permute-done((f32[128,256]{0,1:T(8,128)}, f32[128,256]{0,1:T(8,128)}, u32[]{:S(2)}, u32[]{:S(2)}) %collective-permute-start.2) | collective-permute-done | bytes 131104 | tf_op jit(solution)/shard_map/ppermute | solution.py:20
  (184 shorter events, 79.9 us)
Async XLA Ops:
  7.2 294.1 %copy-start = (bf16[384,3072]{1,0:T(8,128)(2,1)S(1)}, bf16[384,3072]{1,0:T(8,128)(2,1)}, u32[]{:S(2)}) copy-start(bf16[384,3072]{1,0:T(8,128)(2,1)} %param.26) | copy-start | bytes 7077892
  7.2 23.9 %copy-start.16 = (s32[8192]{0:T(1024)S(1)}, s32[8192]{0:T(1024)}, u32[]{:S(2)}) copy-start(s32[8192]{0:T(1024)} %param.19) | copy-start | bytes 98308
  7.2 24.0 %copy-start.23 = (bf16[128,384]{1,0:T(8,128)(2,1)S(1)}, bf16[128,384]{1,0:T(8,128)(2,1)}, u32[]{:S(2)}) copy-start(bf16[128,384]{1,0:T(8,128)(2,1)} %param.16) | copy-start | bytes 294916
  7.2 75.3 %all-gather.2.cloned.1.call-start = ((), (), s32[]{:S(2)}) async-start(), calls=%async_computation.5 | async-start | bytes 4718592 | tf_op jit(solution)/shard_map/all_gather | solution.py:96
  31.1 62.2 %copy-start.21 = (bf16[128,3,128]{2,0,1:T(8,128)(2,1)}, bf16[128,3,128]{2,0,1:T(8,128)(2,1)S(1)}, u32[]{:S(2)}) copy-start(bf16[128,3,128]{2,0,1:T(8,128)(2,1)S(1)} %copy.146) | copy-start | bytes 294916
  31.4 64.2 %copy-start.14 = (bf16[128,3,128]{2,0,1:T(8,128)(2,1)}, bf16[128,3,128]{2,0,1:T(8,128)(2,1)S(1)}, u32[]{:S(2)}) copy-start(bf16[128,3,128]{2,0,1:T(8,128)(2,1)S(1)} %copy.148) | copy-start | bytes 294916
  177.7 26.9 %all-to-all-start.2 = ((bf16[8,128,256]{2,1,0:T(8,128)(2,1)}), bf16[8,128,256]{2,1,0:T(8,128)(2,1)}, u32[]{:S(2)}, u32[]{:S(2)}) async-start(bf16[8,128,256]{2,1,0:T(8,128)(2,1)} %reduce_sum.188), calls=%async_computation.2 | async-start | bytes 1048576 | tf_op jit(solution)/shard_map/all_to_all | solution.py:138
  183.3 70.0 %reduce-scatter.3.cloned.1.call-start = ((), (), s32[]{:S(2)}) async-start(), calls=%async_computation.6 | async-start | bytes 2506752 | tf_op jit(solution)/shard_map/reduce_scatter | solution.py:171
  211.6 70.3 %reduce-scatter.5.cloned.1.call-start = ((), (), s32[]{:S(2)}) async-start(), calls=%async_computation.7 | async-start | bytes 1044480 | tf_op jit(solution)/shard_map/reduce_scatter | solution.py:171
  235.0 13.9 %collective-permute-start = (bf16[1024,256]{1,0:T(8,128)(2,1)}, bf16[1024,256]{1,0:T(8,128)(2,1)}, u32[]{:S(2)}, u32[]{:S(2)}) collective-permute-start(bf16[1024,256]{1,0:T(8,128)(2,1)} %all_gather.33), channel_id=1, source_target_pairs={{0,64},{64,128},{128,192},{192,256},{256,320},{320,384},{384,448},... | collective-permute-start | bytes 1572872 | tf_op jit(solution)/shard_map/ppermute | solution.py:20
  259.0 23.5 %copy-start.19 = (bf16[128,384]{1,0:T(8,128)(2,1)S(1)}, bf16[128,384]{1,0:T(8,128)(2,1)}, u32[]{:S(2)}) copy-start(bf16[128,384]{1,0:T(8,128)(2,1)} %param.21) | copy-start | bytes 294916
  259.0 23.5 %copy-start.24 = (bf16[128,384]{1,0:T(8,128)(2,1)S(1)}, bf16[128,384]{1,0:T(8,128)(2,1)}, u32[]{:S(2)}) copy-start(bf16[128,384]{1,0:T(8,128)(2,1)} %param.25) | copy-start | bytes 294916
  307.1 22.4 %copy-start.5 = (bf16[3,128,1152]{1,2,0:T(8,128)(2,1)}, bf16[3,128,1152]{1,2,0:T(8,128)(2,1)S(1)}, u32[]{:S(2)}) copy-start(bf16[3,128,1152]{1,2,0:T(8,128)(2,1)S(1)} %fusion.25) | copy-start | bytes 2654212
  307.1 22.4 %copy-start.25 = (bf16[3,32,128]{2,1,0:T(8,128)(2,1)S(1)}, bf16[3,32,128]{2,1,0:T(8,128)(2,1)}, u32[]{:S(2)}) copy-start(bf16[3,32,128]{2,1,0:T(8,128)(2,1)} %fusion.50) | copy-start | bytes 73732
  307.1 22.4 %copy-start.26 = (bf16[3,32,128]{2,1,0:T(8,128)(2,1)S(1)}, bf16[3,32,128]{2,1,0:T(8,128)(2,1)}, u32[]{:S(2)}) copy-start(bf16[3,32,128]{2,1,0:T(8,128)(2,1)} %fusion.52) | copy-start | bytes 73732
  307.1 22.4 %copy-start.27 = (bf16[3,32,128]{2,1,0:T(8,128)(2,1)S(1)}, bf16[3,32,128]{2,1,0:T(8,128)(2,1)}, u32[]{:S(2)}) copy-start(bf16[3,32,128]{2,1,0:T(8,128)(2,1)} %fusion.51) | copy-start | bytes 73732
  308.6 30.9 %collective-permute-start.8 = (f32[128,256]{0,1:T(8,128)}, f32[128,256]{0,1:T(8,128)}, u32[]{:S(2)}, u32[]{:S(2)}) collective-permute-start(f32[128,256]{0,1:T(8,128)} %get-tuple-element.43), channel_id=1, source_target_pairs={{64,0},{72,8},{80,16},{88,24},{96,32},{104,40},{112,48},{120,56},{... | collective-permute-start | bytes 393224 | tf_op jit(solution)/shard_map/ppermute | solution.py:20
  312.1 31.2 %collective-permute-start.7 = (f32[128,256]{0,1:T(8,128)}, f32[128,256]{0,1:T(8,128)}, u32[]{:S(2)}, u32[]{:S(2)}) collective-permute-start(f32[128,256]{0,1:T(8,128)} %get-tuple-element.44), channel_id=1, source_target_pairs={{56,0},{64,8},{72,16},{80,24},{88,32},{96,40},{104,48},{112,56},{1... | collective-permute-start | bytes 393224 | tf_op jit(solution)/shard_map/ppermute | solution.py:20
  322.7 24.6 %collective-permute-start.6 = (f32[128,256]{0,1:T(8,128)}, f32[128,256]{0,1:T(8,128)}, u32[]{:S(2)}, u32[]{:S(2)}) collective-permute-start(f32[128,256]{0,1:T(8,128)} %get-tuple-element.42), channel_id=1, source_target_pairs={{48,0},{56,8},{64,16},{72,24},{80,32},{88,40},{96,48},{104,56},{11... | collective-permute-start | bytes 393224 | tf_op jit(solution)/shard_map/ppermute | solution.py:20
  333.5 22.8 %collective-permute-start.5 = (f32[128,256]{0,1:T(8,128)}, f32[128,256]{0,1:T(8,128)}, u32[]{:S(2)}, u32[]{:S(2)}) collective-permute-start(f32[128,256]{0,1:T(8,128)} %get-tuple-element.41), channel_id=1, source_target_pairs={{40,0},{48,8},{56,16},{64,24},{72,32},{80,40},{88,48},{96,56},{104... | collective-permute-start | bytes 393224 | tf_op jit(solution)/shard_map/ppermute | solution.py:20
  335.7 20.6 %collective-permute-start.4 = (f32[128,256]{0,1:T(8,128)}, f32[128,256]{0,1:T(8,128)}, u32[]{:S(2)}, u32[]{:S(2)}) collective-permute-start(f32[128,256]{0,1:T(8,128)} %get-tuple-element.40), channel_id=1, source_target_pairs={{32,0},{40,8},{48,16},{56,24},{64,32},{72,40},{80,48},{88,56},{96,... | collective-permute-start | bytes 393224 | tf_op jit(solution)/shard_map/ppermute | solution.py:20
  339.5 18.3 %collective-permute-start.3 = (f32[128,256]{0,1:T(8,128)}, f32[128,256]{0,1:T(8,128)}, u32[]{:S(2)}, u32[]{:S(2)}) collective-permute-start(f32[128,256]{0,1:T(8,128)} %get-tuple-element.39), channel_id=1, source_target_pairs={{24,0},{32,8},{40,16},{48,24},{56,32},{64,40},{72,48},{80,56},{88,... | collective-permute-start | bytes 393224 | tf_op jit(solution)/shard_map/ppermute | solution.py:20
  343.2 20.5 %collective-permute-start.2 = (f32[128,256]{0,1:T(8,128)}, f32[128,256]{0,1:T(8,128)}, u32[]{:S(2)}, u32[]{:S(2)}) collective-permute-start(f32[128,256]{0,1:T(8,128)} %get-tuple-element.38), channel_id=1, source_target_pairs={{16,0},{24,8},{32,16},{40,24},{48,32},{56,40},{64,48},{72,56},{80,... | collective-permute-start | bytes 393224 | tf_op jit(solution)/shard_map/ppermute | solution.py:20
  347.3 16.5 %collective-permute-start.1 = (f32[128,256]{0,1:T(8,128)}, f32[128,256]{0,1:T(8,128)}, u32[]{:S(2)}, u32[]{:S(2)}) collective-permute-start(f32[128,256]{0,1:T(8,128)} %get-tuple-element.37), channel_id=1, source_target_pairs={{8,0},{16,8},{24,16},{32,24},{40,32},{48,40},{56,48},{64,56},{72,6... | collective-permute-start | bytes 393224 | tf_op jit(solution)/shard_map/ppermute | solution.py:20
  (21 other events, 100.5 us)
Sparse Core Ops, SparseCore 0:
  27.9 54.5 all-gather.1
  211.7 41.5 reduce-scatter.2
  256.2 25.6 reduce-scatter.4

commit v5 on v4

--- a/solution.py
+++ b/solution.py
@@ -94,6 +94,17 @@
     gathered = shared
     for axis in reversed(CTX):
         gathered = lax.all_gather(gathered, axis, axis=0, tiled=True)
+    column_count = norm_input.shape[1]
+    inputs_full = norm_input
+    for axis in reversed(HEAD):
+        inputs_full = lax.all_gather(inputs_full, axis, axis=1, tiled=True)
+    own_window = jnp.concatenate([keys_window, values_window], axis=1)
+    window_block = own_window
+    for axis in reversed(CTX[1:]):
+        window_block = lax.all_gather(window_block, axis, axis=0, tiled=True)
+    earlier = from_behind(window_block, CTX[0], 1)
+    frame = jnp.concatenate([earlier, window_block], axis=0)
+    gathered, inputs_full, frame = lax.optimization_barrier((gathered, inputs_full, frame))
     ordered = (
         gathered.reshape(shard_count, row_count, 2 * key_width)
         .transpose(1, 0, 2)
@@ -157,10 +168,6 @@
     normed_part = normed_part + lax.dot_general(
         shared_grad[:, key_width:], weight_value, contract, preferred_element_type=jnp.float32
     )
-    column_count = norm_input.shape[1]
-    inputs_full = norm_input
-    for axis in reversed(HEAD):
-        inputs_full = lax.all_gather(inputs_full, axis, axis=1, tiled=True)
     inputs_full = inputs_full.astype(jnp.float32)
     square_sum = jnp.sum(inputs_full * inputs_full, axis=1)
     inner_part = jnp.sum(normed_part * norm_gain[None, :] * inputs_full, axis=1)
@@ -191,13 +198,7 @@
     ).astype(jnp.bfloat16)
 
     reach_count = WINDOW // row_count
-    own_window = jnp.concatenate([keys_window, values_window], axis=1)
-    block = own_window
-    for axis in reversed(CTX[1:]):
-        block = lax.all_gather(block, axis, axis=0, tiled=True)
-    earlier = from_behind(block, CTX[0], 1)
-    frame = jnp.concatenate([earlier, block], axis=0)
-    in_block = shard_index % (block.shape[0] // row_count)
+    in_block = shard_index % (window_block.shape[0] // row_count)
     window_all = lax.dynamic_slice_in_dim(frame, in_block * row_count, WINDOW + row_count)
     own_place = first_row + jnp.arange(row_count, dtype=jnp.int32)
     window_place = first_row - WINDOW + jnp.arange(WINDOW + row_count, dtype=jnp.int32)

time: 375 us -> 371 us (0.989)
  waiting for transfers between devices: 87.8 us -> 75.8 us
  local copies, waits for them, and re-layouts: 21.3 us -> 28.4 us
  other arithmetic: 28.9 us -> 32.7 us
    all_gather x1, waiting for transfers between devices: 49.6 us -> 3.55 us  [local(): gathered = lax.all_gather(gathered, axis, axis=0, tiled=True)]
    reduce_scatter x2, waiting for transfers between devices: 23.8 us -> 56.2 us  [local(): reduced = lax.psum_scatter(reduced, axis, scatter_dimension=1, tiled=True)]
    all_to_all x1, waiting for transfers between devices: 0.01 us -> 6.65 us  [local(): lax.all_to_all(summed, CTX[place], split_axis=place, concat_axis=place, t...]
    ppermute x9, waiting for transfers between devices: 14.4 us -> 9.3 us  [from_behind(): lax.ppermute(value, axis, [(source, source + steps) for source in range(f...]
    and x4, other arithmetic: 0.8 us -> 5.66 us  [local(): (key_place[None, :reach] <= block_place[:, None]) & (key_segment[None, :r...]
    unnamed x73 -> x75, local copies, waits for them, and re-layouts: 8.71 us -> 9.43 us
  transfers between devices with their start and end apart: 13 -> 13, of which waited for: 7 -> 7; matrix products, arithmetic and copies ran while one was open for 9% -> 11% of each run, Pallas kernels for 0% -> 0%
where the time goes in v5:
time: 371 us; the launch traced here: 369 us
  blocking collectives  141 us (38%)
  waiting for transfers between devices  75.8 us (20%)
  starting transfers between devices  45.3 us (12%)
  other arithmetic  32.7 us (9%)
  matrix products  31.7 us (9%)
  local copies, waits for them, and re-layouts  28.4 us (8%)
  between operations  14.5 us (4%)
    all_to_all x2, blocking collectives, local(): lax.all_to_all(summed, CTX[place], split_axis=place, concat_axis=place, t...  63.8 us
    reduce_scatter x2, waiting for transfers between devices, local(): reduced = lax.psum_scatter(reduced, axis, scatter_dimension=1, tiled=True)  56.2 us
    ppermute x9, starting transfers between devices, from_behind(): lax.ppermute(value, axis, [(source, source + steps) for source in range(f...  39.7 us
    all_gather x2, blocking collectives, local(): inputs_full = lax.all_gather(inputs_full, axis, axis=1, tiled=True)  20.9 us
    all_gather x2, blocking collectives, local(): gathered = lax.all_gather(gathered, axis, axis=0, tiled=True)  19.6 us
    all_gather x2, blocking collectives, local(): window_block = lax.all_gather(window_block, axis, axis=0, tiled=True)  19.3 us
    all_gather x2, blocking collectives, local(): stream_full = lax.all_gather(stream_full, axis, axis=1, tiled=True)  17.5 us
    reduce_sum x3, other arithmetic, local(): jnp.sum(arrived.astype(jnp.float32), axis=place).astype(jnp.bfloat16)  9.74 us
  transfers between devices with their start and end apart: 13, of which 7 were waited for; matrix products, arithmetic and copies ran while one was open for 11% of the time, Pallas kernels for 0%

profile of v5, /device:TPU:449, one launch (start us, length us, event | category | flops | bytes accessed | tf_op | source)
XLA Modules:
  0.0 369.2 jit_solution(14679304526847135069)
XLA Ops:
  10.4 17.3 %all_gather.28 = bf16[1024,256]{1,0:T(8,128)(2,1)} all-gather(bf16[256,256]{1,0:T(8,128)(2,1)S(1)} %all_gather.27), channel_id=1, replica_groups=mesh['z'=8,'yh'=4,'core'=2,'yl'=2,'x'=4] {'yh'}, dimensions={0}, use_global_device_ids=true | all-gather | bytes 655360 | tf_op jit(solution)/shard_map/all_gather | solution.py:96
  28.6 5.1 %all_gather.32 = bf16[256,256]{1,0:T(8,128)(2,1)S(1)} all-gather(bf16[128,256]{1,0:T(8,128)(2,1)S(1)} %pad_maximum_fusion.5), channel_id=1, replica_groups=mesh['z'=8,'yh'=4,'core'=2,'yl'=2,'x'=4] {'core'}, dimensions={0}, use_global_device_ids=true | all-gather | bytes 196608 | tf_op jit(solution)/shard_map/all_gather | solution.py:104
  33.7 14.2 %all_gather.33 = bf16[1024,256]{1,0:T(8,128)(2,1)S(1)} all-gather(bf16[256,256]{1,0:T(8,128)(2,1)S(1)} %all_gather.32), channel_id=1, replica_groups=mesh['z'=8,'yh'=4,'core'=2,'yl'=2,'x'=4] {'yh'}, dimensions={0}, use_global_device_ids=true | all-gather | bytes 655360 | tf_op jit(solution)/shard_map/all_gather | solution.py:104
  56.1 11.9 %all_gather.30 = bf16[128,1536]{1,0:T(8,128)(2,1)S(1)} all-gather(bf16[128,384]{1,0:T(8,128)(2,1)} %param.21), channel_id=1, replica_groups=mesh['z'=8,'yh'=4,'core'=2,'yl'=2,'x'=4] {'x'}, dimensions={1}, use_global_device_ids=true | all-gather | bytes 491520 | tf_op jit(solution)/shard_map/all_gather | solution.py:100
  73.6 8.9 %all_gather.31 = bf16[128,3072]{1,0:T(8,128)(2,1)} all-gather(bf16[128,1536]{1,0:T(8,128)(2,1)S(1)} %all_gather.30), channel_id=1, replica_groups=mesh['z'=8,'yh'=4,'core'=2,'yl'=2,'x'=4] {'yl'}, dimensions={1}, use_global_device_ids=true | all-gather | bytes 1179648 | tf_op jit(solution)/shard_map/all_gather | solution.py:100
  90.2 3.5 all-gather.2.cloned.1.call-done
  93.8 4.6 %copy.144 = bf16[64,128,256]{2,0,1:T(8,128)(2,1)S(1)} copy(bf16[64,128,256]{2,1,0:T(8,128)(2,1)} %bitcast.222) | data formatting | bytes 8388608 | tf_op jit(solution)/shard_map/reshape | solution.py:109
  115.8 8.5 %all_to_all.15 = bf16[8,4,2,128,256]{4,3,1,0,2:T(8,128)(2,1)} all-to-all(bf16[8,4,2,128,256]{4,3,1,0,2:T(8,128)(2,1)S(1)} %copy.180), channel_id=1, replica_groups=mesh['z'=8,'yh'=4,'core'=2,'yl'=2,'x'=4] {'core'}, dimensions={2} | all-to-all | bytes 8388608 | tf_op jit(solution)/shard_map/all_to_all | solution.py:149
  124.3 5.1 %reduce_sum.187 = bf16[8,4,128,256]{3,2,1,0:T(8,128)(2,1)} reduce(bf16[8,4,2,128,256]{4,3,1,0,2:T(8,128)(2,1)} %all_to_all.15, bf16[]{:T(256)} %constant.78.clone.1), dimensions={2}, to_apply=%region_16.17 | reduce | flops 1048576 | bytes 6291458 | tf_op jit(solution)/shard_map/reduce_sum | solution.py:150
  131.1 55.3 %all_to_all.16 = bf16[8,4,128,256]{3,2,0,1:T(8,128)(2,1)} all-to-all(bf16[8,4,128,256]{3,2,0,1:T(8,128)(2,1)S(1)} %copy.155), channel_id=1, replica_groups=mesh['z'=8,'yh'=4,'core'=2,'yl'=2,'x'=4] {'yh'}, dimensions={1} | all-to-all | bytes 4194304 | tf_op jit(solution)/shard_map/all_to_all | solution.py:149
  189.3 5.5 %all-to-all-start.2 = ((bf16[8,128,256]{2,1,0:T(8,128)(2,1)}), bf16[8,128,256]{2,1,0:T(8,128)(2,1)}, u32[]{:S(2)}, u32[]{:S(2)}) async-start(bf16[8,128,256]{2,1,0:T(8,128)(2,1)} %reduce_sum.188), calls=%async_computation.2 | async-start | bytes 1048576 | tf_op jit(solution)/shard_map/all_to_all | solution.py:149
  197.1 6.7 %all-to-all-done.2 = bf16[8,128,256]{2,1,0:T(8,128)(2,1)} async-done(((bf16[8,128,256]{2,1,0:T(8,128)(2,1)}), bf16[8,128,256]{2,1,0:T(8,128)(2,1)}, u32[]{:S(2)}, u32[]{:S(2)}) %all-to-all-start.2) | async-done | bytes 524320 | tf_op jit(solution)/shard_map/all_to_all | solution.py:149
  217.5 32.4 %reduce-scatter.3.cloned.1.call-done = f32[129,1536]{1,0:T(8,128)} async-done(((f32[129,3072]{1,0:T(8,128)}), f32[129,1536]{1,0:T(8,128)}) %reduce-scatter.3.cloned.1.call-update) | async-done | bytes 792592 | tf_op jit(solution)/shard_map/reduce_scatter | solution.py:178
  256.3 23.8 %reduce-scatter.5.cloned.1.call-done = f32[129,384]{1,0:T(8,128)} async-done(((f32[129,1536]{1,0:T(8,128)}), f32[129,384]{1,0:T(8,128)}) %reduce-scatter.5.cloned.1.call-update) | async-done | bytes 198160 | tf_op jit(solution)/shard_map/reduce_scatter | solution.py:178
  281.8 10.0 %all_gather.34 = bf16[128,1536]{1,0:T(8,128)(2,1)S(1)} all-gather(bf16[128,384]{1,0:T(8,128)(2,1)S(1)} %fusion.69), channel_id=1, replica_groups=mesh['z'=8,'yh'=4,'core'=2,'yl'=2,'x'=4] {'x'}, dimensions={1}, use_global_device_ids=true | all-gather | bytes 491520 | tf_op jit(solution)/shard_map/all_gather | solution.py:195
  291.8 7.5 %all_gather.35 = bf16[128,3072]{1,0:T(8,128)(2,1)S(1)} all-gather(bf16[128,1536]{1,0:T(8,128)(2,1)S(1)} %all_gather.34), channel_id=1, replica_groups=mesh['z'=8,'yh'=4,'core'=2,'yl'=2,'x'=4] {'yl'}, dimensions={1}, use_global_device_ids=true | all-gather | bytes 1179648 | tf_op jit(solution)/shard_map/all_gather | solution.py:195
  307.7 3.6 collective-permute-start.8
  311.3 10.6 %collective-permute-start.7 = (f32[128,256]{0,1:T(8,128)}, f32[128,256]{0,1:T(8,128)}, u32[]{:S(2)}, u32[]{:S(2)}) collective-permute-start(f32[128,256]{0,1:T(8,128)} %get-tuple-element.50), channel_id=1, source_target_pairs={{56,0},{64,8},{72,16},{80,24},{88,32},{96,40},{104,48},{112,56},{1... | collective-permute-start | bytes 393224 | tf_op jit(solution)/shard_map/ppermute | solution.py:20
  321.9 5.3 %collective-permute-start.6 = (f32[128,256]{0,1:T(8,128)}, f32[128,256]{0,1:T(8,128)}, u32[]{:S(2)}, u32[]{:S(2)}) collective-permute-start(f32[128,256]{0,1:T(8,128)} %get-tuple-element.48), channel_id=1, source_target_pairs={{48,0},{56,8},{64,16},{72,24},{80,32},{88,40},{96,48},{104,56},{11... | collective-permute-start | bytes 393224 | tf_op jit(solution)/shard_map/ppermute | solution.py:20
  331.8 3.9 %collective-permute-start.4 = (f32[128,256]{0,1:T(8,128)}, f32[128,256]{0,1:T(8,128)}, u32[]{:S(2)}, u32[]{:S(2)}) collective-permute-start(f32[128,256]{0,1:T(8,128)} %get-tuple-element.46), channel_id=1, source_target_pairs={{32,0},{40,8},{48,16},{56,24},{64,32},{72,40},{80,48},{88,56},{96,... | collective-permute-start | bytes 393224 | tf_op jit(solution)/shard_map/ppermute | solution.py:20
  335.6 3.8 %collective-permute-start.3 = (f32[128,256]{0,1:T(8,128)}, f32[128,256]{0,1:T(8,128)}, u32[]{:S(2)}, u32[]{:S(2)}) collective-permute-start(f32[128,256]{0,1:T(8,128)} %get-tuple-element.45), channel_id=1, source_target_pairs={{24,0},{32,8},{40,16},{48,24},{56,32},{64,40},{72,48},{80,56},{88,... | collective-permute-start | bytes 393224 | tf_op jit(solution)/shard_map/ppermute | solution.py:20
  339.4 3.9 %collective-permute-start.2 = (f32[128,256]{0,1:T(8,128)}, f32[128,256]{0,1:T(8,128)}, u32[]{:S(2)}, u32[]{:S(2)}) collective-permute-start(f32[128,256]{0,1:T(8,128)} %get-tuple-element.44), channel_id=1, source_target_pairs={{16,0},{24,8},{32,16},{40,24},{48,32},{56,40},{64,48},{72,56},{80,... | collective-permute-start | bytes 393224 | tf_op jit(solution)/shard_map/ppermute | solution.py:20
  343.4 5.2 %collective-permute-start.1 = (f32[128,256]{0,1:T(8,128)}, f32[128,256]{0,1:T(8,128)}, u32[]{:S(2)}, u32[]{:S(2)}) collective-permute-start(f32[128,256]{0,1:T(8,128)} %get-tuple-element.43), channel_id=1, source_target_pairs={{8,0},{16,8},{24,16},{32,24},{40,32},{48,40},{56,48},{64,56},{72,6... | collective-permute-start | bytes 393224 | tf_op jit(solution)/shard_map/ppermute | solution.py:20
  354.1 5.7 %collective-permute-done.2 = f32[128,256]{0,1:T(8,128)} collective-permute-done((f32[128,256]{0,1:T(8,128)}, f32[128,256]{0,1:T(8,128)}, u32[]{:S(2)}, u32[]{:S(2)}) %collective-permute-start.2) | collective-permute-done | bytes 131104 | tf_op jit(solution)/shard_map/ppermute | solution.py:20
  (187 shorter events, 92.5 us)
Async XLA Ops:
  7.2 292.2 %copy-start = (bf16[384,3072]{1,0:T(8,128)(2,1)S(1)}, bf16[384,3072]{1,0:T(8,128)(2,1)}, u32[]{:S(2)}) copy-start(bf16[384,3072]{1,0:T(8,128)(2,1)} %param.26) | copy-start | bytes 7077892
  7.2 42.0 %copy-start.15 = (s32[8192]{0:T(1024)S(1)}, s32[8192]{0:T(1024)}, u32[]{:S(2)}) copy-start(s32[8192]{0:T(1024)} %param.19) | copy-start | bytes 98308
  7.2 43.6 %copy-start.23 = (s32[8192]{0:T(1024)S(1)}, s32[8192]{0:T(1024)}, u32[]{:S(2)}) copy-start(s32[8192]{0:T(1024)} %param.20) | copy-start | bytes 98308
  7.2 86.6 %all-gather.2.cloned.1.call-start = ((), (), s32[]{:S(2)}) async-start(), calls=%async_computation.5 | async-start | bytes 4718592 | tf_op jit(solution)/shard_map/all_gather | solution.py:96
  47.8 41.3 %collective-permute-start = (bf16[1024,256]{1,0:T(8,128)(2,1)S(1)}, bf16[1024,256]{1,0:T(8,128)(2,1)S(1)}, u32[]{:S(2)}, u32[]{:S(2)}) collective-permute-start(bf16[1024,256]{1,0:T(8,128)(2,1)S(1)} %all_gather.33), channel_id=1, source_target_pairs={{0,64},{64,128},{128,192},{192,256},{256,320},{320,384},{384,448},... | collective-permute-start | bytes 1572872 | tf_op jit(solution)/shard_map/ppermute | solution.py:20
  87.5 19.8 %copy-start.12 = (bf16[128,3,128]{2,0,1:T(8,128)(2,1)}, bf16[128,3,128]{2,0,1:T(8,128)(2,1)S(1)}, u32[]{:S(2)}) copy-start(bf16[128,3,128]{2,0,1:T(8,128)(2,1)S(1)} %copy.148) | copy-start | bytes 294916
  98.4 12.1 %copy-start.3 = (bf16[64,128,256]{2,0,1:T(8,128)(2,1)}, bf16[64,128,256]{2,0,1:T(8,128)(2,1)S(1)}, u32[]{:S(2)}) copy-start(bf16[64,128,256]{2,0,1:T(8,128)(2,1)S(1)} %copy.144) | copy-start | bytes 12582916
  189.3 14.5 %all-to-all-start.2 = ((bf16[8,128,256]{2,1,0:T(8,128)(2,1)}), bf16[8,128,256]{2,1,0:T(8,128)(2,1)}, u32[]{:S(2)}, u32[]{:S(2)}) async-start(bf16[8,128,256]{2,1,0:T(8,128)(2,1)} %reduce_sum.188), calls=%async_computation.2 | async-start | bytes 1048576 | tf_op jit(solution)/shard_map/all_to_all | solution.py:149
  194.8 55.2 %reduce-scatter.3.cloned.1.call-start = ((), (), s32[]{:S(2)}) async-start(), calls=%async_computation.6 | async-start | bytes 2506752 | tf_op jit(solution)/shard_map/reduce_scatter | solution.py:178
  211.6 68.5 %reduce-scatter.5.cloned.1.call-start = ((), (), s32[]{:S(2)}) async-start(), calls=%async_computation.7 | async-start | bytes 1044480 | tf_op jit(solution)/shard_map/reduce_scatter | solution.py:178
  255.6 25.1 %copy-start.17 = (bf16[128,384]{1,0:T(8,128)(2,1)S(1)}, bf16[128,384]{1,0:T(8,128)(2,1)}, u32[]{:S(2)}) copy-start(bf16[128,384]{1,0:T(8,128)(2,1)} %param.21) | copy-start | bytes 294916
  255.6 25.1 %copy-start.24 = (bf16[128,384]{1,0:T(8,128)(2,1)S(1)}, bf16[128,384]{1,0:T(8,128)(2,1)}, u32[]{:S(2)}) copy-start(bf16[128,384]{1,0:T(8,128)(2,1)} %param.25) | copy-start | bytes 294916
  281.8 18.3 %copy-start.18 = (bf16[128,384]{1,0:T(8,128)(2,1)}, bf16[128,384]{1,0:T(8,128)(2,1)S(1)}, u32[]{:S(2)}) copy-start(bf16[128,384]{1,0:T(8,128)(2,1)S(1)} %fusion.69) | copy-start | bytes 294916
  305.5 21.7 %copy-start.11 = (bf16[3,32,2048]{2,1,0:T(8,128)(2,1)S(1)}, bf16[3,32,2048]{2,1,0:T(8,128)(2,1)}, u32[]{:S(2)}) copy-start(bf16[3,32,2048]{2,1,0:T(8,128)(2,1)} %copy-done.10) | copy-start | bytes 1179652
  305.5 23.1 %copy-start.26 = (bf16[3,32,128]{2,1,0:T(8,128)(2,1)S(1)}, bf16[3,32,128]{2,1,0:T(8,128)(2,1)}, u32[]{:S(2)}) copy-start(bf16[3,32,128]{2,1,0:T(8,128)(2,1)} %fusion.50) | copy-start | bytes 73732
  305.5 23.0 %copy-start.27 = (bf16[3,32,128]{2,1,0:T(8,128)(2,1)S(1)}, bf16[3,32,128]{2,1,0:T(8,128)(2,1)}, u32[]{:S(2)}) copy-start(bf16[3,32,128]{2,1,0:T(8,128)(2,1)} %fusion.52) | copy-start | bytes 73732
  307.7 27.9 %collective-permute-start.8 = (f32[128,256]{0,1:T(8,128)}, f32[128,256]{0,1:T(8,128)}, u32[]{:S(2)}, u32[]{:S(2)}) collective-permute-start(f32[128,256]{0,1:T(8,128)} %get-tuple-element.49), channel_id=1, source_target_pairs={{64,0},{72,8},{80,16},{88,24},{96,32},{104,40},{112,48},{120,56},{... | collective-permute-start | bytes 393224 | tf_op jit(solution)/shard_map/ppermute | solution.py:20
  311.3 28.1 %collective-permute-start.7 = (f32[128,256]{0,1:T(8,128)}, f32[128,256]{0,1:T(8,128)}, u32[]{:S(2)}, u32[]{:S(2)}) collective-permute-start(f32[128,256]{0,1:T(8,128)} %get-tuple-element.50), channel_id=1, source_target_pairs={{56,0},{64,8},{72,16},{80,24},{88,32},{96,40},{104,48},{112,56},{1... | collective-permute-start | bytes 393224 | tf_op jit(solution)/shard_map/ppermute | solution.py:20
  321.9 21.4 %collective-permute-start.6 = (f32[128,256]{0,1:T(8,128)}, f32[128,256]{0,1:T(8,128)}, u32[]{:S(2)}, u32[]{:S(2)}) collective-permute-start(f32[128,256]{0,1:T(8,128)} %get-tuple-element.48), channel_id=1, source_target_pairs={{48,0},{56,8},{64,16},{72,24},{80,32},{88,40},{96,48},{104,56},{11... | collective-permute-start | bytes 393224 | tf_op jit(solution)/shard_map/ppermute | solution.py:20
  329.5 21.2 %collective-permute-start.5 = (f32[128,256]{0,1:T(8,128)}, f32[128,256]{0,1:T(8,128)S(1)}, u32[]{:S(2)}, u32[]{:S(2)}) collective-permute-start(f32[128,256]{0,1:T(8,128)} %get-tuple-element.47), channel_id=1, source_target_pairs={{40,0},{48,8},{56,16},{64,24},{72,32},{80,40},{88,48},{96,56},{104... | collective-permute-start | bytes 393224 | tf_op jit(solution)/shard_map/ppermute | solution.py:20
  331.8 18.9 %collective-permute-start.4 = (f32[128,256]{0,1:T(8,128)}, f32[128,256]{0,1:T(8,128)}, u32[]{:S(2)}, u32[]{:S(2)}) collective-permute-start(f32[128,256]{0,1:T(8,128)} %get-tuple-element.46), channel_id=1, source_target_pairs={{32,0},{40,8},{48,16},{56,24},{64,32},{72,40},{80,48},{88,56},{96,... | collective-permute-start | bytes 393224 | tf_op jit(solution)/shard_map/ppermute | solution.py:20
  335.6 18.5 %collective-permute-start.3 = (f32[128,256]{0,1:T(8,128)}, f32[128,256]{0,1:T(8,128)}, u32[]{:S(2)}, u32[]{:S(2)}) collective-permute-start(f32[128,256]{0,1:T(8,128)} %get-tuple-element.45), channel_id=1, source_target_pairs={{24,0},{32,8},{40,16},{48,24},{56,32},{64,40},{72,48},{80,56},{88,... | collective-permute-start | bytes 393224 | tf_op jit(solution)/shard_map/ppermute | solution.py:20
  339.4 20.4 %collective-permute-start.2 = (f32[128,256]{0,1:T(8,128)}, f32[128,256]{0,1:T(8,128)}, u32[]{:S(2)}, u32[]{:S(2)}) collective-permute-start(f32[128,256]{0,1:T(8,128)} %get-tuple-element.44), channel_id=1, source_target_pairs={{16,0},{24,8},{32,16},{40,24},{48,32},{56,40},{64,48},{72,56},{80,... | collective-permute-start | bytes 393224 | tf_op jit(solution)/shard_map/ppermute | solution.py:20
  343.4 16.6 %collective-permute-start.1 = (f32[128,256]{0,1:T(8,128)}, f32[128,256]{0,1:T(8,128)}, u32[]{:S(2)}, u32[]{:S(2)}) collective-permute-start(f32[128,256]{0,1:T(8,128)} %get-tuple-element.43), channel_id=1, source_target_pairs={{8,0},{16,8},{24,16},{32,24},{40,32},{48,40},{56,48},{64,56},{72,6... | collective-permute-start | bytes 393224 | tf_op jit(solution)/shard_map/ppermute | solution.py:20
  (22 other events, 54.9 us)
Sparse Core Ops, SparseCore 0:
  27.9 65.8 all-gather.1
  211.8 38.1 reduce-scatter.2
  252.8 27.2 reduce-scatter.4

commit v6 on v5

--- a/solution.py
+++ b/solution.py
@@ -36,7 +36,7 @@
     return tensor.transpose(1, 0, 2).reshape(row_count, heads * width)
 
 
-def attend_block(queries, out_grads, keys, values, allowed):
+def attend_forward(queries, keys, values, allowed):
     factor = HEAD_DIM ** (-0.5)
     scores = (
         jnp.einsum("hre,ke->hrk", queries, keys, preferred_element_type=jnp.float32) * factor
@@ -47,6 +47,11 @@
     weights = jnp.exp(scores - logsum)
     weights_low = weights.astype(jnp.bfloat16)
     output = jnp.einsum("hrk,ke->hre", weights_low, values, preferred_element_type=jnp.float32)
+    return weights, weights_low, output
+
+
+def attend_backward(queries, out_grads, keys, values, weights, weights_low, output):
+    factor = HEAD_DIM ** (-0.5)
     row_inner = jnp.sum(out_grads.astype(jnp.float32) * output, axis=2, keepdims=True)
     weight_grads = jnp.einsum(
         "hre,ke->hrk", out_grads, values, preferred_element_type=jnp.float32
@@ -63,6 +68,11 @@
         "hrk,hre->ke", weights_low, out_grads, preferred_element_type=jnp.float32
     )
     return query_grad, key_grad, value_grad
+
+
+def attend_block(queries, out_grads, keys, values, allowed):
+    weights, weights_low, output = attend_forward(queries, keys, values, allowed)
+    return attend_backward(queries, out_grads, keys, values, weights, weights_low, output)
 
 
 def local(
@@ -174,30 +184,6 @@
     head_count = normed_part.shape[1] // column_count
     extra = jnp.tile(jnp.pad(inner_part, (0, column_count - row_count)), head_count)
     reduced = jnp.concatenate([normed_part, extra[None, :]], axis=0)
-    for axis in HEAD:
-        reduced = lax.psum_scatter(reduced, axis, scatter_dimension=1, tiled=True)
-    normed_cols = reduced[:row_count]
-    inner_sum = reduced[row_count, :row_count]
-    gain_cols = lax.dynamic_slice_in_dim(
-        norm_gain, lax.axis_index(HEAD) * column_count, column_count
-    )
-    inputs = norm_input.astype(jnp.float32)
-    gained = normed_cols * gain_cols[None, :]
-    scaling = lax.rsqrt(square_sum / D + 1e-06)[:, None]
-    stream = (
-        scaling * gained
-        - inputs * scaling**3 * (inner_sum / D)[:, None]
-        + upstream.astype(jnp.float32)
-    )
-    grad_stream = stream.astype(jnp.bfloat16)
-    stream_full = grad_stream
-    for axis in reversed(HEAD):
-        stream_full = lax.all_gather(stream_full, axis, axis=1, tiled=True)
-    head_grads = lax.dot_general(
-        stream_full, weight_out, contract, preferred_element_type=jnp.float32
-    ).astype(jnp.bfloat16)
-
-    reach_count = WINDOW // row_count
     in_block = shard_index % (window_block.shape[0] // row_count)
     window_all = lax.dynamic_slice_in_dim(frame, in_block * row_count, WINDOW + row_count)
     own_place = first_row + jnp.arange(row_count, dtype=jnp.int32)
@@ -210,12 +196,46 @@
         & (window_place[None, :] > own_place[:, None] - WINDOW)
         & (window_segment[None, :] == own_segment[:, None])
     )
-    window_qgrad, window_kgrad, window_vgrad = attend_block(
-        split_heads(queries_window),
+    window_queries = split_heads(queries_window)
+    window_weights, window_low, window_out = attend_forward(
+        window_queries, window_all[:, :key_width], window_all[:, key_width:], allowed
+    )
+    reduced = lax.psum_scatter(reduced, HEAD[0], scatter_dimension=1, tiled=True)
+    reduced, window_weights, window_low, window_out = lax.optimization_barrier(
+        (reduced, window_weights, window_low, window_out)
+    )
+    for axis in HEAD[1:]:
+        reduced = lax.psum_scatter(reduced, axis, scatter_dimension=1, tiled=True)
+    normed_cols = reduced[:row_count]
+    inner_sum = reduced[row_count, :row_count]
+    gain_cols = lax.dynamic_slice_in_dim(
+        norm_gain, lax.axis_index(HEAD) * column_count, column_count
+    )
+    inputs = norm_input.astype(jnp.float32)
+    gained = normed_cols * gain_cols[None, :]
+    scaling = lax.rsqrt(square_sum / D + 1e-06)[:, None]
+    stream = (
+        scaling * gained
+        - inputs * scaling**3 * (inner_sum / D)[:, None]
+        + upstream.astype(jnp.float32)
+    )
+    grad_stream = stream.astype(jnp.bfloat16)
+    stream_full = grad_stream
+    for axis in reversed(HEAD):
+        stream_full = lax.all_gather(stream_full, axis, axis=1, tiled=True)
+    head_grads = lax.dot_general(
+        stream_full, weight_out, contract, preferred_element_type=jnp.float32
+    ).astype(jnp.bfloat16)
+
+    reach_count = WINDOW // row_count
+    window_qgrad, window_kgrad, window_vgrad = attend_backward(
+        window_queries,
         split_heads(head_grads),
         window_all[:, :key_width],
         window_all[:, key_width:],
-        allowed,
+        window_weights,
+        window_low,
+        window_out,
     )
     grad_queries = join_heads(window_qgrad).astype(jnp.bfloat16)
     window_part = jnp.concatenate([window_kgrad, window_vgrad], axis=1)

time: 371 us -> 369 us (level)
  waiting for transfers between devices: 75.8 us -> 70 us
    reduce_scatter x2 -> x1, waiting for transfers between devices: 56.2 us -> 22.3 us  [local(): reduced = lax.psum_scatter(reduced, axis, scatter_dimension=1, tiled=True)]
    reduce_scatter x0 -> x1, waiting for transfers between devices: none -> 28.1 us  [local(): lax.psum_scatter(reduced, HEAD[0], scatter_dimension=1, tiled=True)]
  transfers between devices with their start and end apart: 13 -> 13, of which waited for: 7 -> 7; matrix products, arithmetic and copies ran while one was open for 11% -> 12% of each run, Pallas kernels for 0% -> 0%
where the time goes in v6:
time: 369 us; the launch traced here: 367 us
  blocking collectives  141 us (38%)
  waiting for transfers between devices  70 us (19%)
  starting transfers between devices  45.3 us (12%)
  matrix products  34.2 us (9%)
  other arithmetic  33 us (9%)
  local copies, waits for them, and re-layouts  28.9 us (8%)
  between operations  14.4 us (4%)
    all_to_all x2, blocking collectives, local(): lax.all_to_all(summed, CTX[place], split_axis=place, concat_axis=place, t...  63.8 us
    ppermute x9, starting transfers between devices, from_behind(): lax.ppermute(value, axis, [(source, source + steps) for source in range(f...  39.8 us
    reduce_scatter x1, waiting for transfers between devices, local(): lax.psum_scatter(reduced, HEAD[0], scatter_dimension=1, tiled=True)  28.1 us
    reduce_scatter x1, waiting for transfers between devices, local(): reduced = lax.psum_scatter(reduced, axis, scatter_dimension=1, tiled=True)  22.3 us
    all_gather x2, blocking collectives, local(): inputs_full = lax.all_gather(inputs_full, axis, axis=1, tiled=True)  20.9 us
    all_gather x2, blocking collectives, local(): gathered = lax.all_gather(gathered, axis, axis=0, tiled=True)  19.6 us
    all_gather x2, blocking collectives, local(): window_block = lax.all_gather(window_block, axis, axis=0, tiled=True)  19.3 us
    all_gather x2, blocking collectives, local(): stream_full = lax.all_gather(stream_full, axis, axis=1, tiled=True)  17.5 us
  transfers between devices with their start and end apart: 13, of which 7 were waited for; matrix products, arithmetic and copies ran while one was open for 12% of the time, Pallas kernels for 0%

profile of v6, /device:TPU:449, one launch (start us, length us, event | category | flops | bytes accessed | tf_op | source)
XLA Modules:
  0.0 366.9 jit_solution(12887523644222933133)
XLA Ops:
  10.4 17.3 %all_gather.28 = bf16[1024,256]{1,0:T(8,128)(2,1)} all-gather(bf16[256,256]{1,0:T(8,128)(2,1)S(1)} %all_gather.27), channel_id=1, replica_groups=mesh['z'=8,'yh'=4,'core'=2,'yl'=2,'x'=4] {'yh'}, dimensions={0}, use_global_device_ids=true | all-gather | bytes 655360 | tf_op jit(solution)/shard_map/all_gather | solution.py:106
  28.6 5.1 %all_gather.32 = bf16[256,256]{1,0:T(8,128)(2,1)S(1)} all-gather(bf16[128,256]{1,0:T(8,128)(2,1)S(1)} %pad_maximum_fusion.5), channel_id=1, replica_groups=mesh['z'=8,'yh'=4,'core'=2,'yl'=2,'x'=4] {'core'}, dimensions={0}, use_global_device_ids=true | all-gather | bytes 196608 | tf_op jit(solution)/shard_map/all_gather | solution.py:114
  33.7 14.2 %all_gather.33 = bf16[1024,256]{1,0:T(8,128)(2,1)S(1)} all-gather(bf16[256,256]{1,0:T(8,128)(2,1)S(1)} %all_gather.32), channel_id=1, replica_groups=mesh['z'=8,'yh'=4,'core'=2,'yl'=2,'x'=4] {'yh'}, dimensions={0}, use_global_device_ids=true | all-gather | bytes 655360 | tf_op jit(solution)/shard_map/all_gather | solution.py:114
  56.1 11.9 %all_gather.30 = bf16[128,1536]{1,0:T(8,128)(2,1)S(1)} all-gather(bf16[128,384]{1,0:T(8,128)(2,1)} %param.21), channel_id=1, replica_groups=mesh['z'=8,'yh'=4,'core'=2,'yl'=2,'x'=4] {'x'}, dimensions={1}, use_global_device_ids=true | all-gather | bytes 491520 | tf_op jit(solution)/shard_map/all_gather | solution.py:110
  73.6 8.9 %all_gather.31 = bf16[128,3072]{1,0:T(8,128)(2,1)} all-gather(bf16[128,1536]{1,0:T(8,128)(2,1)S(1)} %all_gather.30), channel_id=1, replica_groups=mesh['z'=8,'yh'=4,'core'=2,'yl'=2,'x'=4] {'yl'}, dimensions={1}, use_global_device_ids=true | all-gather | bytes 1179648 | tf_op jit(solution)/shard_map/all_gather | solution.py:110
  90.2 3.5 all-gather.2.cloned.1.call-done
  93.8 4.6 %copy.142 = bf16[64,128,256]{2,0,1:T(8,128)(2,1)S(1)} copy(bf16[64,128,256]{2,1,0:T(8,128)(2,1)} %bitcast.226) | data formatting | bytes 8388608 | tf_op jit(solution)/shard_map/reshape | solution.py:119
  115.8 8.5 %all_to_all.15 = bf16[8,4,2,128,256]{4,3,1,0,2:T(8,128)(2,1)} all-to-all(bf16[8,4,2,128,256]{4,3,1,0,2:T(8,128)(2,1)S(1)} %copy.177), channel_id=1, replica_groups=mesh['z'=8,'yh'=4,'core'=2,'yl'=2,'x'=4] {'core'}, dimensions={2} | all-to-all | bytes 8388608 | tf_op jit(solution)/shard_map/all_to_all | solution.py:159
  124.3 5.1 %reduce_sum.187 = bf16[8,4,128,256]{3,2,1,0:T(8,128)(2,1)} reduce(bf16[8,4,2,128,256]{4,3,1,0,2:T(8,128)(2,1)} %all_to_all.15, bf16[]{:T(256)} %constant.78.clone.1), dimensions={2}, to_apply=%region_16.17 | reduce | flops 1048576 | bytes 6291458 | tf_op jit(solution)/shard_map/reduce_sum | solution.py:160
  131.1 55.3 %all_to_all.16 = bf16[8,4,128,256]{3,2,0,1:T(8,128)(2,1)} all-to-all(bf16[8,4,128,256]{3,2,0,1:T(8,128)(2,1)S(1)} %copy.153), channel_id=1, replica_groups=mesh['z'=8,'yh'=4,'core'=2,'yl'=2,'x'=4] {'yh'}, dimensions={1} | all-to-all | bytes 4194304 | tf_op jit(solution)/shard_map/all_to_all | solution.py:159
  189.3 5.5 %all-to-all-start.2 = ((bf16[8,128,256]{2,1,0:T(8,128)(2,1)}), bf16[8,128,256]{2,1,0:T(8,128)(2,1)}, u32[]{:S(2)}, u32[]{:S(2)}) async-start(bf16[8,128,256]{2,1,0:T(8,128)(2,1)} %reduce_sum.188), calls=%async_computation.2 | async-start | bytes 1048576 | tf_op jit(solution)/shard_map/all_to_all | solution.py:159
  197.1 6.7 %all-to-all-done.2 = bf16[8,128,256]{2,1,0:T(8,128)(2,1)} async-done(((bf16[8,128,256]{2,1,0:T(8,128)(2,1)}), bf16[8,128,256]{2,1,0:T(8,128)(2,1)}, u32[]{:S(2)}, u32[]{:S(2)}) %all-to-all-start.2) | async-done | bytes 524320 | tf_op jit(solution)/shard_map/all_to_all | solution.py:159
  221.8 28.1 %reduce-scatter.3.cloned.1.call-done = f32[129,1536]{1,0:T(8,128)} async-done(((f32[129,3072]{1,0:T(8,128)}), f32[129,1536]{1,0:T(8,128)}) %reduce-scatter.3.cloned.1.call-update) | async-done | bytes 792592 | tf_op jit(solution)/shard_map/reduce_scatter | solution.py:203
  257.8 22.3 %reduce-scatter.5.cloned.1.call-done = f32[129,384]{1,0:T(8,128)} async-done(((f32[129,1536]{1,0:T(8,128)}), f32[129,384]{1,0:T(8,128)}) %reduce-scatter.5.cloned.1.call-update) | async-done | bytes 198160 | tf_op jit(solution)/shard_map/reduce_scatter | solution.py:208
  281.8 10.0 %all_gather.34 = bf16[128,1536]{1,0:T(8,128)(2,1)S(1)} all-gather(bf16[128,384]{1,0:T(8,128)(2,1)S(1)} %fusion.66), channel_id=1, replica_groups=mesh['z'=8,'yh'=4,'core'=2,'yl'=2,'x'=4] {'x'}, dimensions={1}, use_global_device_ids=true | all-gather | bytes 491520 | tf_op jit(solution)/shard_map/all_gather | solution.py:225
  291.8 7.5 %all_gather.35 = bf16[128,3072]{1,0:T(8,128)(2,1)S(1)} all-gather(bf16[128,1536]{1,0:T(8,128)(2,1)S(1)} %all_gather.34), channel_id=1, replica_groups=mesh['z'=8,'yh'=4,'core'=2,'yl'=2,'x'=4] {'yl'}, dimensions={1}, use_global_device_ids=true | all-gather | bytes 1179648 | tf_op jit(solution)/shard_map/all_gather | solution.py:225
  305.3 3.6 collective-permute-start.8
  308.9 10.6 %collective-permute-start.7 = (f32[128,256]{0,1:T(8,128)}, f32[128,256]{0,1:T(8,128)}, u32[]{:S(2)}, u32[]{:S(2)}) collective-permute-start(f32[128,256]{0,1:T(8,128)} %get-tuple-element.60), channel_id=1, source_target_pairs={{56,0},{64,8},{72,16},{80,24},{88,32},{96,40},{104,48},{112,56},{1... | collective-permute-start | bytes 393224 | tf_op jit(solution)/shard_map/ppermute | solution.py:20
  319.5 5.3 %collective-permute-start.6 = (f32[128,256]{0,1:T(8,128)}, f32[128,256]{0,1:T(8,128)}, u32[]{:S(2)}, u32[]{:S(2)}) collective-permute-start(f32[128,256]{0,1:T(8,128)} %get-tuple-element.58), channel_id=1, source_target_pairs={{48,0},{56,8},{64,16},{72,24},{80,32},{88,40},{96,48},{104,56},{11... | collective-permute-start | bytes 393224 | tf_op jit(solution)/shard_map/ppermute | solution.py:20
  329.4 3.9 %collective-permute-start.4 = (f32[128,256]{0,1:T(8,128)}, f32[128,256]{0,1:T(8,128)}, u32[]{:S(2)}, u32[]{:S(2)}) collective-permute-start(f32[128,256]{0,1:T(8,128)} %get-tuple-element.56), channel_id=1, source_target_pairs={{32,0},{40,8},{48,16},{56,24},{64,32},{72,40},{80,48},{88,56},{96,... | collective-permute-start | bytes 393224 | tf_op jit(solution)/shard_map/ppermute | solution.py:20
  333.3 3.8 %collective-permute-start.3 = (f32[128,256]{0,1:T(8,128)}, f32[128,256]{0,1:T(8,128)}, u32[]{:S(2)}, u32[]{:S(2)}) collective-permute-start(f32[128,256]{0,1:T(8,128)} %get-tuple-element.55), channel_id=1, source_target_pairs={{24,0},{32,8},{40,16},{48,24},{56,32},{64,40},{72,48},{80,56},{88,... | collective-permute-start | bytes 393224 | tf_op jit(solution)/shard_map/ppermute | solution.py:20
  337.1 3.9 %collective-permute-start.2 = (f32[128,256]{0,1:T(8,128)}, f32[128,256]{0,1:T(8,128)}, u32[]{:S(2)}, u32[]{:S(2)}) collective-permute-start(f32[128,256]{0,1:T(8,128)} %get-tuple-element.54), channel_id=1, source_target_pairs={{16,0},{24,8},{32,16},{40,24},{48,32},{56,40},{64,48},{72,56},{80,... | collective-permute-start | bytes 393224 | tf_op jit(solution)/shard_map/ppermute | solution.py:20
  341.0 5.2 %collective-permute-start.1 = (f32[128,256]{0,1:T(8,128)}, f32[128,256]{0,1:T(8,128)}, u32[]{:S(2)}, u32[]{:S(2)}) collective-permute-start(f32[128,256]{0,1:T(8,128)} %get-tuple-element.53), channel_id=1, source_target_pairs={{8,0},{16,8},{24,16},{32,24},{40,32},{48,40},{56,48},{64,56},{72,6... | collective-permute-start | bytes 393224 | tf_op jit(solution)/shard_map/ppermute | solution.py:20
  351.7 5.7 %collective-permute-done.2 = f32[128,256]{0,1:T(8,128)} collective-permute-done((f32[128,256]{0,1:T(8,128)}, f32[128,256]{0,1:T(8,128)}, u32[]{:S(2)}, u32[]{:S(2)}) %collective-permute-start.2) | collective-permute-done | bytes 131104 | tf_op jit(solution)/shard_map/ppermute | solution.py:20
  (190 shorter events, 96.0 us)
Async XLA Ops:
  7.2 292.2 %copy-start = (bf16[384,3072]{1,0:T(8,128)(2,1)S(1)}, bf16[384,3072]{1,0:T(8,128)(2,1)}, u32[]{:S(2)}) copy-start(bf16[384,3072]{1,0:T(8,128)(2,1)} %param.26) | copy-start | bytes 7077892
  7.2 42.0 %copy-start.14 = (s32[8192]{0:T(1024)S(1)}, s32[8192]{0:T(1024)}, u32[]{:S(2)}) copy-start(s32[8192]{0:T(1024)} %param.19) | copy-start | bytes 98308
  7.2 43.6 %copy-start.23 = (s32[8192]{0:T(1024)S(1)}, s32[8192]{0:T(1024)}, u32[]{:S(2)}) copy-start(s32[8192]{0:T(1024)} %param.20) | copy-start | bytes 98308
  7.2 86.6 %all-gather.2.cloned.1.call-start = ((), (), s32[]{:S(2)}) async-start(), calls=%async_computation.5 | async-start | bytes 4718592 | tf_op jit(solution)/shard_map/all_gather | solution.py:106
  47.8 41.3 %collective-permute-start = (bf16[1024,256]{1,0:T(8,128)(2,1)S(1)}, bf16[1024,256]{1,0:T(8,128)(2,1)S(1)}, u32[]{:S(2)}, u32[]{:S(2)}) collective-permute-start(bf16[1024,256]{1,0:T(8,128)(2,1)S(1)} %all_gather.33), channel_id=1, source_target_pairs={{0,64},{64,128},{128,192},{192,256},{256,320},{320,384},{384,448},... | collective-permute-start | bytes 1572872 | tf_op jit(solution)/shard_map/ppermute | solution.py:20
  87.5 19.8 %copy-start.11 = (bf16[128,3,128]{2,0,1:T(8,128)(2,1)}, bf16[128,3,128]{2,0,1:T(8,128)(2,1)S(1)}, u32[]{:S(2)}) copy-start(bf16[128,3,128]{2,0,1:T(8,128)(2,1)S(1)} %copy.146) | copy-start | bytes 294916
  189.3 14.5 %all-to-all-start.2 = ((bf16[8,128,256]{2,1,0:T(8,128)(2,1)}), bf16[8,128,256]{2,1,0:T(8,128)(2,1)}, u32[]{:S(2)}, u32[]{:S(2)}) async-start(bf16[8,128,256]{2,1,0:T(8,128)(2,1)} %reduce_sum.188), calls=%async_computation.2 | async-start | bytes 1048576 | tf_op jit(solution)/shard_map/all_to_all | solution.py:159
  194.8 55.2 %reduce-scatter.3.cloned.1.call-start = ((), (), s32[]{:S(2)}) async-start(), calls=%async_computation.6 | async-start | bytes 2506752 | tf_op jit(solution)/shard_map/reduce_scatter | solution.py:203
  211.6 68.5 %reduce-scatter.5.cloned.1.call-start = ((), (), s32[]{:S(2)}) async-start(), calls=%async_computation.7 | async-start | bytes 1044480 | tf_op jit(solution)/shard_map/reduce_scatter | solution.py:208
  255.1 25.6 %copy-start.17 = (bf16[128,384]{1,0:T(8,128)(2,1)S(1)}, bf16[128,384]{1,0:T(8,128)(2,1)}, u32[]{:S(2)}) copy-start(bf16[128,384]{1,0:T(8,128)(2,1)} %param.21) | copy-start | bytes 294916
  255.1 25.6 %copy-start.24 = (bf16[128,384]{1,0:T(8,128)(2,1)S(1)}, bf16[128,384]{1,0:T(8,128)(2,1)}, u32[]{:S(2)}) copy-start(bf16[128,384]{1,0:T(8,128)(2,1)} %param.25) | copy-start | bytes 294916
  303.1 23.1 %copy-start.5 = (f32[1152,128]{0,1:T(8,128)}, f32[1152,128]{0,1:T(8,128)S(1)}, u32[]{:S(2)}) copy-start(f32[1152,128]{0,1:T(8,128)S(1)} %fusion.27) | copy-start | bytes 1769476
  303.1 21.8 %copy-start.10 = (bf16[3,32,2048]{2,1,0:T(8,128)(2,1)S(1)}, bf16[3,32,2048]{2,1,0:T(8,128)(2,1)}, u32[]{:S(2)}) copy-start(bf16[3,32,2048]{2,1,0:T(8,128)(2,1)} %copy-done.9) | copy-start | bytes 1179652
  303.1 23.1 %copy-start.26 = (bf16[3,32,128]{2,1,0:T(8,128)(2,1)S(1)}, bf16[3,32,128]{2,1,0:T(8,128)(2,1)}, u32[]{:S(2)}) copy-start(bf16[3,32,128]{2,1,0:T(8,128)(2,1)} %fusion.48) | copy-start | bytes 73732
  303.1 23.1 %copy-start.27 = (bf16[3,32,128]{2,1,0:T(8,128)(2,1)S(1)}, bf16[3,32,128]{2,1,0:T(8,128)(2,1)}, u32[]{:S(2)}) copy-start(bf16[3,32,128]{2,1,0:T(8,128)(2,1)} %fusion.50) | copy-start | bytes 73732
  303.1 23.1 %copy-start.28 = (bf16[3,32,128]{2,1,0:T(8,128)(2,1)S(1)}, bf16[3,32,128]{2,1,0:T(8,128)(2,1)}, u32[]{:S(2)}) copy-start(bf16[3,32,128]{2,1,0:T(8,128)(2,1)} %fusion.49) | copy-start | bytes 73732
  305.3 27.9 %collective-permute-start.8 = (f32[128,256]{0,1:T(8,128)}, f32[128,256]{0,1:T(8,128)}, u32[]{:S(2)}, u32[]{:S(2)}) collective-permute-start(f32[128,256]{0,1:T(8,128)} %get-tuple-element.59), channel_id=1, source_target_pairs={{64,0},{72,8},{80,16},{88,24},{96,32},{104,40},{112,48},{120,56},{... | collective-permute-start | bytes 393224 | tf_op jit(solution)/shard_map/ppermute | solution.py:20
  308.9 28.1 %collective-permute-start.7 = (f32[128,256]{0,1:T(8,128)}, f32[128,256]{0,1:T(8,128)}, u32[]{:S(2)}, u32[]{:S(2)}) collective-permute-start(f32[128,256]{0,1:T(8,128)} %get-tuple-element.60), channel_id=1, source_target_pairs={{56,0},{64,8},{72,16},{80,24},{88,32},{96,40},{104,48},{112,56},{1... | collective-permute-start | bytes 393224 | tf_op jit(solution)/shard_map/ppermute | solution.py:20
  319.5 21.5 %collective-permute-start.6 = (f32[128,256]{0,1:T(8,128)}, f32[128,256]{0,1:T(8,128)}, u32[]{:S(2)}, u32[]{:S(2)}) collective-permute-start(f32[128,256]{0,1:T(8,128)} %get-tuple-element.58), channel_id=1, source_target_pairs={{48,0},{56,8},{64,16},{72,24},{80,32},{88,40},{96,48},{104,56},{11... | collective-permute-start | bytes 393224 | tf_op jit(solution)/shard_map/ppermute | solution.py:20
  327.1 21.2 %collective-permute-start.5 = (f32[128,256]{0,1:T(8,128)}, f32[128,256]{0,1:T(8,128)S(1)}, u32[]{:S(2)}, u32[]{:S(2)}) collective-permute-start(f32[128,256]{0,1:T(8,128)} %get-tuple-element.57), channel_id=1, source_target_pairs={{40,0},{48,8},{56,16},{64,24},{72,32},{80,40},{88,48},{96,56},{104... | collective-permute-start | bytes 393224 | tf_op jit(solution)/shard_map/ppermute | solution.py:20
  329.4 18.9 %collective-permute-start.4 = (f32[128,256]{0,1:T(8,128)}, f32[128,256]{0,1:T(8,128)}, u32[]{:S(2)}, u32[]{:S(2)}) collective-permute-start(f32[128,256]{0,1:T(8,128)} %get-tuple-element.56), channel_id=1, source_target_pairs={{32,0},{40,8},{48,16},{56,24},{64,32},{72,40},{80,48},{88,56},{96,... | collective-permute-start | bytes 393224 | tf_op jit(solution)/shard_map/ppermute | solution.py:20
  333.3 18.5 %collective-permute-start.3 = (f32[128,256]{0,1:T(8,128)}, f32[128,256]{0,1:T(8,128)}, u32[]{:S(2)}, u32[]{:S(2)}) collective-permute-start(f32[128,256]{0,1:T(8,128)} %get-tuple-element.55), channel_id=1, source_target_pairs={{24,0},{32,8},{40,16},{48,24},{56,32},{64,40},{72,48},{80,56},{88,... | collective-permute-start | bytes 393224 | tf_op jit(solution)/shard_map/ppermute | solution.py:20
  337.1 20.4 %collective-permute-start.2 = (f32[128,256]{0,1:T(8,128)}, f32[128,256]{0,1:T(8,128)}, u32[]{:S(2)}, u32[]{:S(2)}) collective-permute-start(f32[128,256]{0,1:T(8,128)} %get-tuple-element.54), channel_id=1, source_target_pairs={{16,0},{24,8},{32,16},{40,24},{48,32},{56,40},{64,48},{72,56},{80,... | collective-permute-start | bytes 393224 | tf_op jit(solution)/shard_map/ppermute | solution.py:20
  341.0 16.6 %collective-permute-start.1 = (f32[128,256]{0,1:T(8,128)}, f32[128,256]{0,1:T(8,128)}, u32[]{:S(2)}, u32[]{:S(2)}) collective-permute-start(f32[128,256]{0,1:T(8,128)} %get-tuple-element.53), channel_id=1, source_target_pairs={{8,0},{16,8},{24,16},{32,24},{40,32},{48,40},{56,48},{64,56},{72,6... | collective-permute-start | bytes 393224 | tf_op jit(solution)/shard_map/ppermute | solution.py:20
  (22 other events, 68.0 us)
Sparse Core Ops, SparseCore 0:
  27.9 65.8 all-gather.1
  211.7 38.1 reduce-scatter.2
  252.8 27.2 reduce-scatter.4
